TPU v7x, 128 devices: a whole 4x4x4 slice. The times are simulated.
128 devices in a mesh: group: 8 (over z, x_lo), req: 16 (over x_hi, y, core).
Axes of the slice: x: 4 (x_hi: 2, x_lo: 2; x = x_hi * 2 + x_lo), y: 4, z: 4, core: 2. Of those that a mesh axis runs over, the one named last changes fastest.
Arguments:
- layer_input: bfloat16 [16384, 3072], P(('group', 'req')), may hold values from -6 to 6
- queries: bfloat16 [16384, 3072], P(('group', 'req')), may hold values from -240 to 240, as said below
- suffix_kv: bfloat16 [16384, 2048], P(('group', 'req')), may hold values from -6 to 6
- past_kv: bfloat16 [32768, 2048], P(('group', 'req')), may hold values from -6 to 6
- prefix_kv: bfloat16 [2048, 2048], P(('group', 'req')), may hold values from -6 to 6
- suffix_len: int32 [128], P(('group', 'req')), may hold values from 1 to 128, 12288 in all
- past_len: int32 [128], P(('group', 'req')), may hold values from 1 to 256, 16384 in all
- out_weight: bfloat16 [3072, 3072], P('group'), may hold values from -0.109375 to 0.109375
- norm_gain: bfloat16 [3072], replicated, may hold values from 0.5 to 1.5
- gate_weight: bfloat16 [3072, 8192], P(None, 'req'), may hold values from -0.109375 to 0.109375
- up_weight: bfloat16 [3072, 8192], P(None, 'req'), may hold values from -0.109375 to 0.109375
- down_weight: bfloat16 [8192, 3072], P('req'), may hold values from -0.0625 to 0.0625
Outputs:
- layer_output: bfloat16 [16384, 3072], P(('group', 'req'))
Inputs may be any that keep to these rules, and one draw needn't show every extreme that they name: `queries`: normally distributed entries; some rows may be far larger.
All inputs are finite; a program needn't handle non-finite values. No bound on the sum of `suffix_len` or of `past_len` on one device may be relied on, other than what follows from the above.
Results may differ from a plain program's by a relative error of at most 0.012.
Values may be sent and summed in bfloat16 or wider, within the bound.
No kernel may reach another device: no remote copies, remote signals or barrier semaphores. Data moves between devices by JAX's collectives and lax.ppermute only.
A program may use at most 128 MiB of HBM per device.

v0:
```python
import jax
import jax.numpy as jnp
from jax import lax
from jax.sharding import PartitionSpec as P

HEADS = 24
KV_HEADS = 8
HEAD = 128
SINK = 4


def absorb(state, query_heads, key_rows, key_pos, key_valid, query_pos, window):
    maxima, totals, sums = state
    count = key_rows.shape[0]
    key_heads = key_rows[:, : KV_HEADS * HEAD].reshape(count, KV_HEADS, HEAD)
    value_heads = key_rows[:, KV_HEADS * HEAD :].reshape(count, KV_HEADS, HEAD)
    scores = jnp.einsum(
        "skgh,nkh->kgsn", query_heads, key_heads, preferred_element_type=jnp.float32
    ) * HEAD ** (-0.5)
    near = query_pos[:, None] - key_pos[None, :] < window
    allowed = (
        key_valid[None, :]
        & (key_pos[None, :] <= query_pos[:, None])
        & ((key_pos[None, :] < SINK) | near)
    )
    scores = jnp.where(allowed, scores, -1e30)
    new_max = jnp.maximum(maxima, jnp.max(scores, axis=-1))
    expo = jnp.where(allowed, jnp.exp(scores - new_max[..., None]), 0.0)
    factor = jnp.exp(maxima - new_max)
    totals = totals * factor + jnp.sum(expo, axis=-1)
    sums = sums * factor[..., None] + jnp.einsum(
        "kgsn,nkh->kgsh", expo.astype(jnp.bfloat16), value_heads, preferred_element_type=jnp.float32
    )
    return (new_max, totals, sums)


def shards(
    layer_input,
    queries,
    suffix_kv,
    past_kv,
    prefix_kv,
    suffix_len,
    past_len,
    out_weight,
    norm_gain,
    gate_weight,
    up_weight,
    down_weight,
):
    rows_here = queries.shape[0]
    past_slots = past_kv.shape[0]
    prefix_total = prefix_kv.shape[0] * lax.axis_size("req")
    window = prefix_total + past_slots // 2
    past_count = past_len[0]
    offsets = jnp.arange(rows_here, dtype=jnp.int32)
    query_pos = prefix_total + past_count + offsets
    ratio = HEADS // KV_HEADS
    query_heads = queries.reshape(rows_here, KV_HEADS, ratio, HEAD)
    state = (
        jnp.full((KV_HEADS, ratio, rows_here), -1e30, jnp.float32),
        jnp.zeros((KV_HEADS, ratio, rows_here), jnp.float32),
        jnp.zeros((KV_HEADS, ratio, rows_here, HEAD), jnp.float32),
    )
    local_rows = jnp.concatenate([past_kv, suffix_kv], axis=0)
    local_pos = jnp.concatenate([prefix_total + jnp.arange(past_slots, dtype=jnp.int32), query_pos])
    local_valid = jnp.concatenate(
        [jnp.arange(past_slots, dtype=jnp.int32) < past_count, jnp.ones((rows_here,), bool)]
    )
    state = absorb(state, query_heads, local_rows, local_pos, local_valid, query_pos, window)
    piece = lax.all_gather(prefix_kv, "req", axis=0, tiled=True)
    count = piece.shape[0]
    positions = jnp.arange(count, dtype=jnp.int32)
    maxima, totals, sums = absorb(
        state, query_heads, piece, positions, jnp.ones((count,), bool), query_pos, window
    )
    attended = (
        (sums / totals[..., None])
        .transpose(2, 0, 1, 3)
        .reshape(rows_here, HEADS * HEAD)
        .astype(jnp.bfloat16)
    )
    projected = jnp.dot(
        attended,
        lax.all_gather(out_weight, "group", axis=0, tiled=True),
        preferred_element_type=jnp.float32,
    )
    mixed = layer_input.astype(jnp.float32) + projected
    scale = lax.rsqrt(jnp.mean(mixed * mixed, axis=-1, keepdims=True) + 1e-05)
    normed = (mixed * scale * norm_gain.astype(jnp.float32)).astype(jnp.bfloat16)
    gathered = lax.all_gather(normed, "req", axis=0, tiled=True)
    gate = jnp.dot(gathered, gate_weight, preferred_element_type=jnp.float32)
    upper = jnp.dot(gathered, up_weight, preferred_element_type=jnp.float32)
    hidden = (jax.nn.silu(gate) * upper).astype(jnp.bfloat16)
    feed = lax.psum_scatter(
        jnp.dot(hidden, down_weight, preferred_element_type=jnp.float32).astype(jnp.bfloat16),
        "req",
        scatter_dimension=0,
        tiled=True,
    ).astype(jnp.float32)
    live = offsets < suffix_len[0]
    return jnp.where(live[:, None], mixed + feed, 0.0).astype(jnp.bfloat16)


def solution(mesh):
    in_specs = (
        P(("group", "req"), None),
        P(("group", "req"), None),
        P(("group", "req"), None),
        P(("group", "req"), None),
        P(("group", "req"), None),
        P(("group", "req")),
        P(("group", "req")),
        P("group", None),
        P(),
        P(None, "req"),
        P(None, "req"),
        P("req", None),
    )
    out_specs = P(("group", "req"), None)
    return jax.shard_map(shards, mesh=mesh, in_specs=in_specs, out_specs=out_specs, check_vma=False)
```

profile of v0, /device:TPU:1, one launch (start us, length us, event | category | flops | bytes accessed | tf_op | source)
XLA Modules:
  0.0 687.3 jit_solution(6769247069132411062)
XLA Ops:
  6.5 0.0 copy-start
  6.5 0.0 all-gather.4.cloned.1.call-start
  6.5 0.7 all-gather.4.cloned.1.call-update
  7.3 0.0 copy-start.6
  7.3 0.0 all-gather.6.cloned.1.call-start
  7.3 0.7 all-gather.6.cloned.1.call-update
  8.0 0.0 all-gather.8.cloned.1.call-start
  8.7 2.3 copy.29
  11.0 2.1 copy.30
  13.1 2.3 copy.31
  15.3 0.0 copy-done.6
  15.3 0.0 copy-start.3
  15.4 2.5 pad_maximum_fusion
  18.0 0.1 fusion.29
  18.1 0.2 fusion.28
  18.3 0.0 copy-done.3
  18.3 3.1 fusion
  21.4 36.6 %all-gather.4.cloned.1.call-done = bf16[256,2048]{1,0:T(8,128)(2,1)} async-done(((bf16[16,2048]{1,0:T(8,128)(2,1)}), bf16[256,2048]{1,0:T(8,128)(2,1)}) %all-gather.4.cloned.1.call-update) | async-done | bytes 1048592 | tf_op jit(solution)/shard_map/all_gather | solution.py:71
  58.0 2.3 fusion.44
  60.3 2.0 copy.52
  62.4 2.0 copy.38
  64.4 1.9 fusion.3
  66.4 0.0 slice-start
  66.4 0.8 fusion.11
  67.2 0.0 copy-start.5
  67.2 0.0 slice-start.1
  67.2 4.8 fusion.1
  72.0 0.0 copy-start.4
  72.0 0.0 copy-done.5
  72.0 0.8 fusion.14
  72.9 0.0 slice-done
  72.9 0.0 slice-done.1
  72.9 0.3 copy-done.4
  73.1 2.4 fusion.17
  75.6 347.3 %all-gather.6.cloned.1.call-done = bf16[3072,3072]{1,0:T(8,128)(2,1)} async-done(((bf16[384,3072]{1,0:T(8,128)(2,1)}), bf16[3072,3072]{1,0:T(8,128)(2,1)}) %all-gather.6.cloned.1.call-update) | async-done | bytes 18874384 | tf_op jit(solution)/shard_map/all_gather | solution.py:85
  422.9 9.5 %multiply_reduce_fusion = (f32[128]{0:T(128)S(1)}, f32[128,3072]{1,0:T(8,128)S(1)}) fusion(bf16[128,3072]{0,1:T(8,128)(2,1)} %bitcast.103, bf16[3072,3072]{1,0:T(8,128)(2,1)} %all-gather.6.cloned.1.call-done, bf16[128,3072]{1,0:T(8,128)(2,1)} %param.12), kind=kOutput, calls=%fused_computation.30 | convolution fusion | flops 2417491968 | bytes 22020608 | tf_op jit(solution)/shard_map/dot_general | solution.py:83
  432.4 0.0 copy-start.2
  432.4 1.2 copy-done.2
  433.6 1.1 multiply_convert_fusion.1
  434.7 0.0 all-gather.8.cloned.1.call-update
  434.7 0.2 reduce-scatter.2.cloned.1.call-start
  434.9 91.9 %all-gather.8.cloned.1.call-done = bf16[2048,3072]{1,0:T(8,128)(2,1)} async-done(((bf16[128,3072]{1,0:T(8,128)(2,1)}), bf16[2048,3072]{1,0:T(8,128)(2,1)}) %all-gather.8.cloned.1.call-update) | async-done | bytes 12582928 | tf_op jit(solution)/shard_map/all_gather | solution.py:91
  526.8 11.8 %fusion.45 = f32[2048,512]{1,0:T(8,128)} fusion(bf16[2048,3072]{1,0:T(8,128)(2,1)} %all-gather.8.cloned.1.call-done, bf16[3072,512]{1,0:T(8,128)(2,1)} %param.21), kind=kOutput, calls=%fused_computation.71 | convolution fusion | flops 6442450944 | bytes 19922944 | tf_op jit(solution)/shard_map/dot_general | solution.py:92
  538.6 0.0 copy-done
  538.6 20.5 %convolution_convert_fusion = bf16[2048,3072]{1,0:T(8,128)(2,1)} fusion(bf16[512,3072]{1,0:T(8,128)(2,1)S(1)} %copy-done, f32[2048,512]{1,0:T(8,128)} %fusion.45, bf16[2048,3072]{1,0:T(8,128)(2,1)} %all-gather.8.cloned.1.call-done, bf16[3072,512]{1,0:T(8,128)(2,1)} %param.22), kind=kOutput, calls=%fused_computation | convolution fusion | flops 12897484800 | bytes 35651584 | tf_op jit(solution)/shard_map/dot_general | solution.py:96
  559.2 0.0 reduce-scatter.2.cloned.1.call-update
  559.2 0.0 copy-start.1
  560.0 118.0 %reduce-scatter.2.cloned.1.call-done = bf16[128,3072]{1,0:T(8,128)(2,1)} async-done(((bf16[2048,3072]{1,0:T(8,128)(2,1)}), bf16[128,3072]{1,0:T(8,128)(2,1)}) %reduce-scatter.2.cloned.1.call-update) | async-done | bytes 786448 | tf_op jit(solution)/shard_map/reduce_scatter | solution.py:95
  678.0 2.7 select_convert_fusion
  680.8 0.0 copy-done.1
  (13 shorter events, 0.1 us)
Async XLA Ops:
  6.5 532.1 %copy-start = (bf16[512,3072]{1,0:T(8,128)(2,1)S(1)}, bf16[512,3072]{1,0:T(8,128)(2,1)}, u32[]{:S(2)}) copy-start(bf16[512,3072]{1,0:T(8,128)(2,1)} %param.23) | copy-start | bytes 9437188
  6.5 51.5 %all-gather.4.cloned.1.call-start = ((), (), s32[]{:S(2)}) async-start(), calls=%async_computation.1 | async-start | bytes 1114112 | tf_op jit(solution)/shard_map/all_gather | solution.py:71
  7.3 8.1 %copy-start.6 = (bf16[3072]{0:T(1024)(128)(2,1)S(1)}, bf16[3072]{0:T(1024)(128)(2,1)}, u32[]{:S(2)}) copy-start(bf16[3072]{0:T(1024)(128)(2,1)} %param.20) | copy-start | bytes 18436
  7.3 415.6 %all-gather.6.cloned.1.call-start = ((), (), s32[]{:S(2)}) async-start(), calls=%async_computation.2 | async-start | bytes 21233664 | tf_op jit(solution)/shard_map/all_gather | solution.py:85
  8.0 518.8 %all-gather.8.cloned.1.call-start = ((), (), s32[]{:S(2)}) async-start(), calls=%async_computation.3 | async-start | bytes 13369344 | tf_op jit(solution)/shard_map/all_gather | solution.py:91
  15.3 3.0 copy-start.3
  66.4 6.5 slice-start
  67.2 4.8 copy-start.5
  67.2 5.7 slice-start.1
  72.0 1.1 copy-start.4
  432.4 1.2 copy-start.2
  434.7 243.3 %reduce-scatter.2.cloned.1.call-start = ((), (), s32[]{:S(2)}) async-start(), calls=%async_computation.4 | async-start | bytes 13369344 | tf_op jit(solution)/shard_map/reduce_scatter | solution.py:95
  559.2 121.6 %copy-start.1 = (bf16[512,3072]{1,0:T(8,128)(2,1)S(1)}, bf16[512,3072]{1,0:T(8,128)(2,1)}, u32[]{:S(2)}) copy-start(bf16[512,3072]{1,0:T(8,128)(2,1)} %param.23) | copy-start | bytes 9437188
Sparse Core Ops, SparseCore 0:
  9.8 48.1 all-gather.3
  59.7 363.2 all-gather.5
  434.8 91.9 all-gather.7
  559.3 118.6 reduce-scatter.1
where the time goes:
time: 688 us; the launch traced here: 687 us
  waiting for transfers between devices  595 us (86%)
  matrix products  50.1 us (7%)
  between operations  14.8 us (2%)
  local copies, waits for them, and re-layouts  14.5 us (2%)
  other arithmetic  12.4 us (2%)
    all_gather x1, waiting for transfers between devices, shards(): lax.all_gather(out_weight, 'group', axis=0, tiled=True)  347 us
    reduce_scatter x1, waiting for transfers between devices, shards(): lax.psum_scatter(jnp.dot(hidden, down_weight, preferred_element_type=jnp....  118 us
    all_gather x1, waiting for transfers between devices, shards(): gathered = lax.all_gather(normed, 'req', axis=0, tiled=True)  91.9 us
    all_gather x1, waiting for transfers between devices, shards(): piece = lax.all_gather(prefix_kv, 'req', axis=0, tiled=True)  36.6 us
    dot_general x1, matrix products, shards(): jnp.dot(hidden, down_weight, preferred_element_type=jnp.float32)  20.5 us
  transfers between devices with their start and end apart: 4, of which 4 were waited for; matrix products, arithmetic and copies ran while one was open for 4% of the time, Pallas kernels for 0%

commit v1 on v0

--- a/solution.py
+++ b/solution.py
@@ -68,7 +68,10 @@
         [jnp.arange(past_slots, dtype=jnp.int32) < past_count, jnp.ones((rows_here,), bool)]
     )
     state = absorb(state, query_heads, local_rows, local_pos, local_valid, query_pos, window)
-    piece = lax.all_gather(prefix_kv, "req", axis=0, tiled=True)
+    n_req = lax.axis_size("req")
+    piece = lax.all_to_all(
+        jnp.broadcast_to(prefix_kv[None], (n_req,) + prefix_kv.shape), "req", 0, 0, tiled=False
+    ).reshape(prefix_total, prefix_kv.shape[1])
     count = piece.shape[0]
     positions = jnp.arange(count, dtype=jnp.int32)
     maxima, totals, sums = absorb(
@@ -80,11 +83,16 @@
         .reshape(rows_here, HEADS * HEAD)
         .astype(jnp.bfloat16)
     )
-    projected = jnp.dot(
-        attended,
-        lax.all_gather(out_weight, "group", axis=0, tiled=True),
-        preferred_element_type=jnp.float32,
+    n_group = lax.axis_size("group")
+    block = out_weight.shape[0]
+    columns = lax.all_to_all(
+        attended.reshape(rows_here, n_group, block), "group", 1, 0, tiled=False
+    ).reshape(n_group * rows_here, block)
+    partial = jnp.dot(columns, out_weight, preferred_element_type=jnp.float32).astype(jnp.bfloat16)
+    returned = lax.all_to_all(
+        partial.reshape(n_group, rows_here, partial.shape[1]), "group", 0, 0, tiled=False
     )
+    projected = jnp.sum(returned.astype(jnp.float32), axis=0)
     mixed = layer_input.astype(jnp.float32) + projected
     scale = lax.rsqrt(jnp.mean(mixed * mixed, axis=-1, keepdims=True) + 1e-05)
     normed = (mixed * scale * norm_gain.astype(jnp.float32)).astype(jnp.bfloat16)

time: 688 us -> 408 us (0.59)
  waiting for transfers between devices: 595 us -> 283 us
  blocking collectives: 0 us -> 16.7 us
  starting transfers between devices: 0.3 us -> 13.6 us
    all_gather x2 -> x0, waiting for transfers between devices: 384 us -> none  [the longest x1 347 us: shards(): lax.all_gather(out_weight, 'group', axis=0, tiled=True)]
    all_to_all x0 -> x2, waiting for transfers between devices: none -> 73.7 us  [the longest x1 69.7 us: shards(): lax.all_to_all(partial.reshape(n_group, rows_here, partial.shape[1]), 'gr...]
    all_to_all x0 -> x1, blocking collectives: none -> 16.7 us  [shards(): lax.all_to_all(attended.reshape(rows_here, n_group, block), 'group', 1, 0...]
    all_to_all x0 -> x2, starting transfers between devices: none -> 13.3 us  [the longest x1 8.44 us: shards(): lax.all_to_all(jnp.broadcast_to(prefix_kv[None], (n_req,) + prefix_kv.sha...]
  transfers between devices with their start and end apart: 4 -> 4, of which waited for: 4 -> 4; matrix products, arithmetic and copies ran while one was open for 4% -> 3% of each run, Pallas kernels for 0% -> 0%
where the time goes in v1:
time: 408 us
  waiting for transfers between devices  283 us (69%)
  matrix products  47.7 us (12%)
  local copies, waits for them, and re-layouts  18.3 us (4%)
  blocking collectives  16.7 us (4%)
  between operations  15.1 us (4%)
  starting transfers between devices  13.6 us (3%)
  other arithmetic  13.4 us (3%)
    reduce_scatter x1, waiting for transfers between devices, shards(): lax.psum_scatter(jnp.dot(hidden, down_weight, preferred_element_type=jnp....  118 us
    all_gather x1, waiting for transfers between devices, shards(): gathered = lax.all_gather(normed, 'req', axis=0, tiled=True)  90.9 us
    all_to_all x1, waiting for transfers between devices, shards(): lax.all_to_all(partial.reshape(n_group, rows_here, partial.shape[1]), 'gr...  69.7 us
    dot_general x1, matrix products, shards(): jnp.dot(hidden, down_weight, preferred_element_type=jnp.float32)  20.5 us
    all_to_all x1, blocking collectives, shards(): lax.all_to_all(attended.reshape(rows_here, n_group, block), 'group', 1, 0...  16.7 us
    dot_general x1, matrix products, shards(): gate = jnp.dot(gathered, gate_weight, preferred_element_type=jnp.float32)  11.8 us
    all_to_all x1, starting transfers between devices, shards(): lax.all_to_all(jnp.broadcast_to(prefix_kv[None], (n_req,) + prefix_kv.sha...  8.44 us
  transfers between devices with their start and end apart: 4, of which 4 were waited for; matrix products, arithmetic and copies ran while one was open for 3% of the time, Pallas kernels for 0%

profile of v1, /device:TPU:1, one launch (start us, length us, event | category | flops | bytes accessed | tf_op | source)
XLA Modules:
  0.0 407.5 jit_solution(7795687306915118669)
XLA Ops:
  6.5 0.0 copy-start
  6.5 2.1 broadcast_in_dim.79
  8.7 8.4 %all-to-all-start = ((bf16[16,16,2048]{2,1,0:T(8,128)(2,1)}), bf16[16,16,2048]{2,1,0:T(8,128)(2,1)}, u32[]{:S(2)}, u32[]{:S(2)}) async-start(bf16[16,16,2048]{2,1,0:T(8,128)(2,1)} %broadcast_in_dim.79), calls=%async_computation | async-start | bytes 2097152 | tf_op jit(solution)/shard_map/all_to_all | solution.py:72
  17.8 2.3 copy.31
  20.1 2.1 copy.32
  22.1 2.3 copy.33
  24.4 0.0 copy-start.4
  24.4 2.5 pad_maximum_fusion
  26.9 0.1 fusion.29
  27.0 0.2 fusion.28
  27.2 0.0 copy-done.4
  27.2 3.0 fusion
  30.3 4.0 all-to-all-done
  34.3 2.3 fusion.44
  36.5 2.0 copy.37
  38.6 2.1 copy.40
  40.6 0.0 copy-start.6
  40.6 0.0 slice-start
  40.6 2.1 fusion.3
  42.8 0.0 slice-start.1
  42.8 0.8 fusion.11
  43.6 0.0 copy-done.6
  43.6 0.8 fusion.14
  44.4 0.0 copy-start.5
  44.4 0.0 slice-done
  44.4 0.0 slice-done.1
  44.5 1.2 fusion.1
  45.6 0.0 copy-done.5
  45.6 2.4 fusion.17
  48.1 2.3 copy.42
  50.4 16.7 %all_to_all.25 = bf16[1,128,8,384]{3,1,0,2:T(8,128)(2,1)S(1)} all-to-all(bf16[1,128,8,384]{3,1,0,2:T(8,128)(2,1)} %copy.42), channel_id=1, replica_groups=mesh['group'=8,'req'=16] {'group'}, dimensions={2} | all-to-all | bytes 1572864 | tf_op jit(solution)/shard_map/all_to_all | solution.py:88
  67.1 7.0 %convolution_convert_fusion.1 = bf16[1024,3072]{1,0:T(8,128)(2,1)} fusion(bf16[1024,384]{1,0:T(8,128)(2,1)S(1)} %bitcast.112, bf16[384,3072]{1,0:T(8,128)(2,1)} %param.19), kind=kOutput, calls=%fused_computation.2 | convolution fusion | flops 2419064832 | bytes 9437184 | tf_op jit(solution)/shard_map/dot_general | solution.py:91
  74.1 0.0 copy-start.7
  74.1 4.9 %all-to-all-start.2 = ((bf16[8,128,3072]{2,1,0:T(8,128)(2,1)}), bf16[8,128,3072]{2,1,0:T(8,128)(2,1)}, u32[]{:S(2)}, u32[]{:S(2)}) async-start(bf16[8,128,3072]{2,1,0:T(8,128)(2,1)} %bitcast.108), calls=%async_computation.2 | async-start | bytes 12582912 | tf_op jit(solution)/shard_map/all_to_all | solution.py:92
  78.9 0.0 all-gather.2.cloned.1.call-start
  79.0 0.0 copy-done.7
  79.0 69.7 %all-to-all-done.2 = bf16[8,128,3072]{2,1,0:T(8,128)(2,1)} async-done(((bf16[8,128,3072]{2,1,0:T(8,128)(2,1)}), bf16[8,128,3072]{2,1,0:T(8,128)(2,1)}, u32[]{:S(2)}, u32[]{:S(2)}) %all-to-all-start.2) | async-done | bytes 6291488 | tf_op jit(solution)/shard_map/all_to_all | solution.py:92
  148.7 0.0 copy-start.3
  148.7 4.1 %convert_reduce_fusion = f32[128,3072]{1,0:T(8,128)S(1)} fusion(bf16[8,128,3072]{2,1,0:T(8,128)(2,1)} %all-to-all-done.2), kind=kLoop, calls=%fused_computation | loop fusion | flops 5898240 | bytes 7864320 | tf_op jit(solution)/shard_map/reduce_sum | solution.py:95
  152.8 0.0 copy-done.3
  152.8 0.0 copy-start.2
  152.8 0.3 multiply_reduce_fusion
  153.2 0.9 copy-done.2
  154.0 1.1 multiply_convert_fusion.1
  155.2 0.0 all-gather.2.cloned.1.call-update
  155.2 0.2 reduce-scatter.2.cloned.1.call-start
  155.4 90.9 %all-gather.2.cloned.1.call-done = bf16[2048,3072]{1,0:T(8,128)(2,1)} async-done(((bf16[128,3072]{1,0:T(8,128)(2,1)}), bf16[2048,3072]{1,0:T(8,128)(2,1)}) %all-gather.2.cloned.1.call-update) | async-done | bytes 12582928 | tf_op jit(solution)/shard_map/all_gather | solution.py:99
  246.4 11.8 %fusion.45 = f32[2048,512]{1,0:T(8,128)} fusion(bf16[2048,3072]{1,0:T(8,128)(2,1)} %all-gather.2.cloned.1.call-done, bf16[3072,512]{1,0:T(8,128)(2,1)} %param.21), kind=kOutput, calls=%fused_computation.73 | convolution fusion | flops 6442450944 | bytes 19922944 | tf_op jit(solution)/shard_map/dot_general | solution.py:100
  258.2 0.0 copy-done
  258.2 20.5 %convolution_convert_fusion = bf16[2048,3072]{1,0:T(8,128)(2,1)} fusion(bf16[512,3072]{1,0:T(8,128)(2,1)S(1)} %copy-done, f32[2048,512]{1,0:T(8,128)} %fusion.45, bf16[2048,3072]{1,0:T(8,128)(2,1)} %all-gather.2.cloned.1.call-done, bf16[3072,512]{1,0:T(8,128)(2,1)} %param.22), kind=kOutput, calls=%fused_computation.1 | convolution fusion | flops 12897484800 | bytes 35651584 | tf_op jit(solution)/shard_map/dot_general | solution.py:104
  278.7 0.0 reduce-scatter.2.cloned.1.call-update
  278.7 0.0 copy-start.1
  279.6 118.1 %reduce-scatter.2.cloned.1.call-done = bf16[128,3072]{1,0:T(8,128)(2,1)} async-done(((bf16[2048,3072]{1,0:T(8,128)(2,1)}), bf16[128,3072]{1,0:T(8,128)(2,1)}) %reduce-scatter.2.cloned.1.call-update) | async-done | bytes 786448 | tf_op jit(solution)/shard_map/reduce_scatter | solution.py:103
  397.6 3.0 select_convert_fusion
  400.7 0.0 copy-done.1
  (13 shorter events, 0.1 us)
Async XLA Ops:
  6.5 251.7 %copy-start = (bf16[512,3072]{1,0:T(8,128)(2,1)S(1)}, bf16[512,3072]{1,0:T(8,128)(2,1)}, u32[]{:S(2)}) copy-start(bf16[512,3072]{1,0:T(8,128)(2,1)} %param.23) | copy-start | bytes 9437188
  8.7 25.6 %all-to-all-start = ((bf16[16,16,2048]{2,1,0:T(8,128)(2,1)}), bf16[16,16,2048]{2,1,0:T(8,128)(2,1)}, u32[]{:S(2)}, u32[]{:S(2)}) async-start(bf16[16,16,2048]{2,1,0:T(8,128)(2,1)} %broadcast_in_dim.79), calls=%async_computation | async-start | bytes 2097152 | tf_op jit(solution)/shard_map/all_to_all | solution.py:72
  24.4 2.8 copy-start.4
  40.6 2.9 copy-start.6
  40.6 3.8 slice-start
  42.8 1.7 slice-start.1
  44.4 1.2 copy-start.5
  74.1 4.9 %copy-start.7 = (bf16[3072]{0:T(1024)(128)(2,1)S(1)}, bf16[3072]{0:T(1024)(128)(2,1)}, u32[]{:S(2)}) copy-start(bf16[3072]{0:T(1024)(128)(2,1)} %param.20) | copy-start | bytes 18436
  74.1 74.7 %all-to-all-start.2 = ((bf16[8,128,3072]{2,1,0:T(8,128)(2,1)}), bf16[8,128,3072]{2,1,0:T(8,128)(2,1)}, u32[]{:S(2)}, u32[]{:S(2)}) async-start(bf16[8,128,3072]{2,1,0:T(8,128)(2,1)} %bitcast.108), calls=%async_computation.2 | async-start | bytes 12582912 | tf_op jit(solution)/shard_map/all_to_all | solution.py:92
  78.9 167.4 %all-gather.2.cloned.1.call-start = ((), (), s32[]{:S(2)}) async-start(), calls=%async_computation.4 | async-start | bytes 13369344 | tf_op jit(solution)/shard_map/all_gather | solution.py:99
  148.7 4.1 %copy-start.3 = (bf16[128,3072]{1,0:T(8,128)(2,1)S(1)}, bf16[128,3072]{1,0:T(8,128)(2,1)}, u32[]{:S(2)}) copy-start(bf16[128,3072]{1,0:T(8,128)(2,1)} %param.12) | copy-start | bytes 2359300
  152.8 1.2 copy-start.2
  155.2 242.4 %reduce-scatter.2.cloned.1.call-start = ((), (), s32[]{:S(2)}) async-start(), calls=%async_computation.5 | async-start | bytes 13369344 | tf_op jit(solution)/shard_map/reduce_scatter | solution.py:103
  278.7 121.9 %copy-start.1 = (bf16[512,3072]{1,0:T(8,128)(2,1)S(1)}, bf16[512,3072]{1,0:T(8,128)(2,1)}, u32[]{:S(2)}) copy-start(bf16[512,3072]{1,0:T(8,128)(2,1)} %param.23) | copy-start | bytes 9437188
Sparse Core Ops, SparseCore 0:
  155.3 91.0 all-gather.1
  278.8 118.7 reduce-scatter.1

commit v2 on v1

--- a/solution.py
+++ b/solution.py
@@ -85,29 +85,37 @@
     )
     n_group = lax.axis_size("group")
     block = out_weight.shape[0]
-    columns = lax.all_to_all(
-        attended.reshape(rows_here, n_group, block), "group", 1, 0, tiled=False
-    ).reshape(n_group * rows_here, block)
-    partial = jnp.dot(columns, out_weight, preferred_element_type=jnp.float32).astype(jnp.bfloat16)
-    returned = lax.all_to_all(
-        partial.reshape(n_group, rows_here, partial.shape[1]), "group", 0, 0, tiled=False
-    )
-    projected = jnp.sum(returned.astype(jnp.float32), axis=0)
-    mixed = layer_input.astype(jnp.float32) + projected
-    scale = lax.rsqrt(jnp.mean(mixed * mixed, axis=-1, keepdims=True) + 1e-05)
-    normed = (mixed * scale * norm_gain.astype(jnp.float32)).astype(jnp.bfloat16)
-    gathered = lax.all_gather(normed, "req", axis=0, tiled=True)
-    gate = jnp.dot(gathered, gate_weight, preferred_element_type=jnp.float32)
-    upper = jnp.dot(gathered, up_weight, preferred_element_type=jnp.float32)
-    hidden = (jax.nn.silu(gate) * upper).astype(jnp.bfloat16)
-    feed = lax.psum_scatter(
-        jnp.dot(hidden, down_weight, preferred_element_type=jnp.float32).astype(jnp.bfloat16),
-        "req",
-        scatter_dimension=0,
-        tiled=True,
-    ).astype(jnp.float32)
-    live = offsets < suffix_len[0]
-    return jnp.where(live[:, None], mixed + feed, 0.0).astype(jnp.bfloat16)
+    chunks = 2
+    size = rows_here // chunks
+    outputs = []
+    for c in range(chunks):
+        rows = slice(c * size, (c + 1) * size)
+        columns = lax.all_to_all(
+            attended[rows].reshape(size, n_group, block), "group", 1, 0, tiled=False
+        ).reshape(n_group * size, block)
+        partial = jnp.dot(columns, out_weight, preferred_element_type=jnp.float32).astype(
+            jnp.bfloat16
+        )
+        returned = lax.all_to_all(
+            partial.reshape(n_group, size, partial.shape[1]), "group", 0, 0, tiled=False
+        )
+        projected = jnp.sum(returned.astype(jnp.float32), axis=0)
+        mixed = layer_input[rows].astype(jnp.float32) + projected
+        scale = lax.rsqrt(jnp.mean(mixed * mixed, axis=-1, keepdims=True) + 1e-05)
+        normed = (mixed * scale * norm_gain.astype(jnp.float32)).astype(jnp.bfloat16)
+        gathered = lax.all_gather(normed, "req", axis=0, tiled=True)
+        gate = jnp.dot(gathered, gate_weight, preferred_element_type=jnp.float32)
+        upper = jnp.dot(gathered, up_weight, preferred_element_type=jnp.float32)
+        hidden = (jax.nn.silu(gate) * upper).astype(jnp.bfloat16)
+        feed = lax.psum_scatter(
+            jnp.dot(hidden, down_weight, preferred_element_type=jnp.float32).astype(jnp.bfloat16),
+            "req",
+            scatter_dimension=0,
+            tiled=True,
+        ).astype(jnp.float32)
+        live = offsets[rows] < suffix_len[0]
+        outputs.append(jnp.where(live[:, None], mixed + feed, 0.0).astype(jnp.bfloat16))
+    return jnp.concatenate(outputs, axis=0)
 
 
 def solution(mesh):

time: 408 us -> 481 us (1.18)
  waiting for transfers between devices: 283 us -> 344 us
  blocking collectives: 16.7 us -> 0 us
  starting transfers between devices: 13.6 us -> 27.9 us
  matrix products: 47.7 us -> 60.8 us
    reduce_scatter x1 -> x2, waiting for transfers between devices: 118 us -> 161 us  [shards(): lax.psum_scatter(jnp.dot(hidden, down_weight, preferred_element_type=jnp....]
    all_to_all x1 -> x0, blocking collectives: 16.7 us -> none  [shards(): lax.all_to_all(attended.reshape(rows_here, n_group, block), 'group', 1, 0...]
    all_gather x1 -> x2, waiting for transfers between devices: 90.9 us -> 107 us  [shards(): gathered = lax.all_gather(normed, 'req', axis=0, tiled=True)]
    all_to_all x1 -> x4, starting transfers between devices: 4.87 us -> 19.2 us  [the longest x2 10.6 us: shards(): lax.all_to_all(partial.reshape(n_group, size, partial.shape[1]), 'group',...]
    dot_general x1 -> x2, matrix products: 11.8 us -> 16.9 us  [shards(): gate = jnp.dot(gathered, gate_weight, preferred_element_type=jnp.float32)]
    dot_general x1 -> x2, matrix products: 20.5 us -> 24.4 us  [shards(): jnp.dot(hidden, down_weight, preferred_element_type=jnp.float32)]
    dot_general x1 -> x2, matrix products: 6.97 us -> 10.5 us  [shards(): jnp.dot(columns, out_weight, preferred_element_type=jnp.float32)]
    all_to_all x1 -> x4, waiting for transfers between devices: 69.7 us -> 70.2 us  [the longest x2 62.2 us: shards(): lax.all_to_all(partial.reshape(n_group, size, partial.shape[1]), 'group',...]
  transfers between devices with their start and end apart: 4 -> 9, of which waited for: 4 -> 9; matrix products, arithmetic and copies ran while one was open for 3% -> 14% of each run, Pallas kernels for 0% -> 0%
where the time goes in v2:
time: 481 us; the launch traced here: 480 us
  waiting for transfers between devices  344 us (72%)
  matrix products  60.8 us (13%)
  starting transfers between devices  27.9 us (6%)
  local copies, waits for them, and re-layouts  17.3 us (4%)
  other arithmetic  15.4 us (3%)
  between operations  14.7 us (3%)
    reduce_scatter x2, waiting for transfers between devices, shards(): lax.psum_scatter(jnp.dot(hidden, down_weight, preferred_element_type=jnp....  161 us
    all_gather x2, waiting for transfers between devices, shards(): gathered = lax.all_gather(normed, 'req', axis=0, tiled=True)  107 us
    all_to_all x2, waiting for transfers between devices, shards(): lax.all_to_all(partial.reshape(n_group, size, partial.shape[1]), 'group',...  62.2 us
    dot_general x2, matrix products, shards(): jnp.dot(hidden, down_weight, preferred_element_type=jnp.float32)  24.4 us
    dot_general x2, matrix products, shards(): gate = jnp.dot(gathered, gate_weight, preferred_element_type=jnp.float32)  16.9 us
    all_to_all x2, starting transfers between devices, shards(): lax.all_to_all(partial.reshape(n_group, size, partial.shape[1]), 'group',...  10.6 us
    dot_general x2, matrix products, shards(): jnp.dot(columns, out_weight, preferred_element_type=jnp.float32)  10.5 us
  transfers between devices with their start and end apart: 9, of which 9 were waited for; matrix products, arithmetic and copies ran while one was open for 14% of the time, Pallas kernels for 0%

profile of v2, /device:TPU:1, one launch (start us, length us, event | category | flops | bytes accessed | tf_op | source)
XLA Modules:
  0.0 479.7 jit_solution(9212100602893958897)
XLA Ops:
  6.5 0.0 copy-start
  6.5 2.1 broadcast_in_dim.88
  8.6 8.4 %all-to-all-start = ((bf16[16,16,2048]{2,1,0:T(8,128)(2,1)}), bf16[16,16,2048]{2,1,0:T(8,128)(2,1)}, u32[]{:S(2)}, u32[]{:S(2)}) async-start(bf16[16,16,2048]{2,1,0:T(8,128)(2,1)} %broadcast_in_dim.88), calls=%async_computation | async-start | bytes 2097152 | tf_op jit(solution)/shard_map/all_to_all | solution.py:72
  17.8 2.3 copy.50
  20.0 2.1 copy.51
  22.1 2.3 copy.52
  24.4 2.5 pad_maximum_fusion
  26.9 0.1 fusion.28
  27.0 0.2 fusion.27
  27.2 0.0 copy-done.4
  27.2 3.0 fusion
  30.2 4.0 all-to-all-done
  34.2 2.3 fusion.44
  36.5 2.0 copy.57
  38.5 2.1 copy.60
  40.6 2.1 fusion.3
  42.7 0.0 slice-start.1
  42.7 0.8 fusion.11
  43.5 0.0 copy-done.6
  43.5 1.1 fusion.13
  44.6 0.0 copy-start.5
  44.6 0.0 slice-done
  44.6 0.0 slice-done.1
  44.6 1.2 fusion.1
  45.8 0.0 copy-done.5
  45.8 2.8 fusion.16
  48.7 0.1 fusion.45
  48.7 0.3 copy.85
  49.0 0.8 copy.66
  49.8 5.1 %all-to-all-start.3 = ((bf16[1,64,8,384]{3,1,0,2:T(8,128)(2,1)}), bf16[1,64,8,384]{3,1,0,2:T(8,128)(2,1)}, u32[]{:S(2)}, u32[]{:S(2)}) async-start(bf16[1,64,8,384]{3,1,0,2:T(8,128)(2,1)} %copy.66), calls=%async_computation.4 | async-start | bytes 786432 | tf_op jit(solution)/shard_map/all_to_all | solution.py:93
  54.9 0.3 copy.86
  55.2 0.8 copy.64
  56.0 6.5 %all-to-all-done.3 = bf16[1,64,8,384]{3,1,0,2:T(8,128)(2,1)} async-done(((bf16[1,64,8,384]{3,1,0,2:T(8,128)(2,1)}), bf16[1,64,8,384]{3,1,0,2:T(8,128)(2,1)}, u32[]{:S(2)}, u32[]{:S(2)}) %all-to-all-start.3) | async-done | bytes 393248 | tf_op jit(solution)/shard_map/all_to_all | solution.py:93
  62.5 3.5 all-to-all-start.1
  65.9 5.3 %convolution_convert_fusion.2 = bf16[512,3072]{1,0:T(8,128)(2,1)} fusion(bf16[512,384]{1,0:T(8,128)(2,1)} %bitcast.28, bf16[384,3072]{1,0:T(8,128)(2,1)} %param.19), kind=kOutput, calls=%fused_computation.6 | convolution fusion | flops 1209532416 | bytes 5898240 | tf_op jit(solution)/shard_map/dot_general | solution.py:96
  71.2 1.5 all-to-all-done.1
  72.7 4.5 all-to-all-start.4
  77.2 5.2 %convolution_convert_fusion.3 = bf16[512,3072]{1,0:T(8,128)(2,1)} fusion(bf16[512,384]{1,0:T(8,128)(2,1)S(1)} %bitcast.134, bf16[384,3072]{1,0:T(8,128)(2,1)} %param.19), kind=kOutput, calls=%fused_computation.7 | convolution fusion | flops 1209532416 | bytes 5898240 | tf_op jit(solution)/shard_map/dot_general | solution.py:96
  82.4 29.9 %all-to-all-done.4 = bf16[8,64,3072]{2,1,0:T(8,128)(2,1)} async-done(((bf16[8,64,3072]{2,1,0:T(8,128)(2,1)}), bf16[8,64,3072]{2,1,0:T(8,128)(2,1)}, u32[]{:S(2)}, u32[]{:S(2)}) %all-to-all-start.4) | async-done | bytes 3145760 | tf_op jit(solution)/shard_map/all_to_all | solution.py:99
  112.3 6.2 %all-to-all-start.2 = ((bf16[8,64,3072]{2,1,0:T(8,128)(2,1)}), bf16[8,64,3072]{2,1,0:T(8,128)(2,1)}, u32[]{:S(2)}, u32[]{:S(2)}) async-start(bf16[8,64,3072]{2,1,0:T(8,128)(2,1)} %bitcast.126), calls=%async_computation.2 | async-start | bytes 6291456 | tf_op jit(solution)/shard_map/all_to_all | solution.py:99
  118.4 0.2 all-gather.5.cloned.1.call-start
  118.6 0.0 copy-done.7
  118.7 3.4 convert_reduce_fusion
  122.0 32.3 %all-to-all-done.2 = bf16[8,64,3072]{2,1,0:T(8,128)(2,1)} async-done(((bf16[8,64,3072]{2,1,0:T(8,128)(2,1)}), bf16[8,64,3072]{2,1,0:T(8,128)(2,1)}, u32[]{:S(2)}, u32[]{:S(2)}) %all-to-all-start.2) | async-done | bytes 3145760 | tf_op jit(solution)/shard_map/all_to_all | solution.py:99
  154.3 2.6 convert_reduce_fusion.1
  157.0 0.3 multiply_reduce_fusion.1
  157.3 1.2 multiply_convert_fusion.3
  158.5 0.0 all-gather.5.cloned.1.call-update
  158.5 0.0 all-gather.3.cloned.1.call-start
  158.6 0.7 all-gather.3.cloned.1.call-update
  159.3 0.0 reduce-scatter.5.cloned.1.call-start
  159.3 64.2 %all-gather.5.cloned.1.call-done = bf16[1024,3072]{1,0:T(8,128)(2,1)} async-done(((bf16[64,3072]{1,0:T(8,128)(2,1)}), bf16[1024,3072]{1,0:T(8,128)(2,1)}) %all-gather.5.cloned.1.call-update) | async-done | bytes 6291472 | tf_op jit(solution)/shard_map/all_gather | solution.py:106
  223.6 8.4 %fusion.47 = f32[1024,512]{1,0:T(8,128)} fusion(bf16[1024,3072]{1,0:T(8,128)(2,1)} %all-gather.5.cloned.1.call-done, bf16[3072,512]{1,0:T(8,128)(2,1)} %param.21), kind=kOutput, calls=%fused_computation.88 | convolution fusion | flops 3221225472 | bytes 11534336 | tf_op jit(solution)/shard_map/dot_general | solution.py:107
  232.0 12.3 %convolution_convert_fusion = bf16[1024,3072]{1,0:T(8,128)(2,1)} fusion(bf16[512,3072]{1,0:T(8,128)(2,1)S(1)} %copy-done, f32[1024,512]{1,0:T(8,128)} %fusion.47, bf16[1024,3072]{1,0:T(8,128)(2,1)} %all-gather.5.cloned.1.call-done, bf16[3072,512]{1,0:T(8,128)(2,1)} %param.22), kind=kOutput, calls=%fused_computation.2 | convolution fusion | flops 6448742400 | bytes 20971520 | tf_op jit(solution)/shard_map/dot_general | solution.py:111
  244.3 0.0 reduce-scatter.5.cloned.1.call-update
  244.3 0.0 reduce-scatter.3.cloned.1.call-start
  244.4 43.1 %all-gather.3.cloned.1.call-done = bf16[1024,3072]{1,0:T(8,128)(2,1)} async-done(((bf16[64,3072]{1,0:T(8,128)(2,1)}), bf16[1024,3072]{1,0:T(8,128)(2,1)}) %all-gather.3.cloned.1.call-update) | async-done | bytes 6291472 | tf_op jit(solution)/shard_map/all_gather | solution.py:106
  287.5 8.4 %fusion.46 = f32[1024,512]{1,0:T(8,128)} fusion(bf16[1024,3072]{1,0:T(8,128)(2,1)} %all-gather.3.cloned.1.call-done, bf16[3072,512]{1,0:T(8,128)(2,1)} %param.21), kind=kOutput, calls=%fused_computation.87 | convolution fusion | flops 3221225472 | bytes 11534336 | tf_op jit(solution)/shard_map/dot_general | solution.py:107
  295.9 12.2 %convolution_convert_fusion.1 = bf16[1024,3072]{1,0:T(8,128)(2,1)} fusion(bf16[512,3072]{1,0:T(8,128)(2,1)S(1)} %copy-done, f32[1024,512]{1,0:T(8,128)} %fusion.46, bf16[1024,3072]{1,0:T(8,128)(2,1)} %all-gather.3.cloned.1.call-done, bf16[3072,512]{1,0:T(8,128)(2,1)} %param.22), kind=kOutput, calls=%fused_computation.3 | convolution fusion | flops 6448742400 | bytes 20971520 | tf_op jit(solution)/shard_map/dot_general | solution.py:111
  308.1 0.0 reduce-scatter.3.cloned.1.call-update
  308.8 0.1 slice_compare_fusion
  308.8 68.6 %reduce-scatter.5.cloned.1.call-done = bf16[64,3072]{1,0:T(8,128)(2,1)} async-done(((bf16[1024,3072]{1,0:T(8,128)(2,1)}), bf16[64,3072]{1,0:T(8,128)(2,1)}) %reduce-scatter.5.cloned.1.call-update) | async-done | bytes 393232 | tf_op jit(solution)/shard_map/reduce_scatter | solution.py:110
  377.4 92.7 %reduce-scatter.3.cloned.1.call-done = bf16[64,3072]{1,0:T(8,128)(2,1)} async-done(((bf16[1024,3072]{1,0:T(8,128)(2,1)}), bf16[64,3072]{1,0:T(8,128)(2,1)}) %reduce-scatter.3.cloned.1.call-update) | async-done | bytes 393232 | tf_op jit(solution)/shard_map/reduce_scatter | solution.py:110
  470.1 3.0 select_convert_fusion.1
  (26 shorter events, 0.1 us)
Async XLA Ops:
  6.5 225.5 %copy-start = (bf16[512,3072]{1,0:T(8,128)(2,1)S(1)}, bf16[512,3072]{1,0:T(8,128)(2,1)}, u32[]{:S(2)}) copy-start(bf16[512,3072]{1,0:T(8,128)(2,1)} %param.23) | copy-start | bytes 9437188
  8.6 25.6 %all-to-all-start = ((bf16[16,16,2048]{2,1,0:T(8,128)(2,1)}), bf16[16,16,2048]{2,1,0:T(8,128)(2,1)}, u32[]{:S(2)}, u32[]{:S(2)}) async-start(bf16[16,16,2048]{2,1,0:T(8,128)(2,1)} %broadcast_in_dim.88), calls=%async_computation | async-start | bytes 2097152 | tf_op jit(solution)/shard_map/all_to_all | solution.py:72
  24.4 2.8 copy-start.4
  40.6 2.9 copy-start.6
  40.6 4.0 slice-start
  42.7 1.9 slice-start.1
  44.6 1.2 copy-start.5
  49.8 12.7 %all-to-all-start.3 = ((bf16[1,64,8,384]{3,1,0,2:T(8,128)(2,1)}), bf16[1,64,8,384]{3,1,0,2:T(8,128)(2,1)}, u32[]{:S(2)}, u32[]{:S(2)}) async-start(bf16[1,64,8,384]{3,1,0,2:T(8,128)(2,1)} %copy.66), calls=%async_computation.4 | async-start | bytes 786432 | tf_op jit(solution)/shard_map/all_to_all | solution.py:93
  62.5 10.3 %all-to-all-start.1 = ((bf16[1,64,8,384]{3,1,0,2:T(8,128)(2,1)}), bf16[1,64,8,384]{3,1,0,2:T(8,128)(2,1)S(1)}, u32[]{:S(2)}, u32[]{:S(2)}) async-start(bf16[1,64,8,384]{3,1,0,2:T(8,128)(2,1)} %copy.64), calls=%async_computation.1 | async-start | bytes 786432 | tf_op jit(solution)/shard_map/all_to_all | solution.py:93
  72.7 39.5 %all-to-all-start.4 = ((bf16[8,64,3072]{2,1,0:T(8,128)(2,1)}), bf16[8,64,3072]{2,1,0:T(8,128)(2,1)}, u32[]{:S(2)}, u32[]{:S(2)}) async-start(bf16[8,64,3072]{2,1,0:T(8,128)(2,1)} %bitcast.127), calls=%async_computation.5 | async-start | bytes 6291456 | tf_op jit(solution)/shard_map/all_to_all | solution.py:99
  112.3 6.4 %copy-start.7 = (bf16[3072]{0:T(1024)(128)(2,1)S(1)}, bf16[3072]{0:T(1024)(128)(2,1)}, u32[]{:S(2)}) copy-start(bf16[3072]{0:T(1024)(128)(2,1)} %param.20) | copy-start | bytes 18436
  112.3 42.1 %all-to-all-start.2 = ((bf16[8,64,3072]{2,1,0:T(8,128)(2,1)}), bf16[8,64,3072]{2,1,0:T(8,128)(2,1)}, u32[]{:S(2)}, u32[]{:S(2)}) async-start(bf16[8,64,3072]{2,1,0:T(8,128)(2,1)} %bitcast.126), calls=%async_computation.2 | async-start | bytes 6291456 | tf_op jit(solution)/shard_map/all_to_all | solution.py:99
  118.4 105.1 %all-gather.5.cloned.1.call-start = ((), (), s32[]{:S(2)}) async-start(), calls=%async_computation.9 | async-start | bytes 6684672 | tf_op jit(solution)/shard_map/all_gather | solution.py:106
  154.3 2.6 copy-start.1
  154.3 2.6 copy-start.3
  157.0 1.5 copy-start.2
  158.5 128.9 %all-gather.3.cloned.1.call-start = ((), (), s32[]{:S(2)}) async-start(), calls=%async_computation.7 | async-start | bytes 6684672 | tf_op jit(solution)/shard_map/all_gather | solution.py:106
  159.3 218.1 %reduce-scatter.5.cloned.1.call-start = ((), (), s32[]{:S(2)}) async-start(), calls=%async_computation.10 | async-start | bytes 6684672 | tf_op jit(solution)/shard_map/reduce_scatter | solution.py:110
  244.3 225.8 %reduce-scatter.3.cloned.1.call-start = ((), (), s32[]{:S(2)}) async-start(), calls=%async_computation.8 | async-start | bytes 6684672 | tf_op jit(solution)/shard_map/reduce_scatter | solution.py:110
Sparse Core Ops, SparseCore 0:
  158.7 64.8 all-gather.4
  226.0 61.3 all-gather.2
  291.7 85.7 reduce-scatter.4
  381.5 88.5 reduce-scatter.2

commit v3 on v1

--- a/solution.py
+++ b/solution.py
@@ -7,6 +7,9 @@
 KV_HEADS = 8
 HEAD = 128
 SINK = 4
+GROUP = ("z", "x_lo")
+REQ = ("x_hi", "y", "core")
+ALL = GROUP + REQ
 
 
 def absorb(state, query_heads, key_rows, key_pos, key_valid, query_pos, window):
@@ -50,7 +53,7 @@
 ):
     rows_here = queries.shape[0]
     past_slots = past_kv.shape[0]
-    prefix_total = prefix_kv.shape[0] * lax.axis_size("req")
+    prefix_total = prefix_kv.shape[0] * lax.axis_size(REQ)
     window = prefix_total + past_slots // 2
     past_count = past_len[0]
     offsets = jnp.arange(rows_here, dtype=jnp.int32)
@@ -68,9 +71,9 @@
         [jnp.arange(past_slots, dtype=jnp.int32) < past_count, jnp.ones((rows_here,), bool)]
     )
     state = absorb(state, query_heads, local_rows, local_pos, local_valid, query_pos, window)
-    n_req = lax.axis_size("req")
+    n_req = lax.axis_size(REQ)
     piece = lax.all_to_all(
-        jnp.broadcast_to(prefix_kv[None], (n_req,) + prefix_kv.shape), "req", 0, 0, tiled=False
+        jnp.broadcast_to(prefix_kv[None], (n_req,) + prefix_kv.shape), REQ, 0, 0, tiled=False
     ).reshape(prefix_total, prefix_kv.shape[1])
     count = piece.shape[0]
     positions = jnp.arange(count, dtype=jnp.int32)
@@ -83,26 +86,31 @@
         .reshape(rows_here, HEADS * HEAD)
         .astype(jnp.bfloat16)
     )
-    n_group = lax.axis_size("group")
-    block = out_weight.shape[0]
+    pair = lax.all_gather(out_weight, "x_lo", axis=0, tiled=True)
+    n_z = lax.axis_size("z")
+    block = pair.shape[0]
     columns = lax.all_to_all(
-        attended.reshape(rows_here, n_group, block), "group", 1, 0, tiled=False
-    ).reshape(n_group * rows_here, block)
-    partial = jnp.dot(columns, out_weight, preferred_element_type=jnp.float32).astype(jnp.bfloat16)
+        attended.reshape(rows_here, n_z, block), "z", 1, 0, tiled=False
+    ).reshape(n_z * rows_here, block)
+    partial = jnp.dot(columns, pair, preferred_element_type=jnp.float32).astype(jnp.bfloat16)
     returned = lax.all_to_all(
-        partial.reshape(n_group, rows_here, partial.shape[1]), "group", 0, 0, tiled=False
+        partial.reshape(n_z, rows_here, partial.shape[1]), "z", 0, 0, tiled=False
     )
     projected = jnp.sum(returned.astype(jnp.float32), axis=0)
     mixed = layer_input.astype(jnp.float32) + projected
     scale = lax.rsqrt(jnp.mean(mixed * mixed, axis=-1, keepdims=True) + 1e-05)
     normed = (mixed * scale * norm_gain.astype(jnp.float32)).astype(jnp.bfloat16)
-    gathered = lax.all_gather(normed, "req", axis=0, tiled=True)
-    gate = jnp.dot(gathered, gate_weight, preferred_element_type=jnp.float32)
-    upper = jnp.dot(gathered, up_weight, preferred_element_type=jnp.float32)
+    swap = [(0, 1), (1, 0)]
+    gate_both = jnp.concatenate([gate_weight, lax.ppermute(gate_weight, "core", swap)], axis=1)
+    up_both = jnp.concatenate([up_weight, lax.ppermute(up_weight, "core", swap)], axis=1)
+    down_both = jnp.concatenate([down_weight, lax.ppermute(down_weight, "core", swap)], axis=0)
+    gathered = lax.all_gather(normed, ("x_hi", "y"), axis=0, tiled=True)
+    gate = jnp.dot(gathered, gate_both, preferred_element_type=jnp.float32)
+    upper = jnp.dot(gathered, up_both, preferred_element_type=jnp.float32)
     hidden = (jax.nn.silu(gate) * upper).astype(jnp.bfloat16)
     feed = lax.psum_scatter(
-        jnp.dot(hidden, down_weight, preferred_element_type=jnp.float32).astype(jnp.bfloat16),
-        "req",
+        jnp.dot(hidden, down_both, preferred_element_type=jnp.float32).astype(jnp.bfloat16),
+        ("x_hi", "y"),
         scatter_dimension=0,
         tiled=True,
     ).astype(jnp.float32)
@@ -111,19 +119,21 @@
 
 
 def solution(mesh):
+    sizes = [mesh.shape["group"] // 2, 2, 2, mesh.shape["req"] // 4, 2]
+    fine = jax.sharding.Mesh(mesh.devices.reshape(sizes), ALL)
     in_specs = (
-        P(("group", "req"), None),
-        P(("group", "req"), None),
-        P(("group", "req"), None),
-        P(("group", "req"), None),
-        P(("group", "req"), None),
-        P(("group", "req")),
-        P(("group", "req")),
-        P("group", None),
+        P(ALL, None),
+        P(ALL, None),
+        P(ALL, None),
+        P(ALL, None),
+        P(ALL, None),
+        P(ALL),
+        P(ALL),
+        P(GROUP, None),
         P(),
-        P(None, "req"),
-        P(None, "req"),
-        P("req", None),
+        P(None, REQ),
+        P(None, REQ),
+        P(REQ, None),
     )
-    out_specs = P(("group", "req"), None)
-    return jax.shard_map(shards, mesh=mesh, in_specs=in_specs, out_specs=out_specs, check_vma=False)
+    out_specs = P(ALL, None)
+    return jax.shard_map(shards, mesh=fine, in_specs=in_specs, out_specs=out_specs, check_vma=False)

time: 408 us -> 362 us (0.89)
  waiting for transfers between devices: 283 us -> 255 us
  local copies, waits for them, and re-layouts: 18.3 us -> 7.51 us
  matrix products: 47.7 us -> 42.4 us
    all_to_all x1, waiting for transfers between devices: 69.7 us -> 36.8 us  [shards(): lax.all_to_all(partial.reshape(n_z, rows_here, partial.shape[1]), 'z', 0,...]
    reduce_scatter x1, waiting for transfers between devices: 118 us -> 95.3 us  [shards(): lax.psum_scatter(jnp.dot(hidden, down_both, preferred_element_type=jnp.fl...]
    all_gather x1 -> x2, waiting for transfers between devices: 90.9 us -> 110 us  [the longest x1 80.5 us: shards(): gathered = lax.all_gather(normed, ('x_hi', 'y'), axis=0, tiled=True)]
    ppermute x0 -> x3, waiting for transfers between devices: none -> 5.12 us  [the longest x1 5.12 us: shards(): lax.ppermute(gate_weight, 'core', swap)]
    dot_general x3 -> x4, matrix products: 39.3 us -> 36.3 us  [the longest x1 10.7 us: shards(): gate = jnp.dot(gathered, gate_both, preferred_element_type=jnp.float32)]
  transfers between devices with their start and end apart: 4 -> 8, of which waited for: 4 -> 6; matrix products, arithmetic and copies ran while one was open for 3% -> 9% of each run, Pallas kernels for 0% -> 0%
where the time goes in v3:
time: 362 us; the launch traced here: 361 us
  waiting for transfers between devices  255 us (70%)
  matrix products  42.4 us (12%)
  blocking collectives  16 us (4%)
  starting transfers between devices  15.6 us (4%)
  between operations  14.7 us (4%)
  other arithmetic  9.79 us (3%)
  local copies, waits for them, and re-layouts  7.51 us (2%)
    reduce_scatter x1, waiting for transfers between devices, shards(): lax.psum_scatter(jnp.dot(hidden, down_both, preferred_element_type=jnp.fl...  95.3 us
    all_gather x1, waiting for transfers between devices, shards(): gathered = lax.all_gather(normed, ('x_hi', 'y'), axis=0, tiled=True)  80.5 us
    all_to_all x1, waiting for transfers between devices, shards(): lax.all_to_all(partial.reshape(n_z, rows_here, partial.shape[1]), 'z', 0,...  36.8 us
    all_gather x1, waiting for transfers between devices, shards(): pair = lax.all_gather(out_weight, 'x_lo', axis=0, tiled=True)  29.1 us
    all_to_all x1, blocking collectives, shards(): lax.all_to_all(attended.reshape(rows_here, n_z, block), 'z', 1, 0, tiled=...  16 us
    dot_general x1, matrix products, shards(): gate = jnp.dot(gathered, gate_both, preferred_element_type=jnp.float32)  10.7 us
    dot_general x1, matrix products, shards(): jnp.dot(hidden, down_both, preferred_element_type=jnp.float32)  10.6 us
    dot_general x1, matrix products, shards(): upper = jnp.dot(gathered, up_both, preferred_element_type=jnp.float32)  8.67 us
  transfers between devices with their start and end apart: 8, of which 6 were waited for; matrix products, arithmetic and copies ran while one was open for 9% of the time, Pallas kernels for 0%

profile of v3, /device:TPU:1, one launch (start us, length us, event | category | flops | bytes accessed | tf_op | source)
XLA Modules:
  0.0 361.3 jit_solution(1225307912721061585)
XLA Ops:
  6.5 0.0 copy-start.1
  6.5 2.0 broadcast_in_dim.79
  8.5 8.4 %all-to-all-start = ((bf16[16,16,2048]{2,1,0:T(8,128)(2,1)}), bf16[16,16,2048]{2,1,0:T(8,128)(2,1)S(1)}, u32[]{:S(2)}, u32[]{:S(2)}) async-start(bf16[16,16,2048]{2,1,0:T(8,128)(2,1)} %broadcast_in_dim.79), calls=%async_computation | async-start | bytes 2097152 | tf_op jit(solution)/shard_map/all_to_all | solution.py:75
  17.0 0.0 all-gather.3.cloned.1.call-start
  17.0 0.7 all-gather.3.cloned.1.call-update
  18.4 0.0 copy-done.1
  18.4 0.5 copy.31
  19.0 1.3 copy.32
  20.3 1.5 copy.33
  21.8 1.0 pad_maximum_fusion
  22.9 0.1 fusion.44
  23.0 0.2 fusion.43
  23.2 3.1 fusion.15
  26.3 7.8 %all-to-all-done = bf16[16,16,2048]{2,1,0:T(8,128)(2,1)S(1)} async-done(((bf16[16,16,2048]{2,1,0:T(8,128)(2,1)}), bf16[16,16,2048]{2,1,0:T(8,128)(2,1)S(1)}, u32[]{:S(2)}, u32[]{:S(2)}) %all-to-all-start) | async-done | bytes 1048608 | tf_op jit(solution)/shard_map/all_to_all | solution.py:75
  34.1 0.1 fusion.62
  34.1 0.2 copy.37
  34.4 0.0 slice-start
  34.4 0.2 copy.40
  34.6 0.0 slice-start.1
  34.6 0.7 fusion.18
  35.3 0.8 fusion.26
  36.1 0.0 slice-done
  36.1 1.1 slice-done.1
  37.1 1.1 fusion.16
  38.3 0.0 copy-start.2
  38.3 0.8 fusion.29
  39.2 0.3 copy-done.2
  39.4 1.5 fusion.32
  41.0 0.3 copy.42
  41.3 16.0 %all_to_all.25 = bf16[1,128,4,768]{3,1,0,2:T(8,128)(2,1)S(1)} all-to-all(bf16[1,128,4,768]{3,1,0,2:T(8,128)(2,1)S(1)} %copy.42), channel_id=1, replica_groups=mesh['z'=4,'x_lo'=2,'x_hi'=2,'y'=4,'core'=2] {'z'}, dimensions={2} | all-to-all | bytes 1572864 | tf_op jit(solution)/shard_map/all_to_all | solution.py:92
  57.3 29.1 %all-gather.3.cloned.1.call-done = bf16[768,3072]{1,0:T(8,128)(2,1)} async-done(((bf16[384,3072]{1,0:T(8,128)(2,1)}), bf16[768,3072]{1,0:T(8,128)(2,1)}) %all-gather.3.cloned.1.call-update) | async-done | bytes 4718608 | tf_op jit(solution)/shard_map/all_gather | solution.py:89
  86.4 6.3 %convolution_convert_fusion = bf16[512,3072]{1,0:T(8,128)(2,1)} fusion(bf16[512,768]{1,0:T(8,128)(2,1)S(1)} %bitcast.109, bf16[768,3072]{1,0:T(8,128)(2,1)} %all-gather.3.cloned.1.call-done), kind=kOutput, calls=%fused_computation.16 | convolution fusion | flops 2417491968 | bytes 8650752 | tf_op jit(solution)/shard_map/dot_general | solution.py:95
  92.7 0.0 copy-start.3
  92.7 4.8 %all-to-all-start.2 = ((bf16[4,128,3072]{2,1,0:T(8,128)(2,1)}), bf16[4,128,3072]{2,1,0:T(8,128)(2,1)}, u32[]{:S(2)}, u32[]{:S(2)}) async-start(bf16[4,128,3072]{2,1,0:T(8,128)(2,1)} %bitcast.26), calls=%async_computation.2 | async-start | bytes 6291456 | tf_op jit(solution)/shard_map/all_to_all | solution.py:96
  97.5 0.0 copy-start
  97.5 0.0 all-gather.5.cloned.1.call-start
  97.6 0.0 copy-done.3
  97.6 36.8 %all-to-all-done.2 = bf16[4,128,3072]{2,1,0:T(8,128)(2,1)} async-done(((bf16[4,128,3072]{2,1,0:T(8,128)(2,1)}), bf16[4,128,3072]{2,1,0:T(8,128)(2,1)}, u32[]{:S(2)}, u32[]{:S(2)}) %all-to-all-start.2) | async-done | bytes 3145760 | tf_op jit(solution)/shard_map/all_to_all | solution.py:96
  134.4 2.6 convert_reduce_fusion
  137.0 0.0 copy-done
  137.0 0.3 multiply_reduce_fusion
  137.3 1.2 multiply_convert_fusion.2
  138.5 0.0 all-gather.5.cloned.1.call-update
  138.5 0.0 reduce-scatter.2.cloned.1.call-start
  138.5 1.8 collective-permute-start
  140.3 0.1 collective-permute-start.1
  140.4 0.4 collective-permute-start.2
  140.8 5.1 %collective-permute-done = bf16[3072,512]{1,0:T(8,128)(2,1)} collective-permute-done((bf16[3072,512]{1,0:T(8,128)(2,1)}, bf16[3072,512]{1,0:T(8,128)(2,1)}, u32[]{:S(2)}, u32[]{:S(2)}) %collective-permute-start) | collective-permute-done | bytes 3145760 | tf_op jit(solution)/shard_map/ppermute | solution.py:104
  145.9 80.5 %all-gather.5.cloned.1.call-done = bf16[1024,3072]{1,0:T(8,128)(2,1)} async-done(((bf16[128,3072]{1,0:T(8,128)(2,1)}), bf16[1024,3072]{1,0:T(8,128)(2,1)}) %all-gather.5.cloned.1.call-update) | async-done | bytes 6291472 | tf_op jit(solution)/shard_map/all_gather | solution.py:107
  226.4 0.0 copy-start.4
  226.4 0.0 copy-start.5
  226.4 10.7 %fusion = f32[1024,1024]{1,0:T(8,128)S(1)} fusion(bf16[1024,3072]{1,0:T(8,128)(2,1)} %all-gather.5.cloned.1.call-done, bf16[3072,512]{1,0:T(8,128)(2,1)} %collective-permute-done, bf16[3072,512]{1,0:T(8,128)(2,1)} %param.21), kind=kOutput, calls=%fused_computation | convolution fusion | flops 6455033856 | bytes 16777216 | tf_op jit(solution)/shard_map/dot_general | solution.py:108
  237.2 0.0 copy-start.6
  237.2 0.0 collective-permute-done.1
  237.2 0.0 copy-done.4
  237.2 0.0 copy-done.5
  237.2 8.7 %fusion.4 = f32[1024,1024]{1,0:T(8,128)S(1)} fusion(bf16[1024,3072]{1,0:T(8,128)(2,1)S(1)} %copy-done.4, bf16[3072,512]{1,0:T(8,128)(2,1)} %collective-permute-done.1, bf16[3072,512]{1,0:T(8,128)(2,1)S(1)} %copy-done.5), kind=kOutput, calls=%fused_computation.4 | convolution fusion | flops 6455033856 | bytes 16777216 | tf_op jit(solution)/shard_map/dot_general | solution.py:109
  245.9 0.0 collective-permute-done.2
  245.9 0.0 copy-done.6
  245.9 10.6 %fusion.12 = bf16[1024,3072]{1,0:T(8,128)(2,1)} fusion(bf16[512,3072]{1,0:T(8,128)(2,1)} %collective-permute-done.2, bf16[512,3072]{1,0:T(8,128)(2,1)S(1)} %copy-done.6, f32[1024,1024]{1,0:T(8,128)S(1)} %fusion.4, f32[1024,1024]{1,0:T(8,128)S(1)} %fusion), kind=kOutput, calls=%fused_computation.13 | convolution fusion | flops 6464471040 | bytes 20971520 | tf_op jit(solution)/shard_map/dot_general | solution.py:112
  256.5 0.0 reduce-scatter.2.cloned.1.call-update
  257.2 95.3 %reduce-scatter.2.cloned.1.call-done = bf16[128,3072]{1,0:T(8,128)(2,1)} async-done(((bf16[1024,3072]{1,0:T(8,128)(2,1)}), bf16[128,3072]{1,0:T(8,128)(2,1)}) %reduce-scatter.2.cloned.1.call-update) | async-done | bytes 786448 | tf_op jit(solution)/shard_map/reduce_scatter | solution.py:111
  352.4 2.3 select_convert_fusion
  (13 shorter events, 0.1 us)
Async XLA Ops:
  6.5 11.9 %copy-start.1 = (bf16[256,2048]{1,0:T(8,128)(2,1)S(1)}, bf16[256,2048]{1,0:T(8,128)(2,1)}, u32[]{:S(2)}) copy-start(bf16[256,2048]{1,0:T(8,128)(2,1)} %param.15) | copy-start | bytes 3145732
  8.5 25.5 %all-to-all-start = ((bf16[16,16,2048]{2,1,0:T(8,128)(2,1)}), bf16[16,16,2048]{2,1,0:T(8,128)(2,1)S(1)}, u32[]{:S(2)}, u32[]{:S(2)}) async-start(bf16[16,16,2048]{2,1,0:T(8,128)(2,1)} %broadcast_in_dim.79), calls=%async_computation | async-start | bytes 2097152 | tf_op jit(solution)/shard_map/all_to_all | solution.py:75
  17.0 69.5 %all-gather.3.cloned.1.call-start = ((), (), s32[]{:S(2)}) async-start(), calls=%async_computation.4 | async-start | bytes 7077888 | tf_op jit(solution)/shard_map/all_gather | solution.py:89
  34.4 1.7 slice-start
  34.6 2.6 slice-start.1
  38.3 1.1 copy-start.2
  92.7 4.8 %copy-start.3 = (bf16[3072]{0:T(1024)(128)(2,1)S(1)}, bf16[3072]{0:T(1024)(128)(2,1)}, u32[]{:S(2)}) copy-start(bf16[3072]{0:T(1024)(128)(2,1)} %param.20) | copy-start | bytes 18436
  92.7 41.7 %all-to-all-start.2 = ((bf16[4,128,3072]{2,1,0:T(8,128)(2,1)}), bf16[4,128,3072]{2,1,0:T(8,128)(2,1)}, u32[]{:S(2)}, u32[]{:S(2)}) async-start(bf16[4,128,3072]{2,1,0:T(8,128)(2,1)} %bitcast.26), calls=%async_computation.2 | async-start | bytes 6291456 | tf_op jit(solution)/shard_map/all_to_all | solution.py:96
  97.5 39.5 %copy-start = (bf16[128,3072]{1,0:T(8,128)(2,1)S(1)}, bf16[128,3072]{1,0:T(8,128)(2,1)}, u32[]{:S(2)}) copy-start(bf16[128,3072]{1,0:T(8,128)(2,1)} %param.12) | copy-start | bytes 2359300
  97.5 128.9 %all-gather.5.cloned.1.call-start = ((), (), s32[]{:S(2)}) async-start(), calls=%async_computation.5 | async-start | bytes 7077888 | tf_op jit(solution)/shard_map/all_gather | solution.py:107
  138.5 213.9 %reduce-scatter.2.cloned.1.call-start = ((), (), s32[]{:S(2)}) async-start(), calls=%async_computation.6 | async-start | bytes 7077888 | tf_op jit(solution)/shard_map/reduce_scatter | solution.py:111
  138.5 7.4 %collective-permute-start = (bf16[3072,512]{1,0:T(8,128)(2,1)}, bf16[3072,512]{1,0:T(8,128)(2,1)}, u32[]{:S(2)}, u32[]{:S(2)}) collective-permute-start(bf16[3072,512]{1,0:T(8,128)(2,1)} %param.21), channel_id=1, source_target_pairs={{0,1},{1,0},{2,3},{3,2},{4,5},{5,4},{6,7},{7,6},{8,9},{9,8},{10,11... | collective-permute-start | bytes 9437192 | tf_op jit(solution)/shard_map/ppermute | solution.py:104
  140.3 96.8 %collective-permute-start.1 = (bf16[3072,512]{1,0:T(8,128)(2,1)}, bf16[3072,512]{1,0:T(8,128)(2,1)}, u32[]{:S(2)}, u32[]{:S(2)}) collective-permute-start(bf16[3072,512]{1,0:T(8,128)(2,1)} %param.22), channel_id=1, source_target_pairs={{0,1},{1,0},{2,3},{3,2},{4,5},{5,4},{6,7},{7,6},{8,9},{9,8},{10,11... | collective-permute-start | bytes 9437192 | tf_op jit(solution)/shard_map/ppermute | solution.py:105
  140.4 105.5 %collective-permute-start.2 = (bf16[512,3072]{1,0:T(8,128)(2,1)}, bf16[512,3072]{1,0:T(8,128)(2,1)}, u32[]{:S(2)}, u32[]{:S(2)}) collective-permute-start(bf16[512,3072]{1,0:T(8,128)(2,1)} %param.23), channel_id=1, source_target_pairs={{0,1},{1,0},{2,3},{3,2},{4,5},{5,4},{6,7},{7,6},{8,9},{9,8},{10,11... | collective-permute-start | bytes 9437192 | tf_op jit(solution)/shard_map/ppermute | solution.py:106
  226.4 10.8 %copy-start.4 = (bf16[1024,3072]{1,0:T(8,128)(2,1)S(1)}, bf16[1024,3072]{1,0:T(8,128)(2,1)}, u32[]{:S(2)}) copy-start(bf16[1024,3072]{1,0:T(8,128)(2,1)} %all-gather.5.cloned.1.call-done) | copy-start | bytes 18874372
  226.4 10.8 %copy-start.5 = (bf16[3072,512]{1,0:T(8,128)(2,1)S(1)}, bf16[3072,512]{1,0:T(8,128)(2,1)}, u32[]{:S(2)}) copy-start(bf16[3072,512]{1,0:T(8,128)(2,1)} %param.22) | copy-start | bytes 9437188
  237.2 8.7 %copy-start.6 = (bf16[512,3072]{1,0:T(8,128)(2,1)S(1)}, bf16[512,3072]{1,0:T(8,128)(2,1)}, u32[]{:S(2)}) copy-start(bf16[512,3072]{1,0:T(8,128)(2,1)} %param.23) | copy-start | bytes 9437188
Sparse Core Ops, SparseCore 0:
  19.4 66.9 all-gather.2
  138.6 87.7 all-gather.4
  256.6 95.7 reduce-scatter.1

commit v4 on v3

--- a/solution.py
+++ b/solution.py
@@ -86,11 +86,13 @@
         .reshape(rows_here, HEADS * HEAD)
         .astype(jnp.bfloat16)
     )
-    pair = lax.all_gather(out_weight, "x_lo", axis=0, tiled=True)
+    pair = jnp.concatenate([out_weight, lax.ppermute(out_weight, "x_lo", [(0, 1), (1, 0)])])
     n_z = lax.axis_size("z")
     block = pair.shape[0]
+    halves = attended.reshape(rows_here, n_z, 2, out_weight.shape[0])
+    halves = jnp.where(lax.axis_index("x_lo") == 0, halves, halves[:, :, ::-1])
     columns = lax.all_to_all(
-        attended.reshape(rows_here, n_z, block), "z", 1, 0, tiled=False
+        halves.reshape(rows_here, n_z, block), "z", 1, 0, tiled=False
     ).reshape(n_z * rows_here, block)
     partial = jnp.dot(columns, pair, preferred_element_type=jnp.float32).astype(jnp.bfloat16)
     returned = lax.all_to_all(

time: 362 us -> 358 us (0.989)
  waiting for transfers between devices: 255 us -> 249 us
    all_gather x1 -> x0, waiting for transfers between devices: 29.1 us -> none  [shards(): pair = lax.all_gather(out_weight, 'x_lo', axis=0, tiled=True)]
    ppermute x0 -> x1, waiting for transfers between devices: none -> 21.7 us  [shards(): lax.ppermute(out_weight, 'x_lo', [(0, 1), (1, 0)])]
  transfers between devices with their start and end apart: 8 -> 8, of which waited for: 6 -> 6; matrix products, arithmetic and copies ran while one was open for 9% -> 10% of each run, Pallas kernels for 0% -> 0%
where the time goes in v4:
time: 358 us; the launch traced here: 357 us
  waiting for transfers between devices  249 us (70%)
  matrix products  42.7 us (12%)
  starting transfers between devices  16.1 us (4%)
  blocking collectives  15.4 us (4%)
  between operations  15 us (4%)
  other arithmetic  12.3 us (3%)
  local copies, waits for them, and re-layouts  6.97 us (2%)
    reduce_scatter x1, waiting for transfers between devices, shards(): lax.psum_scatter(jnp.dot(hidden, down_both, preferred_element_type=jnp.fl...  95.2 us
    all_gather x1, waiting for transfers between devices, shards(): gathered = lax.all_gather(normed, ('x_hi', 'y'), axis=0, tiled=True)  80.8 us
    all_to_all x1, waiting for transfers between devices, shards(): lax.all_to_all(partial.reshape(n_z, rows_here, partial.shape[1]), 'z', 0,...  37.4 us
    ppermute x1, waiting for transfers between devices, shards(): lax.ppermute(out_weight, 'x_lo', [(0, 1), (1, 0)])  21.7 us
    all_to_all x1, blocking collectives, shards(): lax.all_to_all(halves.reshape(rows_here, n_z, block), 'z', 1, 0, tiled=Fa...  15.4 us
    dot_general x1, matrix products, shards(): gate = jnp.dot(gathered, gate_both, preferred_element_type=jnp.float32)  10.7 us
    dot_general x1, matrix products, shards(): jnp.dot(hidden, down_both, preferred_element_type=jnp.float32)  10.6 us
    dot_general x1, matrix products, shards(): upper = jnp.dot(gathered, up_both, preferred_element_type=jnp.float32)  8.67 us
  transfers between devices with their start and end apart: 8, of which 6 were waited for; matrix products, arithmetic and copies ran while one was open for 10% of the time, Pallas kernels for 0%

profile of v4, /device:TPU:1, one launch (start us, length us, event | category | flops | bytes accessed | tf_op | source)
XLA Modules:
  0.0 357.1 jit_solution(14406951242886392388)
XLA Ops:
  6.5 0.0 copy-start.2
  6.5 2.0 broadcast_in_dim.79
  8.5 8.4 %all-to-all-start = ((bf16[16,16,2048]{2,1,0:T(8,128)(2,1)}), bf16[16,16,2048]{2,1,0:T(8,128)(2,1)S(1)}, u32[]{:S(2)}, u32[]{:S(2)}) async-start(bf16[16,16,2048]{2,1,0:T(8,128)(2,1)} %broadcast_in_dim.79), calls=%async_computation | async-start | bytes 2097152 | tf_op jit(solution)/shard_map/all_to_all | solution.py:75
  17.0 0.3 collective-permute-start
  18.0 1.5 copy.31
  19.5 0.0 copy-done.2
  19.5 0.3 copy.32
  19.8 1.5 copy.33
  21.3 1.0 pad_maximum_fusion
  22.4 0.1 fusion.51
  22.5 0.2 fusion.50
  22.7 3.0 fusion.22
  25.7 8.3 %all-to-all-done = bf16[16,16,2048]{2,1,0:T(8,128)(2,1)S(1)} async-done(((bf16[16,16,2048]{2,1,0:T(8,128)(2,1)}), bf16[16,16,2048]{2,1,0:T(8,128)(2,1)S(1)}, u32[]{:S(2)}, u32[]{:S(2)}) %all-to-all-start) | async-done | bytes 1048608 | tf_op jit(solution)/shard_map/all_to_all | solution.py:75
  34.1 0.1 fusion.70
  34.1 0.2 copy.37
  34.3 0.2 copy.40
  34.6 0.7 fusion.25
  35.2 0.0 slice-start
  35.2 3.5 fusion.23
  38.8 0.0 slice-start.1
  38.8 0.8 fusion.33
  39.6 0.0 copy-start.1
  39.6 0.8 fusion.36
  40.5 0.0 slice-done
  40.5 0.5 slice-done.1
  41.0 0.4 copy-done.1
  41.4 1.6 fusion.39
  42.9 0.2 reverse_select_fusion
  43.1 0.3 copy.55
  43.4 15.4 %all_to_all.25 = bf16[1,128,4,768]{3,1,0,2:T(8,128)(2,1)S(1)} all-to-all(bf16[1,128,4,768]{3,1,0,2:T(8,128)(2,1)S(1)} %copy.55), channel_id=1, replica_groups=mesh['z'=4,'x_lo'=2,'x_hi'=2,'y'=4,'core'=2] {'z'}, dimensions={2} | all-to-all | bytes 1572864 | tf_op jit(solution)/shard_map/all_to_all | solution.py:94
  58.8 21.7 %collective-permute-done = bf16[384,3072]{1,0:T(8,128)(2,1)} collective-permute-done((bf16[384,3072]{1,0:T(8,128)(2,1)}, bf16[384,3072]{1,0:T(8,128)(2,1)}, u32[]{:S(2)}, u32[]{:S(2)}) %collective-permute-start) | collective-permute-done | bytes 2359328 | tf_op jit(solution)/shard_map/ppermute | solution.py:89
  80.5 6.6 %fusion.19 = bf16[512,3072]{1,0:T(8,128)(2,1)} fusion(bf16[512,768]{1,0:T(8,128)(2,1)S(1)} %bitcast.110, bf16[384,3072]{1,0:T(8,128)(2,1)} %collective-permute-done, bf16[384,3072]{1,0:T(8,128)(2,1)} %param.19), kind=kOutput, calls=%fused_computation.20 | convolution fusion | flops 2426929152 | bytes 8650752 | tf_op jit(solution)/shard_map/dot_general | solution.py:97
  87.1 0.0 copy-start.3
  87.1 5.2 %all-to-all-start.2 = ((bf16[4,128,3072]{2,1,0:T(8,128)(2,1)}), bf16[4,128,3072]{2,1,0:T(8,128)(2,1)}, u32[]{:S(2)}, u32[]{:S(2)}) async-start(bf16[4,128,3072]{2,1,0:T(8,128)(2,1)} %bitcast.27), calls=%async_computation.2 | async-start | bytes 6291456 | tf_op jit(solution)/shard_map/all_to_all | solution.py:98
  92.3 0.0 copy-start
  92.3 0.0 all-gather.2.cloned.1.call-start
  92.3 0.0 copy-done.3
  92.3 37.4 %all-to-all-done.2 = bf16[4,128,3072]{2,1,0:T(8,128)(2,1)} async-done(((bf16[4,128,3072]{2,1,0:T(8,128)(2,1)}), bf16[4,128,3072]{2,1,0:T(8,128)(2,1)}, u32[]{:S(2)}, u32[]{:S(2)}) %all-to-all-start.2) | async-done | bytes 3145760 | tf_op jit(solution)/shard_map/all_to_all | solution.py:98
  129.7 2.6 convert_reduce_fusion
  132.3 0.0 copy-done
  132.3 0.3 multiply_reduce_fusion
  132.6 1.2 multiply_convert_fusion.2
  133.8 0.0 all-gather.2.cloned.1.call-update
  133.8 0.0 reduce-scatter.2.cloned.1.call-start
  133.9 1.7 collective-permute-start.1
  135.5 0.1 collective-permute-start.2
  135.6 0.4 collective-permute-start.3
  136.0 5.1 %collective-permute-done.1 = bf16[3072,512]{1,0:T(8,128)(2,1)} collective-permute-done((bf16[3072,512]{1,0:T(8,128)(2,1)}, bf16[3072,512]{1,0:T(8,128)(2,1)}, u32[]{:S(2)}, u32[]{:S(2)}) %collective-permute-start.1) | collective-permute-done | bytes 3145760 | tf_op jit(solution)/shard_map/ppermute | solution.py:106
  141.1 80.8 %all-gather.2.cloned.1.call-done = bf16[1024,3072]{1,0:T(8,128)(2,1)} async-done(((bf16[128,3072]{1,0:T(8,128)(2,1)}), bf16[1024,3072]{1,0:T(8,128)(2,1)}) %all-gather.2.cloned.1.call-update) | async-done | bytes 6291472 | tf_op jit(solution)/shard_map/all_gather | solution.py:109
  221.9 0.0 copy-start.4
  221.9 0.0 copy-start.5
  221.9 10.7 %fusion = f32[1024,1024]{1,0:T(8,128)S(1)} fusion(bf16[1024,3072]{1,0:T(8,128)(2,1)} %all-gather.2.cloned.1.call-done, bf16[3072,512]{1,0:T(8,128)(2,1)} %collective-permute-done.1, bf16[3072,512]{1,0:T(8,128)(2,1)} %param.21), kind=kOutput, calls=%fused_computation | convolution fusion | flops 6455033856 | bytes 16777216 | tf_op jit(solution)/shard_map/dot_general | solution.py:110
  232.7 0.0 copy-start.6
  232.7 0.0 collective-permute-done.2
  232.7 0.0 copy-done.4
  232.7 0.0 copy-done.5
  232.7 8.7 %fusion.4 = f32[1024,1024]{1,0:T(8,128)S(1)} fusion(bf16[1024,3072]{1,0:T(8,128)(2,1)S(1)} %copy-done.4, bf16[3072,512]{1,0:T(8,128)(2,1)} %collective-permute-done.2, bf16[3072,512]{1,0:T(8,128)(2,1)S(1)} %copy-done.5), kind=kOutput, calls=%fused_computation.4 | convolution fusion | flops 6455033856 | bytes 16777216 | tf_op jit(solution)/shard_map/dot_general | solution.py:111
  241.4 0.0 collective-permute-done.3
  241.4 0.0 copy-done.6
  241.4 10.6 %fusion.12 = bf16[1024,3072]{1,0:T(8,128)(2,1)} fusion(bf16[512,3072]{1,0:T(8,128)(2,1)} %collective-permute-done.3, bf16[512,3072]{1,0:T(8,128)(2,1)S(1)} %copy-done.6, f32[1024,1024]{1,0:T(8,128)S(1)} %fusion.4, f32[1024,1024]{1,0:T(8,128)S(1)} %fusion), kind=kOutput, calls=%fused_computation.13 | convolution fusion | flops 6464471040 | bytes 20971520 | tf_op jit(solution)/shard_map/dot_general | solution.py:114
  252.0 0.0 reduce-scatter.2.cloned.1.call-update
  252.7 95.2 %reduce-scatter.2.cloned.1.call-done = bf16[128,3072]{1,0:T(8,128)(2,1)} async-done(((bf16[1024,3072]{1,0:T(8,128)(2,1)}), bf16[128,3072]{1,0:T(8,128)(2,1)}) %reduce-scatter.2.cloned.1.call-update) | async-done | bytes 786448 | tf_op jit(solution)/shard_map/reduce_scatter | solution.py:113
  347.9 2.3 select_convert_fusion
  (13 shorter events, 0.1 us)
Async XLA Ops:
  6.5 13.0 %copy-start.2 = (bf16[128,2048]{1,0:T(8,128)(2,1)S(1)}, bf16[128,2048]{1,0:T(8,128)(2,1)}, u32[]{:S(2)}) copy-start(bf16[128,2048]{1,0:T(8,128)(2,1)} %param.14) | copy-start | bytes 1572868
  8.5 25.5 %all-to-all-start = ((bf16[16,16,2048]{2,1,0:T(8,128)(2,1)}), bf16[16,16,2048]{2,1,0:T(8,128)(2,1)S(1)}, u32[]{:S(2)}, u32[]{:S(2)}) async-start(bf16[16,16,2048]{2,1,0:T(8,128)(2,1)} %broadcast_in_dim.79), calls=%async_computation | async-start | bytes 2097152 | tf_op jit(solution)/shard_map/all_to_all | solution.py:75
  17.0 63.5 %collective-permute-start = (bf16[384,3072]{1,0:T(8,128)(2,1)}, bf16[384,3072]{1,0:T(8,128)(2,1)}, u32[]{:S(2)}, u32[]{:S(2)}) collective-permute-start(bf16[384,3072]{1,0:T(8,128)(2,1)} %param.19), channel_id=1, source_target_pairs={{0,16},{16,0},{1,17},{17,1},{2,18},{18,2},{3,19},{19,3},{4,20},{20... | collective-permute-start | bytes 7077896 | tf_op jit(solution)/shard_map/ppermute | solution.py:89
  35.2 5.2 %slice-start = ((s8[4718592]{0:T(1024)(128)(4,1)}), s8[524288]{0:T(1024)(128)(4,1)S(1)}, s32[]{:S(2)}) async-start(s8[4718592]{0:T(1024)(128)(4,1)} %bitcast.101), calls=%async_computation.6 | async-start | bytes 1048576
  38.8 2.2 slice-start.1
  39.6 1.8 copy-start.1
  87.1 5.2 %copy-start.3 = (bf16[3072]{0:T(1024)(128)(2,1)S(1)}, bf16[3072]{0:T(1024)(128)(2,1)}, u32[]{:S(2)}) copy-start(bf16[3072]{0:T(1024)(128)(2,1)} %param.20) | copy-start | bytes 18436
  87.1 42.6 %all-to-all-start.2 = ((bf16[4,128,3072]{2,1,0:T(8,128)(2,1)}), bf16[4,128,3072]{2,1,0:T(8,128)(2,1)}, u32[]{:S(2)}, u32[]{:S(2)}) async-start(bf16[4,128,3072]{2,1,0:T(8,128)(2,1)} %bitcast.27), calls=%async_computation.2 | async-start | bytes 6291456 | tf_op jit(solution)/shard_map/all_to_all | solution.py:98
  92.3 40.0 %copy-start = (bf16[128,3072]{1,0:T(8,128)(2,1)S(1)}, bf16[128,3072]{1,0:T(8,128)(2,1)}, u32[]{:S(2)}) copy-start(bf16[128,3072]{1,0:T(8,128)(2,1)} %param.12) | copy-start | bytes 2359300
  92.3 129.6 %all-gather.2.cloned.1.call-start = ((), (), s32[]{:S(2)}) async-start(), calls=%async_computation.4 | async-start | bytes 7077888 | tf_op jit(solution)/shard_map/all_gather | solution.py:109
  133.8 214.1 %reduce-scatter.2.cloned.1.call-start = ((), (), s32[]{:S(2)}) async-start(), calls=%async_computation.5 | async-start | bytes 7077888 | tf_op jit(solution)/shard_map/reduce_scatter | solution.py:113
  133.9 7.3 %collective-permute-start.1 = (bf16[3072,512]{1,0:T(8,128)(2,1)}, bf16[3072,512]{1,0:T(8,128)(2,1)}, u32[]{:S(2)}, u32[]{:S(2)}) collective-permute-start(bf16[3072,512]{1,0:T(8,128)(2,1)} %param.21), channel_id=1, source_target_pairs={{0,1},{1,0},{2,3},{3,2},{4,5},{5,4},{6,7},{7,6},{8,9},{9,8},{10,11... | collective-permute-start | bytes 9437192 | tf_op jit(solution)/shard_map/ppermute | solution.py:106
  135.5 97.2 %collective-permute-start.2 = (bf16[3072,512]{1,0:T(8,128)(2,1)}, bf16[3072,512]{1,0:T(8,128)(2,1)}, u32[]{:S(2)}, u32[]{:S(2)}) collective-permute-start(bf16[3072,512]{1,0:T(8,128)(2,1)} %param.22), channel_id=1, source_target_pairs={{0,1},{1,0},{2,3},{3,2},{4,5},{5,4},{6,7},{7,6},{8,9},{9,8},{10,11... | collective-permute-start | bytes 9437192 | tf_op jit(solution)/shard_map/ppermute | solution.py:107
  135.6 105.8 %collective-permute-start.3 = (bf16[512,3072]{1,0:T(8,128)(2,1)}, bf16[512,3072]{1,0:T(8,128)(2,1)}, u32[]{:S(2)}, u32[]{:S(2)}) collective-permute-start(bf16[512,3072]{1,0:T(8,128)(2,1)} %param.23), channel_id=1, source_target_pairs={{0,1},{1,0},{2,3},{3,2},{4,5},{5,4},{6,7},{7,6},{8,9},{9,8},{10,11... | collective-permute-start | bytes 9437192 | tf_op jit(solution)/shard_map/ppermute | solution.py:108
  221.9 10.8 %copy-start.4 = (bf16[1024,3072]{1,0:T(8,128)(2,1)S(1)}, bf16[1024,3072]{1,0:T(8,128)(2,1)}, u32[]{:S(2)}) copy-start(bf16[1024,3072]{1,0:T(8,128)(2,1)} %all-gather.2.cloned.1.call-done) | copy-start | bytes 18874372
  221.9 10.8 %copy-start.5 = (bf16[3072,512]{1,0:T(8,128)(2,1)S(1)}, bf16[3072,512]{1,0:T(8,128)(2,1)}, u32[]{:S(2)}) copy-start(bf16[3072,512]{1,0:T(8,128)(2,1)} %param.22) | copy-start | bytes 9437188
  232.7 8.7 %copy-start.6 = (bf16[512,3072]{1,0:T(8,128)(2,1)S(1)}, bf16[512,3072]{1,0:T(8,128)(2,1)}, u32[]{:S(2)}) copy-start(bf16[512,3072]{1,0:T(8,128)(2,1)} %param.23) | copy-start | bytes 9437188
Sparse Core Ops, SparseCore 0:
  133.9 87.9 all-gather.1
  252.1 95.7 reduce-scatter.1

commit v5 on v4

--- a/solution.py
+++ b/solution.py
@@ -110,12 +110,11 @@
     gate = jnp.dot(gathered, gate_both, preferred_element_type=jnp.float32)
     upper = jnp.dot(gathered, up_both, preferred_element_type=jnp.float32)
     hidden = (jax.nn.silu(gate) * upper).astype(jnp.bfloat16)
-    feed = lax.psum_scatter(
-        jnp.dot(hidden, down_both, preferred_element_type=jnp.float32).astype(jnp.bfloat16),
-        ("x_hi", "y"),
-        scatter_dimension=0,
-        tiled=True,
-    ).astype(jnp.float32)
+    parts = jnp.dot(hidden, down_both, preferred_element_type=jnp.float32).astype(jnp.bfloat16)
+    parts = lax.all_to_all(
+        parts.reshape(-1, rows_here, parts.shape[1]), ("x_hi", "y"), 0, 0, tiled=False
+    )
+    feed = jnp.sum(parts.astype(jnp.float32), axis=0)
     live = offsets < suffix_len[0]
     return jnp.where(live[:, None], mixed + feed, 0.0).astype(jnp.bfloat16)
 

time: 358 us -> 341 us (0.953)
  waiting for transfers between devices: 249 us -> 224 us
  starting transfers between devices: 16.1 us -> 20.8 us
    reduce_scatter x1 -> x0, waiting for transfers between devices: 95.2 us -> none  [shards(): lax.psum_scatter(jnp.dot(hidden, down_both, preferred_element_type=jnp.fl...]
    all_to_all x0 -> x1, waiting for transfers between devices: none -> 70.5 us  [shards(): lax.all_to_all(parts.reshape(-1, rows_here, parts.shape[1]), ('x_hi', 'y'...]
    all_to_all x0 -> x1, starting transfers between devices: none -> 4.76 us  [shards(): lax.all_to_all(parts.reshape(-1, rows_here, parts.shape[1]), ('x_hi', 'y'...]
    reduce_sum x0 -> x1, other arithmetic: none -> 4.03 us  [shards(): feed = jnp.sum(parts.astype(jnp.float32), axis=0)]
where the time goes in v5:
time: 341 us; the launch traced here: 340 us
  waiting for transfers between devices  224 us (66%)
  matrix products  42.7 us (13%)
  starting transfers between devices  20.8 us (6%)
  blocking collectives  15.4 us (5%)
  other arithmetic  15.3 us (4%)
  between operations  15 us (4%)
  local copies, waits for them, and re-layouts  7.07 us (2%)
    all_gather x1, waiting for transfers between devices, shards(): gathered = lax.all_gather(normed, ('x_hi', 'y'), axis=0, tiled=True)  80.8 us
    all_to_all x1, waiting for transfers between devices, shards(): lax.all_to_all(parts.reshape(-1, rows_here, parts.shape[1]), ('x_hi', 'y'...  70.5 us
    all_to_all x1, waiting for transfers between devices, shards(): lax.all_to_all(partial.reshape(n_z, rows_here, partial.shape[1]), 'z', 0,...  37.4 us
    ppermute x1, waiting for transfers between devices, shards(): lax.ppermute(out_weight, 'x_lo', [(0, 1), (1, 0)])  21.7 us
    all_to_all x1, blocking collectives, shards(): lax.all_to_all(halves.reshape(rows_here, n_z, block), 'z', 1, 0, tiled=Fa...  15.4 us
    dot_general x1, matrix products, shards(): gate = jnp.dot(gathered, gate_both, preferred_element_type=jnp.float32)  10.7 us
    dot_general x1, matrix products, shards(): jnp.dot(hidden, down_both, preferred_element_type=jnp.float32)  10.6 us
    dot_general x1, matrix products, shards(): upper = jnp.dot(gathered, up_both, preferred_element_type=jnp.float32)  8.67 us
  transfers between devices with their start and end apart: 8, of which 6 were waited for; matrix products, arithmetic and copies ran while one was open for 10% of the time, Pallas kernels for 0%

profile of v5, /device:TPU:1, one launch (start us, length us, event | category | flops | bytes accessed | tf_op | source)
XLA Modules:
  0.0 340.0 jit_solution(17096597828297078180)
XLA Ops:
  6.5 0.0 copy-start.1
  6.5 2.0 broadcast_in_dim.79
  8.6 8.4 %all-to-all-start = ((bf16[16,16,2048]{2,1,0:T(8,128)(2,1)}), bf16[16,16,2048]{2,1,0:T(8,128)(2,1)S(1)}, u32[]{:S(2)}, u32[]{:S(2)}) async-start(bf16[16,16,2048]{2,1,0:T(8,128)(2,1)} %broadcast_in_dim.79), calls=%async_computation | async-start | bytes 2097152 | tf_op jit(solution)/shard_map/all_to_all | solution.py:75
  17.0 0.3 collective-permute-start
  18.0 0.0 copy-done.1
  18.0 0.5 copy.31
  18.6 1.3 copy.32
  19.9 1.5 copy.33
  21.4 1.0 pad_maximum_fusion
  22.5 0.1 fusion.51
  22.6 0.2 fusion.50
  22.8 3.0 fusion.22
  25.8 8.2 %all-to-all-done = bf16[16,16,2048]{2,1,0:T(8,128)(2,1)S(1)} async-done(((bf16[16,16,2048]{2,1,0:T(8,128)(2,1)}), bf16[16,16,2048]{2,1,0:T(8,128)(2,1)S(1)}, u32[]{:S(2)}, u32[]{:S(2)}) %all-to-all-start) | async-done | bytes 1048608 | tf_op jit(solution)/shard_map/all_to_all | solution.py:75
  34.1 0.1 fusion.70
  34.2 0.2 copy.37
  34.4 0.2 copy.40
  34.6 0.7 fusion.25
  35.3 0.0 slice-start
  35.3 3.5 %fusion.23 = f32[8,3,128]{2,1,0:T(4,128)S(1)} fusion(f32[8,384,128,3]{2,1,3,0:T(8,128)} %get-tuple-element.15, f32[8,3,128]{2,1,0:T(4,128)S(1)} %get-tuple-element.12, pred[128,384]{0,1:T(8,128)(4,1)S(1)} %fusion.50), kind=kLoop, calls=%fused_computation.24 | loop fusion | flops 5895168 | bytes 4792320 | tf_op jit(solution)/shard_map/reduce_sum | solution.py:33
  38.8 0.0 slice-start.1
  38.8 0.8 fusion.33
  39.6 0.0 copy-start.2
  39.6 0.8 fusion.36
  40.5 0.0 slice-done
  40.5 0.5 slice-done.1
  41.0 0.4 copy-done.2
  41.4 1.6 fusion.39
  43.0 0.2 reverse_select_fusion
  43.1 0.3 copy.55
  43.4 15.4 %all_to_all.30 = bf16[1,128,4,768]{3,1,0,2:T(8,128)(2,1)S(1)} all-to-all(bf16[1,128,4,768]{3,1,0,2:T(8,128)(2,1)S(1)} %copy.55), channel_id=1, replica_groups=mesh['z'=4,'x_lo'=2,'x_hi'=2,'y'=4,'core'=2] {'z'}, dimensions={2} | all-to-all | bytes 1572864 | tf_op jit(solution)/shard_map/all_to_all | solution.py:94
  58.8 21.7 %collective-permute-done = bf16[384,3072]{1,0:T(8,128)(2,1)} collective-permute-done((bf16[384,3072]{1,0:T(8,128)(2,1)}, bf16[384,3072]{1,0:T(8,128)(2,1)}, u32[]{:S(2)}, u32[]{:S(2)}) %collective-permute-start) | collective-permute-done | bytes 2359328 | tf_op jit(solution)/shard_map/ppermute | solution.py:89
  80.5 6.6 %fusion.19 = bf16[512,3072]{1,0:T(8,128)(2,1)} fusion(bf16[512,768]{1,0:T(8,128)(2,1)S(1)} %bitcast.113, bf16[384,3072]{1,0:T(8,128)(2,1)} %collective-permute-done, bf16[384,3072]{1,0:T(8,128)(2,1)} %param.19), kind=kOutput, calls=%fused_computation.21 | convolution fusion | flops 2426929152 | bytes 8650752 | tf_op jit(solution)/shard_map/dot_general | solution.py:97
  87.1 0.0 copy-start.3
  87.1 5.2 %all-to-all-start.2 = ((bf16[4,128,3072]{2,1,0:T(8,128)(2,1)}), bf16[4,128,3072]{2,1,0:T(8,128)(2,1)}, u32[]{:S(2)}, u32[]{:S(2)}) async-start(bf16[4,128,3072]{2,1,0:T(8,128)(2,1)} %bitcast.108), calls=%async_computation.2 | async-start | bytes 6291456 | tf_op jit(solution)/shard_map/all_to_all | solution.py:98
  92.3 0.0 copy-start
  92.3 0.0 all-gather.2.cloned.1.call-start
  92.3 0.0 copy-done.3
  92.3 37.4 %all-to-all-done.2 = bf16[4,128,3072]{2,1,0:T(8,128)(2,1)} async-done(((bf16[4,128,3072]{2,1,0:T(8,128)(2,1)}), bf16[4,128,3072]{2,1,0:T(8,128)(2,1)}, u32[]{:S(2)}, u32[]{:S(2)}) %all-to-all-start.2) | async-done | bytes 3145760 | tf_op jit(solution)/shard_map/all_to_all | solution.py:98
  129.7 2.6 convert_reduce_fusion.1
  132.3 0.0 copy-done
  132.3 0.3 multiply_reduce_fusion
  132.6 1.2 multiply_convert_fusion.2
  133.8 0.0 all-gather.2.cloned.1.call-update
  133.8 1.6 collective-permute-start.1
  135.5 0.1 collective-permute-start.2
  135.6 0.4 collective-permute-start.3
  136.0 5.1 %collective-permute-done.1 = bf16[3072,512]{1,0:T(8,128)(2,1)} collective-permute-done((bf16[3072,512]{1,0:T(8,128)(2,1)}, bf16[3072,512]{1,0:T(8,128)(2,1)}, u32[]{:S(2)}, u32[]{:S(2)}) %collective-permute-start.1) | collective-permute-done | bytes 3145760 | tf_op jit(solution)/shard_map/ppermute | solution.py:106
  141.1 80.8 %all-gather.2.cloned.1.call-done = bf16[1024,3072]{1,0:T(8,128)(2,1)} async-done(((bf16[128,3072]{1,0:T(8,128)(2,1)}), bf16[1024,3072]{1,0:T(8,128)(2,1)}) %all-gather.2.cloned.1.call-update) | async-done | bytes 6291472 | tf_op jit(solution)/shard_map/all_gather | solution.py:109
  221.9 0.0 copy-start.4
  221.9 0.0 copy-start.5
  221.9 10.7 %fusion = f32[1024,1024]{1,0:T(8,128)S(1)} fusion(bf16[1024,3072]{1,0:T(8,128)(2,1)} %all-gather.2.cloned.1.call-done, bf16[3072,512]{1,0:T(8,128)(2,1)} %collective-permute-done.1, bf16[3072,512]{1,0:T(8,128)(2,1)} %param.21), kind=kOutput, calls=%fused_computation.1 | convolution fusion | flops 6455033856 | bytes 16777216 | tf_op jit(solution)/shard_map/dot_general | solution.py:110
  232.7 0.0 copy-start.6
  232.7 0.0 collective-permute-done.2
  232.7 0.0 copy-done.4
  232.7 0.0 copy-done.5
  232.7 8.7 %fusion.4 = f32[1024,1024]{1,0:T(8,128)S(1)} fusion(bf16[1024,3072]{1,0:T(8,128)(2,1)S(1)} %copy-done.4, bf16[3072,512]{1,0:T(8,128)(2,1)} %collective-permute-done.2, bf16[3072,512]{1,0:T(8,128)(2,1)S(1)} %copy-done.5), kind=kOutput, calls=%fused_computation.5 | convolution fusion | flops 6455033856 | bytes 16777216 | tf_op jit(solution)/shard_map/dot_general | solution.py:111
  241.4 0.0 collective-permute-done.3
  241.4 0.0 copy-done.6
  241.4 10.6 %fusion.12 = bf16[1024,3072]{1,0:T(8,128)(2,1)} fusion(bf16[512,3072]{1,0:T(8,128)(2,1)} %collective-permute-done.3, bf16[512,3072]{1,0:T(8,128)(2,1)S(1)} %copy-done.6, f32[1024,1024]{1,0:T(8,128)S(1)} %fusion.4, f32[1024,1024]{1,0:T(8,128)S(1)} %fusion), kind=kOutput, calls=%fused_computation.14 | convolution fusion | flops 6464471040 | bytes 20971520 | tf_op jit(solution)/shard_map/dot_general | solution.py:113
  252.0 4.8 %all-to-all-start.3 = ((bf16[8,128,3072]{2,1,0:T(8,128)(2,1)}), bf16[8,128,3072]{2,1,0:T(8,128)(2,1)}, u32[]{:S(2)}, u32[]{:S(2)}) async-start(bf16[8,128,3072]{2,1,0:T(8,128)(2,1)} %bitcast.106), calls=%async_computation.3 | async-start | bytes 12582912 | tf_op jit(solution)/shard_map/all_to_all | solution.py:114
  257.4 70.5 %all-to-all-done.3 = bf16[8,128,3072]{2,1,0:T(8,128)(2,1)} async-done(((bf16[8,128,3072]{2,1,0:T(8,128)(2,1)}), bf16[8,128,3072]{2,1,0:T(8,128)(2,1)}, u32[]{:S(2)}, u32[]{:S(2)}) %all-to-all-start.3) | async-done | bytes 6291488 | tf_op jit(solution)/shard_map/all_to_all | solution.py:114
  327.9 4.0 %convert_reduce_fusion = f32[128,3072]{1,0:T(8,128)S(1)} fusion(bf16[8,128,3072]{2,1,0:T(8,128)(2,1)} %all-to-all-done.3), kind=kLoop, calls=%fused_computation | loop fusion | flops 5898240 | bytes 7864320 | tf_op jit(solution)/shard_map/reduce_sum | solution.py:117
  331.9 1.3 select_convert_fusion
  (13 shorter events, 0.1 us)
Async XLA Ops:
  6.5 11.5 %copy-start.1 = (bf16[256,2048]{1,0:T(8,128)(2,1)S(1)}, bf16[256,2048]{1,0:T(8,128)(2,1)}, u32[]{:S(2)}) copy-start(bf16[256,2048]{1,0:T(8,128)(2,1)} %param.15) | copy-start | bytes 3145732
  8.6 25.5 %all-to-all-start = ((bf16[16,16,2048]{2,1,0:T(8,128)(2,1)}), bf16[16,16,2048]{2,1,0:T(8,128)(2,1)S(1)}, u32[]{:S(2)}, u32[]{:S(2)}) async-start(bf16[16,16,2048]{2,1,0:T(8,128)(2,1)} %broadcast_in_dim.79), calls=%async_computation | async-start | bytes 2097152 | tf_op jit(solution)/shard_map/all_to_all | solution.py:75
  17.0 63.5 %collective-permute-start = (bf16[384,3072]{1,0:T(8,128)(2,1)}, bf16[384,3072]{1,0:T(8,128)(2,1)}, u32[]{:S(2)}, u32[]{:S(2)}) collective-permute-start(bf16[384,3072]{1,0:T(8,128)(2,1)} %param.19), channel_id=1, source_target_pairs={{0,16},{16,0},{1,17},{17,1},{2,18},{18,2},{3,19},{19,3},{4,20},{20... | collective-permute-start | bytes 7077896 | tf_op jit(solution)/shard_map/ppermute | solution.py:89
  35.3 5.2 %slice-start = ((s8[4718592]{0:T(1024)(128)(4,1)}), s8[524288]{0:T(1024)(128)(4,1)S(1)}, s32[]{:S(2)}) async-start(s8[4718592]{0:T(1024)(128)(4,1)} %bitcast.102), calls=%async_computation.5 | async-start | bytes 1048576
  38.8 2.2 slice-start.1
  39.6 1.8 copy-start.2
  87.1 5.2 %copy-start.3 = (bf16[3072]{0:T(1024)(128)(2,1)S(1)}, bf16[3072]{0:T(1024)(128)(2,1)}, u32[]{:S(2)}) copy-start(bf16[3072]{0:T(1024)(128)(2,1)} %param.20) | copy-start | bytes 18436
  87.1 42.6 %all-to-all-start.2 = ((bf16[4,128,3072]{2,1,0:T(8,128)(2,1)}), bf16[4,128,3072]{2,1,0:T(8,128)(2,1)}, u32[]{:S(2)}, u32[]{:S(2)}) async-start(bf16[4,128,3072]{2,1,0:T(8,128)(2,1)} %bitcast.108), calls=%async_computation.2 | async-start | bytes 6291456 | tf_op jit(solution)/shard_map/all_to_all | solution.py:98
  92.3 40.0 %copy-start = (bf16[128,3072]{1,0:T(8,128)(2,1)S(1)}, bf16[128,3072]{1,0:T(8,128)(2,1)}, u32[]{:S(2)}) copy-start(bf16[128,3072]{1,0:T(8,128)(2,1)} %param.12) | copy-start | bytes 2359300
  92.3 129.6 %all-gather.2.cloned.1.call-start = ((), (), s32[]{:S(2)}) async-start(), calls=%async_computation.4 | async-start | bytes 7077888 | tf_op jit(solution)/shard_map/all_gather | solution.py:109
  133.8 7.3 %collective-permute-start.1 = (bf16[3072,512]{1,0:T(8,128)(2,1)}, bf16[3072,512]{1,0:T(8,128)(2,1)}, u32[]{:S(2)}, u32[]{:S(2)}) collective-permute-start(bf16[3072,512]{1,0:T(8,128)(2,1)} %param.21), channel_id=1, source_target_pairs={{0,1},{1,0},{2,3},{3,2},{4,5},{5,4},{6,7},{7,6},{8,9},{9,8},{10,11... | collective-permute-start | bytes 9437192 | tf_op jit(solution)/shard_map/ppermute | solution.py:106
  135.5 97.2 %collective-permute-start.2 = (bf16[3072,512]{1,0:T(8,128)(2,1)}, bf16[3072,512]{1,0:T(8,128)(2,1)}, u32[]{:S(2)}, u32[]{:S(2)}) collective-permute-start(bf16[3072,512]{1,0:T(8,128)(2,1)} %param.22), channel_id=1, source_target_pairs={{0,1},{1,0},{2,3},{3,2},{4,5},{5,4},{6,7},{7,6},{8,9},{9,8},{10,11... | collective-permute-start | bytes 9437192 | tf_op jit(solution)/shard_map/ppermute | solution.py:107
  135.6 105.8 %collective-permute-start.3 = (bf16[512,3072]{1,0:T(8,128)(2,1)}, bf16[512,3072]{1,0:T(8,128)(2,1)}, u32[]{:S(2)}, u32[]{:S(2)}) collective-permute-start(bf16[512,3072]{1,0:T(8,128)(2,1)} %param.23), channel_id=1, source_target_pairs={{0,1},{1,0},{2,3},{3,2},{4,5},{5,4},{6,7},{7,6},{8,9},{9,8},{10,11... | collective-permute-start | bytes 9437192 | tf_op jit(solution)/shard_map/ppermute | solution.py:108
  221.9 10.8 %copy-start.4 = (bf16[1024,3072]{1,0:T(8,128)(2,1)S(1)}, bf16[1024,3072]{1,0:T(8,128)(2,1)}, u32[]{:S(2)}) copy-start(bf16[1024,3072]{1,0:T(8,128)(2,1)} %all-gather.2.cloned.1.call-done) | copy-start | bytes 18874372
  221.9 10.8 %copy-start.5 = (bf16[3072,512]{1,0:T(8,128)(2,1)S(1)}, bf16[3072,512]{1,0:T(8,128)(2,1)}, u32[]{:S(2)}) copy-start(bf16[3072,512]{1,0:T(8,128)(2,1)} %param.22) | copy-start | bytes 9437188
  232.7 8.7 %copy-start.6 = (bf16[512,3072]{1,0:T(8,128)(2,1)S(1)}, bf16[512,3072]{1,0:T(8,128)(2,1)}, u32[]{:S(2)}) copy-start(bf16[512,3072]{1,0:T(8,128)(2,1)} %param.23) | copy-start | bytes 9437188
  252.0 75.9 %all-to-all-start.3 = ((bf16[8,128,3072]{2,1,0:T(8,128)(2,1)}), bf16[8,128,3072]{2,1,0:T(8,128)(2,1)}, u32[]{:S(2)}, u32[]{:S(2)}) async-start(bf16[8,128,3072]{2,1,0:T(8,128)(2,1)} %bitcast.106), calls=%async_computation.3 | async-start | bytes 12582912 | tf_op jit(solution)/shard_map/all_to_all | solution.py:114
Sparse Core Ops, SparseCore 0:
  134.0 87.9 all-gather.1

commit v6 on v5

--- a/solution.py
+++ b/solution.py
@@ -106,15 +106,29 @@
     gate_both = jnp.concatenate([gate_weight, lax.ppermute(gate_weight, "core", swap)], axis=1)
     up_both = jnp.concatenate([up_weight, lax.ppermute(up_weight, "core", swap)], axis=1)
     down_both = jnp.concatenate([down_weight, lax.ppermute(down_weight, "core", swap)], axis=0)
-    gathered = lax.all_gather(normed, ("x_hi", "y"), axis=0, tiled=True)
+    feed_axes = ("x_hi", "y")
+    n_feed = lax.axis_size(feed_axes)
+    half = rows_here // 2
+    gathered = jnp.concatenate(
+        [
+            lax.all_gather(normed[:half], feed_axes, axis=0, tiled=True),
+            lax.all_to_all(
+                jnp.broadcast_to(normed[half:][None], (n_feed, half, normed.shape[1])),
+                feed_axes,
+                0,
+                0,
+                tiled=False,
+            ).reshape(n_feed * half, normed.shape[1]),
+        ]
+    )
     gate = jnp.dot(gathered, gate_both, preferred_element_type=jnp.float32)
     upper = jnp.dot(gathered, up_both, preferred_element_type=jnp.float32)
     hidden = (jax.nn.silu(gate) * upper).astype(jnp.bfloat16)
     parts = jnp.dot(hidden, down_both, preferred_element_type=jnp.float32).astype(jnp.bfloat16)
     parts = lax.all_to_all(
-        parts.reshape(-1, rows_here, parts.shape[1]), ("x_hi", "y"), 0, 0, tiled=False
+        parts.reshape(2, n_feed, half, parts.shape[1]), feed_axes, 1, 1, tiled=False
     )
-    feed = jnp.sum(parts.astype(jnp.float32), axis=0)
+    feed = jnp.sum(parts.astype(jnp.float32), axis=1).reshape(rows_here, parts.shape[-1])
     live = offsets < suffix_len[0]
     return jnp.where(live[:, None], mixed + feed, 0.0).astype(jnp.bfloat16)
 

time: 341 us -> 350 us (1.026)
  waiting for transfers between devices: 224 us -> 217 us
  starting transfers between devices: 20.8 us -> 27.5 us
  local copies, waits for them, and re-layouts: 7.07 us -> 12.9 us
  matrix products: 42.7 us -> 47.5 us
    all_gather x1, waiting for transfers between devices: 80.8 us -> 35.2 us  [shards(): lax.all_gather(normed[:half], feed_axes, axis=0, tiled=True)]
    all_to_all x1 -> x2, waiting for transfers between devices: 70.5 us -> 114 us  [the longest x1 70.5 us: shards(): lax.all_to_all(parts.reshape(2, n_feed, half, parts.shape[1]), feed_axes,...]
    all_to_all x1 -> x2, starting transfers between devices: 4.76 us -> 11.5 us  [the longest x1 6.73 us: shards(): lax.all_to_all(jnp.broadcast_to(normed[half:][None], (n_feed, half, norme...]
    ppermute x1, waiting for transfers between devices: 5.12 us -> 0.01 us  [shards(): lax.ppermute(gate_weight, 'core', swap)]
    dot_general x1, matrix products: 8.67 us -> 12.5 us  [shards(): upper = jnp.dot(gathered, up_both, preferred_element_type=jnp.float32)]
  transfers between devices with their start and end apart: 8 -> 9, of which waited for: 6 -> 6; matrix products, arithmetic and copies ran while one was open for 10% -> 13% of each run, Pallas kernels for 0% -> 0%
where the time goes in v6:
time: 350 us; the launch traced here: 349 us
  waiting for transfers between devices  217 us (62%)
  matrix products  47.5 us (14%)
  starting transfers between devices  27.5 us (8%)
  blocking collectives  15.4 us (4%)
  between operations  15 us (4%)
  other arithmetic  14.4 us (4%)
  local copies, waits for them, and re-layouts  12.9 us (4%)
    all_to_all x1, waiting for transfers between devices, shards(): lax.all_to_all(parts.reshape(2, n_feed, half, parts.shape[1]), feed_axes,...  70.5 us
    all_to_all x1, waiting for transfers between devices, shards(): lax.all_to_all(jnp.broadcast_to(normed[half:][None], (n_feed, half, norme...  43.5 us
    all_to_all x1, waiting for transfers between devices, shards(): lax.all_to_all(partial.reshape(n_z, rows_here, partial.shape[1]), 'z', 0,...  37.4 us
    all_gather x1, waiting for transfers between devices, shards(): lax.all_gather(normed[:half], feed_axes, axis=0, tiled=True)  35.2 us
    ppermute x1, waiting for transfers between devices, shards(): lax.ppermute(out_weight, 'x_lo', [(0, 1), (1, 0)])  21.7 us
    all_to_all x1, blocking collectives, shards(): lax.all_to_all(halves.reshape(rows_here, n_z, block), 'z', 1, 0, tiled=Fa...  15.4 us
    dot_general x1, matrix products, shards(): gate = jnp.dot(gathered, gate_both, preferred_element_type=jnp.float32)  13.4 us
    dot_general x1, matrix products, shards(): upper = jnp.dot(gathered, up_both, preferred_element_type=jnp.float32)  12.5 us
  transfers between devices with their start and end apart: 9, of which 6 were waited for; matrix products, arithmetic and copies ran while one was open for 13% of the time, Pallas kernels for 0%

profile of v6, /device:TPU:1, one launch (start us, length us, event | category | flops | bytes accessed | tf_op | source)
XLA Modules:
  0.0 349.3 jit_solution(384116554729353003)
XLA Ops:
  6.5 2.0 broadcast_in_dim.85
  8.5 8.4 %all-to-all-start = ((bf16[16,16,2048]{2,1,0:T(8,128)(2,1)}), bf16[16,16,2048]{2,1,0:T(8,128)(2,1)S(1)}, u32[]{:S(2)}, u32[]{:S(2)}) async-start(bf16[16,16,2048]{2,1,0:T(8,128)(2,1)} %broadcast_in_dim.85), calls=%async_computation | async-start | bytes 2097152 | tf_op jit(solution)/shard_map/all_to_all | solution.py:75
  17.0 0.3 collective-permute-start
  18.0 1.5 copy.31
  19.5 0.0 copy-done.2
  19.5 0.3 copy.32
  19.8 1.5 copy.33
  21.3 1.0 pad_maximum_fusion.5
  22.4 0.1 fusion.54
  22.5 0.2 fusion.53
  22.7 3.0 fusion.22
  25.7 8.3 %all-to-all-done = bf16[16,16,2048]{2,1,0:T(8,128)(2,1)S(1)} async-done(((bf16[16,16,2048]{2,1,0:T(8,128)(2,1)}), bf16[16,16,2048]{2,1,0:T(8,128)(2,1)S(1)}, u32[]{:S(2)}, u32[]{:S(2)}) %all-to-all-start) | async-done | bytes 1048608 | tf_op jit(solution)/shard_map/all_to_all | solution.py:75
  34.0 0.1 fusion.72
  34.1 0.2 copy.37
  34.3 0.2 copy.40
  34.5 0.7 fusion.25
  35.2 0.0 slice-start
  35.2 3.5 %fusion.23 = f32[8,3,128]{2,1,0:T(4,128)S(1)} fusion(f32[8,384,128,3]{2,1,3,0:T(8,128)} %get-tuple-element.17, f32[8,3,128]{2,1,0:T(4,128)S(1)} %get-tuple-element.14, pred[128,384]{0,1:T(8,128)(4,1)S(1)} %fusion.53), kind=kLoop, calls=%fused_computation.25 | loop fusion | flops 5895168 | bytes 4792320 | tf_op jit(solution)/shard_map/reduce_sum | solution.py:33
  38.8 0.0 slice-start.1
  38.8 0.8 fusion.35
  39.6 0.0 copy-start.1
  39.6 0.8 fusion.37
  40.4 0.0 slice-done
  40.5 0.5 slice-done.1
  40.9 0.4 copy-done.1
  41.4 1.6 fusion.42
  42.9 0.2 reverse_select_fusion
  43.1 0.3 copy.56
  43.4 15.4 %all_to_all.35 = bf16[1,128,4,768]{3,1,0,2:T(8,128)(2,1)S(1)} all-to-all(bf16[1,128,4,768]{3,1,0,2:T(8,128)(2,1)S(1)} %copy.56), channel_id=1, replica_groups=mesh['z'=4,'x_lo'=2,'x_hi'=2,'y'=4,'core'=2] {'z'}, dimensions={2} | all-to-all | bytes 1572864 | tf_op jit(solution)/shard_map/all_to_all | solution.py:94
  58.8 21.7 %collective-permute-done = bf16[384,3072]{1,0:T(8,128)(2,1)} collective-permute-done((bf16[384,3072]{1,0:T(8,128)(2,1)}, bf16[384,3072]{1,0:T(8,128)(2,1)}, u32[]{:S(2)}, u32[]{:S(2)}) %collective-permute-start) | collective-permute-done | bytes 2359328 | tf_op jit(solution)/shard_map/ppermute | solution.py:89
  80.5 6.6 %fusion.19 = bf16[512,3072]{1,0:T(8,128)(2,1)} fusion(bf16[512,768]{1,0:T(8,128)(2,1)S(1)} %bitcast.118, bf16[384,3072]{1,0:T(8,128)(2,1)} %collective-permute-done, bf16[384,3072]{1,0:T(8,128)(2,1)} %param.19), kind=kOutput, calls=%fused_computation.22 | convolution fusion | flops 2426929152 | bytes 8650752 | tf_op jit(solution)/shard_map/dot_general | solution.py:97
  87.1 0.0 copy-start.3
  87.1 5.2 %all-to-all-start.2 = ((bf16[4,128,3072]{2,1,0:T(8,128)(2,1)}), bf16[4,128,3072]{2,1,0:T(8,128)(2,1)}, u32[]{:S(2)}, u32[]{:S(2)}) async-start(bf16[4,128,3072]{2,1,0:T(8,128)(2,1)} %bitcast.27), calls=%async_computation.2 | async-start | bytes 6291456 | tf_op jit(solution)/shard_map/all_to_all | solution.py:98
  92.3 0.0 copy-start
  92.3 0.0 all-gather.2.cloned.1.call-start
  92.3 0.0 copy-done.3
  92.3 37.4 %all-to-all-done.2 = bf16[4,128,3072]{2,1,0:T(8,128)(2,1)} async-done(((bf16[4,128,3072]{2,1,0:T(8,128)(2,1)}), bf16[4,128,3072]{2,1,0:T(8,128)(2,1)}, u32[]{:S(2)}, u32[]{:S(2)}) %all-to-all-start.2) | async-done | bytes 3145760 | tf_op jit(solution)/shard_map/all_to_all | solution.py:98
  129.7 2.6 convert_reduce_fusion.1
  132.3 0.0 copy-done
  132.3 0.3 multiply_reduce_fusion
  132.6 0.3 multiply_convert_fusion.1
  132.9 0.8 fusion.73
  133.7 0.0 all-gather.2.cloned.1.call-update
  133.7 1.6 collective-permute-start.1
  135.4 2.0 broadcast_in_dim.88
  137.4 6.7 %all-to-all-start.3 = ((bf16[8,64,3072]{2,1,0:T(8,128)(2,1)}), bf16[8,64,3072]{2,1,0:T(8,128)(2,1)}, u32[]{:S(2)}, u32[]{:S(2)}) async-start(bf16[8,64,3072]{2,1,0:T(8,128)(2,1)} %broadcast_in_dim.88), calls=%async_computation.3 | async-start | bytes 6291456 | tf_op jit(solution)/shard_map/all_to_all | solution.py:115
  144.1 0.3 collective-permute-start.2
  144.4 0.2 collective-permute-start.3
  144.6 0.0 collective-permute-done.1
  144.6 43.5 %all-to-all-done.3 = bf16[8,64,3072]{2,1,0:T(8,128)(2,1)} async-done(((bf16[8,64,3072]{2,1,0:T(8,128)(2,1)}), bf16[8,64,3072]{2,1,0:T(8,128)(2,1)}, u32[]{:S(2)}, u32[]{:S(2)}) %all-to-all-start.3) | async-done | bytes 3145760 | tf_op jit(solution)/shard_map/all_to_all | solution.py:115
  188.2 35.2 %all-gather.2.cloned.1.call-done = bf16[512,3072]{1,0:T(8,128)(2,1)} async-done(((bf16[64,3072]{1,0:T(8,128)(2,1)}), bf16[512,3072]{1,0:T(8,128)(2,1)}) %all-gather.2.cloned.1.call-update) | async-done | bytes 3145744 | tf_op jit(solution)/shard_map/all_gather | solution.py:114
  223.4 13.4 %fusion = f32[1024,1024]{1,0:T(8,128)} fusion(bf16[3072,512]{1,0:T(8,128)(2,1)} %collective-permute-done.1, bf16[3072,512]{1,0:T(8,128)(2,1)} %param.21, bf16[512,3072]{1,0:T(8,128)(2,1)} %bitcast.28, bf16[512,3072]{1,0:T(8,128)(2,1)} %all-gather.2.cloned.1.call-done), kind=kOutput, calls=%fused_computation.2 | convolution fusion | flops 6467616768 | bytes 16777216 | tf_op jit(solution)/shard_map/dot_general | solution.py:124
  236.7 0.0 collective-permute-done.2
  236.7 0.0 copy-done.4
  236.7 0.0 copy-done.6
  236.8 12.5 %multiply_convert_fusion = bf16[1024,1024]{1,0:T(8,128)(2,1)} fusion(f32[1024,1024]{1,0:T(8,128)} %fusion, bf16[3072,512]{1,0:T(8,128)(2,1)} %collective-permute-done.2, bf16[3072,512]{1,0:T(8,128)(2,1)S(1)} %copy-done.4, bf16[512,3072]{1,0:T(8,128)(2,1)} %bitcast.28, bf16[512,3072]{1,0:T(8,128)(2,1)S(1)} %copy-done.6), kind=kOutput, calls=%fused_computation.23 | convolution fusion | flops 6473908224 | bytes 18874368 | tf_op jit(solution)/shard_map/dot_general | solution.py:125
  249.2 0.0 collective-permute-done.3
  249.2 0.0 copy-done.5
  249.2 9.0 %fusion.12 = bf16[1024,3072]{1,0:T(8,128)(2,1)S(1)} fusion(bf16[1024,1024]{1,0:T(8,128)(2,1)} %multiply_convert_fusion, bf16[512,3072]{1,0:T(8,128)(2,1)} %collective-permute-done.3, bf16[512,3072]{1,0:T(8,128)(2,1)S(1)} %copy-done.5), kind=kOutput, calls=%fused_computation.15 | convolution fusion | flops 6458179584 | bytes 14680064 | tf_op jit(solution)/shard_map/dot_general | solution.py:127
  258.2 3.1 copy.43
  261.3 4.7 %all-to-all-start.4 = ((bf16[2,8,64,3072]{3,2,0,1:T(8,128)(2,1)}), bf16[2,8,64,3072]{3,2,0,1:T(8,128)(2,1)}, u32[]{:S(2)}, u32[]{:S(2)}) async-start(bf16[2,8,64,3072]{3,2,0,1:T(8,128)(2,1)} %copy.43), calls=%async_computation.4 | async-start | bytes 12582912 | tf_op jit(solution)/shard_map/all_to_all | solution.py:128
  266.7 70.5 %all-to-all-done.4 = bf16[2,8,64,3072]{3,2,0,1:T(8,128)(2,1)} async-done(((bf16[2,8,64,3072]{3,2,0,1:T(8,128)(2,1)}), bf16[2,8,64,3072]{3,2,0,1:T(8,128)(2,1)}, u32[]{:S(2)}, u32[]{:S(2)}) %all-to-all-start.4) | async-done | bytes 6291488 | tf_op jit(solution)/shard_map/all_to_all | solution.py:128
  337.2 4.0 %convert_reduce_fusion = f32[2,64,3072]{2,1,0:T(8,128)S(1)} fusion(bf16[2,8,64,3072]{3,2,0,1:T(8,128)(2,1)} %all-to-all-done.4), kind=kLoop, calls=%fused_computation | loop fusion | flops 5898240 | bytes 7864320 | tf_op jit(solution)/shard_map/reduce_sum | solution.py:131
  341.2 1.3 fusion.40
  (17 shorter events, 0.1 us)
Async XLA Ops:
  6.5 13.0 %copy-start.2 = (bf16[128,2048]{1,0:T(8,128)(2,1)S(1)}, bf16[128,2048]{1,0:T(8,128)(2,1)}, u32[]{:S(2)}) copy-start(bf16[128,2048]{1,0:T(8,128)(2,1)} %param.14) | copy-start | bytes 1572868
  8.5 25.5 %all-to-all-start = ((bf16[16,16,2048]{2,1,0:T(8,128)(2,1)}), bf16[16,16,2048]{2,1,0:T(8,128)(2,1)S(1)}, u32[]{:S(2)}, u32[]{:S(2)}) async-start(bf16[16,16,2048]{2,1,0:T(8,128)(2,1)} %broadcast_in_dim.85), calls=%async_computation | async-start | bytes 2097152 | tf_op jit(solution)/shard_map/all_to_all | solution.py:75
  17.0 63.5 %collective-permute-start = (bf16[384,3072]{1,0:T(8,128)(2,1)}, bf16[384,3072]{1,0:T(8,128)(2,1)}, u32[]{:S(2)}, u32[]{:S(2)}) collective-permute-start(bf16[384,3072]{1,0:T(8,128)(2,1)} %param.19), channel_id=1, source_target_pairs={{0,16},{16,0},{1,17},{17,1},{2,18},{18,2},{3,19},{19,3},{4,20},{20... | collective-permute-start | bytes 7077896 | tf_op jit(solution)/shard_map/ppermute | solution.py:89
  35.2 5.2 %slice-start = ((s8[4718592]{0:T(1024)(128)(4,1)}), s8[524288]{0:T(1024)(128)(4,1)S(1)}, s32[]{:S(2)}) async-start(s8[4718592]{0:T(1024)(128)(4,1)} %bitcast.108), calls=%async_computation.6 | async-start | bytes 1048576
  38.8 2.2 slice-start.1
  39.6 1.8 copy-start.1
  87.1 5.2 %copy-start.3 = (bf16[3072]{0:T(1024)(128)(2,1)S(1)}, bf16[3072]{0:T(1024)(128)(2,1)}, u32[]{:S(2)}) copy-start(bf16[3072]{0:T(1024)(128)(2,1)} %param.20) | copy-start | bytes 18436
  87.1 42.6 %all-to-all-start.2 = ((bf16[4,128,3072]{2,1,0:T(8,128)(2,1)}), bf16[4,128,3072]{2,1,0:T(8,128)(2,1)}, u32[]{:S(2)}, u32[]{:S(2)}) async-start(bf16[4,128,3072]{2,1,0:T(8,128)(2,1)} %bitcast.27), calls=%async_computation.2 | async-start | bytes 6291456 | tf_op jit(solution)/shard_map/all_to_all | solution.py:98
  92.3 40.0 %copy-start = (bf16[128,3072]{1,0:T(8,128)(2,1)S(1)}, bf16[128,3072]{1,0:T(8,128)(2,1)}, u32[]{:S(2)}) copy-start(bf16[128,3072]{1,0:T(8,128)(2,1)} %param.12) | copy-start | bytes 2359300
  92.3 131.1 %all-gather.2.cloned.1.call-start = ((), (), s32[]{:S(2)}) async-start(), calls=%async_computation.5 | async-start | bytes 3538944 | tf_op jit(solution)/shard_map/all_gather | solution.py:114
  133.7 10.9 %collective-permute-start.1 = (bf16[3072,512]{1,0:T(8,128)(2,1)}, bf16[3072,512]{1,0:T(8,128)(2,1)}, u32[]{:S(2)}, u32[]{:S(2)}) collective-permute-start(bf16[3072,512]{1,0:T(8,128)(2,1)} %param.21), channel_id=1, source_target_pairs={{0,1},{1,0},{2,3},{3,2},{4,5},{5,4},{6,7},{7,6},{8,9},{9,8},{10,11... | collective-permute-start | bytes 9437192 | tf_op jit(solution)/shard_map/ppermute | solution.py:106
  137.4 50.8 %all-to-all-start.3 = ((bf16[8,64,3072]{2,1,0:T(8,128)(2,1)}), bf16[8,64,3072]{2,1,0:T(8,128)(2,1)}, u32[]{:S(2)}, u32[]{:S(2)}) async-start(bf16[8,64,3072]{2,1,0:T(8,128)(2,1)} %broadcast_in_dim.88), calls=%async_computation.3 | async-start | bytes 6291456 | tf_op jit(solution)/shard_map/all_to_all | solution.py:115
  144.1 92.6 %collective-permute-start.2 = (bf16[3072,512]{1,0:T(8,128)(2,1)}, bf16[3072,512]{1,0:T(8,128)(2,1)}, u32[]{:S(2)}, u32[]{:S(2)}) collective-permute-start(bf16[3072,512]{1,0:T(8,128)(2,1)} %param.22), channel_id=1, source_target_pairs={{0,1},{1,0},{2,3},{3,2},{4,5},{5,4},{6,7},{7,6},{8,9},{9,8},{10,11... | collective-permute-start | bytes 9437192 | tf_op jit(solution)/shard_map/ppermute | solution.py:107
  144.4 104.8 %collective-permute-start.3 = (bf16[512,3072]{1,0:T(8,128)(2,1)}, bf16[512,3072]{1,0:T(8,128)(2,1)}, u32[]{:S(2)}, u32[]{:S(2)}) collective-permute-start(bf16[512,3072]{1,0:T(8,128)(2,1)} %param.23), channel_id=1, source_target_pairs={{0,1},{1,0},{2,3},{3,2},{4,5},{5,4},{6,7},{7,6},{8,9},{9,8},{10,11... | collective-permute-start | bytes 9437192 | tf_op jit(solution)/shard_map/ppermute | solution.py:108
  223.4 13.4 %copy-start.4 = (bf16[3072,512]{1,0:T(8,128)(2,1)S(1)}, bf16[3072,512]{1,0:T(8,128)(2,1)}, u32[]{:S(2)}) copy-start(bf16[3072,512]{1,0:T(8,128)(2,1)} %param.22) | copy-start | bytes 9437188
  223.4 13.4 %copy-start.6 = (bf16[512,3072]{1,0:T(8,128)(2,1)S(1)}, bf16[512,3072]{1,0:T(8,128)(2,1)}, u32[]{:S(2)}) copy-start(bf16[512,3072]{1,0:T(8,128)(2,1)} %all-gather.2.cloned.1.call-done) | copy-start | bytes 9437188
  236.7 12.5 %copy-start.5 = (bf16[512,3072]{1,0:T(8,128)(2,1)S(1)}, bf16[512,3072]{1,0:T(8,128)(2,1)}, u32[]{:S(2)}) copy-start(bf16[512,3072]{1,0:T(8,128)(2,1)} %param.23) | copy-start | bytes 9437188
  261.3 75.9 %all-to-all-start.4 = ((bf16[2,8,64,3072]{3,2,0,1:T(8,128)(2,1)}), bf16[2,8,64,3072]{3,2,0,1:T(8,128)(2,1)}, u32[]{:S(2)}, u32[]{:S(2)}) async-start(bf16[2,8,64,3072]{3,2,0,1:T(8,128)(2,1)} %copy.43), calls=%async_computation.4 | async-start | bytes 12582912 | tf_op jit(solution)/shard_map/all_to_all | solution.py:128
Sparse Core Ops, SparseCore 0:
  133.9 89.4 all-gather.1

commit v7 on v5

--- a/solution.py
+++ b/solution.py
@@ -106,13 +106,17 @@
     gate_both = jnp.concatenate([gate_weight, lax.ppermute(gate_weight, "core", swap)], axis=1)
     up_both = jnp.concatenate([up_weight, lax.ppermute(up_weight, "core", swap)], axis=1)
     down_both = jnp.concatenate([down_weight, lax.ppermute(down_weight, "core", swap)], axis=0)
-    gathered = lax.all_gather(normed, ("x_hi", "y"), axis=0, tiled=True)
+    feed_axes = ("x_hi", "y")
+    n_feed = lax.axis_size(feed_axes)
+    gathered = lax.all_to_all(
+        jnp.broadcast_to(normed[None], (n_feed,) + normed.shape), feed_axes, 0, 0, tiled=False
+    ).reshape(n_feed * rows_here, normed.shape[1])
     gate = jnp.dot(gathered, gate_both, preferred_element_type=jnp.float32)
     upper = jnp.dot(gathered, up_both, preferred_element_type=jnp.float32)
     hidden = (jax.nn.silu(gate) * upper).astype(jnp.bfloat16)
     parts = jnp.dot(hidden, down_both, preferred_element_type=jnp.float32).astype(jnp.bfloat16)
     parts = lax.all_to_all(
-        parts.reshape(-1, rows_here, parts.shape[1]), ("x_hi", "y"), 0, 0, tiled=False
+        parts.reshape(n_feed, rows_here, parts.shape[1]), feed_axes, 0, 0, tiled=False
     )
     feed = jnp.sum(parts.astype(jnp.float32), axis=0)
     live = offsets < suffix_len[0]

time: 341 us -> 321 us (0.941)
  waiting for transfers between devices: 224 us -> 207 us
  between operations: 15 us -> 1.61 us
  starting transfers between devices: 20.8 us -> 28 us
    all_gather x1 -> x0, waiting for transfers between devices: 80.8 us -> none  [shards(): gathered = lax.all_gather(normed, ('x_hi', 'y'), axis=0, tiled=True)]
    all_to_all x1 -> x2, waiting for transfers between devices: 70.5 us -> 134 us  [the longest x1 70.6 us: shards(): lax.all_to_all(parts.reshape(n_feed, rows_here, parts.shape[1]), feed_axe...]
    all_to_all x1 -> x2, starting transfers between devices: 4.76 us -> 11.5 us  [the longest x1 6.35 us: shards(): lax.all_to_all(jnp.broadcast_to(normed[None], (n_feed,) + normed.shape),...]
    broadcast_in_dim x0 -> x1, local copies, waits for them, and re-layouts: none -> 3.42 us  [shards(): jnp.broadcast_to(normed[None], (n_feed,) + normed.shape)]
  transfers between devices with their start and end apart: 8 -> 8, of which waited for: 6 -> 6; matrix products, arithmetic and copies ran while one was open for 10% -> 11% of each run, Pallas kernels for 0% -> 0%
where the time goes in v7:
time: 321 us
  waiting for transfers between devices  207 us (64%)
  matrix products  44 us (14%)
  starting transfers between devices  28 us (9%)
  blocking collectives  15.4 us (5%)
  other arithmetic  14.4 us (4%)
  local copies, waits for them, and re-layouts  10.4 us (3%)
    all_to_all x1, waiting for transfers between devices, shards(): lax.all_to_all(parts.reshape(n_feed, rows_here, parts.shape[1]), feed_axe...  70.6 us
    all_to_all x1, waiting for transfers between devices, shards(): lax.all_to_all(jnp.broadcast_to(normed[None], (n_feed,) + normed.shape),...  63.5 us
    all_to_all x1, waiting for transfers between devices, shards(): lax.all_to_all(partial.reshape(n_z, rows_here, partial.shape[1]), 'z', 0,...  37.8 us
    ppermute x1, waiting for transfers between devices, shards(): lax.ppermute(out_weight, 'x_lo', [(0, 1), (1, 0)])  21.7 us
    all_to_all x1, blocking collectives, shards(): lax.all_to_all(halves.reshape(rows_here, n_z, block), 'z', 1, 0, tiled=Fa...  15.4 us
    dot_general x1, matrix products, shards(): gate = jnp.dot(gathered, gate_both, preferred_element_type=jnp.float32)  10.7 us
    dot_general x1, matrix products, shards(): jnp.dot(hidden, down_both, preferred_element_type=jnp.float32)  10.6 us
    dot_general x1, matrix products, shards(): upper = jnp.dot(gathered, up_both, preferred_element_type=jnp.float32)  9.89 us
  transfers between devices with their start and end apart: 8, of which 6 were waited for; matrix products, arithmetic and copies ran while one was open for 11% of the time, Pallas kernels for 0%

profile of v7, /device:TPU:1, one launch (start us, length us, event | category | flops | bytes accessed | tf_op | source)
XLA Modules:
  0.0 320.7 jit_solution(1701924136619118118)
XLA Ops:
  0.0 0.0 copy-start.2
  0.0 2.0 broadcast_in_dim.85
  2.0 8.4 %all-to-all-start = ((bf16[16,16,2048]{2,1,0:T(8,128)(2,1)}), bf16[16,16,2048]{2,1,0:T(8,128)(2,1)S(1)}, u32[]{:S(2)}, u32[]{:S(2)}) async-start(bf16[16,16,2048]{2,1,0:T(8,128)(2,1)} %broadcast_in_dim.85), calls=%async_computation | async-start | bytes 2097152 | tf_op jit(solution)/shard_map/all_to_all | solution.py:75
  10.4 0.3 collective-permute-start
  11.5 1.5 copy.31
  12.9 0.0 copy-done.2
  13.0 0.3 copy.32
  13.2 1.5 copy.33
  14.8 1.0 pad_maximum_fusion
  15.8 0.1 fusion.51
  15.9 0.2 fusion.50
  16.1 3.0 fusion.22
  19.2 8.3 %all-to-all-done = bf16[16,16,2048]{2,1,0:T(8,128)(2,1)S(1)} async-done(((bf16[16,16,2048]{2,1,0:T(8,128)(2,1)}), bf16[16,16,2048]{2,1,0:T(8,128)(2,1)S(1)}, u32[]{:S(2)}, u32[]{:S(2)}) %all-to-all-start) | async-done | bytes 1048608 | tf_op jit(solution)/shard_map/all_to_all | solution.py:75
  27.5 0.1 fusion.70
  27.6 0.2 copy.37
  27.8 0.2 copy.40
  28.0 0.7 fusion.25
  28.7 0.0 slice-start
  28.7 3.5 %fusion.23 = f32[8,3,128]{2,1,0:T(4,128)S(1)} fusion(f32[8,384,128,3]{2,1,3,0:T(8,128)} %get-tuple-element.15, f32[8,3,128]{2,1,0:T(4,128)S(1)} %get-tuple-element.12, pred[128,384]{0,1:T(8,128)(4,1)S(1)} %fusion.50), kind=kLoop, calls=%fused_computation.24 | loop fusion | flops 5895168 | bytes 4792320 | tf_op jit(solution)/shard_map/reduce_sum | solution.py:33
  32.2 0.0 slice-start.1
  32.2 0.8 fusion.33
  33.0 0.0 copy-start.1
  33.1 0.8 fusion.36
  33.9 0.0 slice-done
  33.9 0.5 slice-done.1
  34.4 0.4 copy-done.1
  34.8 1.6 fusion.39
  36.4 0.2 reverse_select_fusion
  36.5 0.3 copy.55
  36.8 15.4 %all_to_all.35 = bf16[1,128,4,768]{3,1,0,2:T(8,128)(2,1)S(1)} all-to-all(bf16[1,128,4,768]{3,1,0,2:T(8,128)(2,1)S(1)} %copy.55), channel_id=1, replica_groups=mesh['z'=4,'x_lo'=2,'x_hi'=2,'y'=4,'core'=2] {'z'}, dimensions={2} | all-to-all | bytes 1572864 | tf_op jit(solution)/shard_map/all_to_all | solution.py:94
  52.2 21.7 %collective-permute-done = bf16[384,3072]{1,0:T(8,128)(2,1)} collective-permute-done((bf16[384,3072]{1,0:T(8,128)(2,1)}, bf16[384,3072]{1,0:T(8,128)(2,1)}, u32[]{:S(2)}, u32[]{:S(2)}) %collective-permute-start) | collective-permute-done | bytes 2359328 | tf_op jit(solution)/shard_map/ppermute | solution.py:89
  73.9 6.7 %fusion.19 = bf16[512,3072]{1,0:T(8,128)(2,1)} fusion(bf16[512,768]{1,0:T(8,128)(2,1)S(1)} %bitcast.113, bf16[384,3072]{1,0:T(8,128)(2,1)} %collective-permute-done, bf16[384,3072]{1,0:T(8,128)(2,1)} %param.19), kind=kOutput, calls=%fused_computation.21 | convolution fusion | flops 2426929152 | bytes 8650752 | tf_op jit(solution)/shard_map/dot_general | solution.py:97
  80.6 0.0 copy-start.3
  80.6 5.2 %all-to-all-start.2 = ((bf16[4,128,3072]{2,1,0:T(8,128)(2,1)}), bf16[4,128,3072]{2,1,0:T(8,128)(2,1)}, u32[]{:S(2)}, u32[]{:S(2)}) async-start(bf16[4,128,3072]{2,1,0:T(8,128)(2,1)} %bitcast.27), calls=%async_computation.2 | async-start | bytes 6291456 | tf_op jit(solution)/shard_map/all_to_all | solution.py:98
  85.7 0.0 copy-done.3
  85.7 0.0 copy-start
  85.7 37.8 %all-to-all-done.2 = bf16[4,128,3072]{2,1,0:T(8,128)(2,1)} async-done(((bf16[4,128,3072]{2,1,0:T(8,128)(2,1)}), bf16[4,128,3072]{2,1,0:T(8,128)(2,1)}, u32[]{:S(2)}, u32[]{:S(2)}) %all-to-all-start.2) | async-done | bytes 3145760 | tf_op jit(solution)/shard_map/all_to_all | solution.py:98
  123.5 2.6 convert_reduce_fusion.1
  126.1 0.0 copy-done
  126.1 0.3 multiply_reduce_fusion
  126.4 0.3 multiply_convert_fusion.2
  126.7 3.4 %broadcast_in_dim.88 = bf16[8,128,3072]{2,1,0:T(8,128)(2,1)} broadcast(bf16[128,3072]{1,0:T(8,128)(2,1)S(1)} %multiply_convert_fusion.2), dimensions={1,2} | broadcast | bytes 7077888 | tf_op jit(solution)/shard_map/broadcast_in_dim | solution.py:112
  130.2 6.3 %all-to-all-start.3 = ((bf16[8,128,3072]{2,1,0:T(8,128)(2,1)}), bf16[8,128,3072]{2,1,0:T(8,128)(2,1)}, u32[]{:S(2)}, u32[]{:S(2)}) async-start(bf16[8,128,3072]{2,1,0:T(8,128)(2,1)} %broadcast_in_dim.88), calls=%async_computation.3 | async-start | bytes 12582912 | tf_op jit(solution)/shard_map/all_to_all | solution.py:111
  136.5 2.1 collective-permute-start.1
  138.6 0.1 collective-permute-start.2
  138.7 0.4 collective-permute-start.3
  139.1 5.1 %collective-permute-done.1 = bf16[3072,512]{1,0:T(8,128)(2,1)} collective-permute-done((bf16[3072,512]{1,0:T(8,128)(2,1)}, bf16[3072,512]{1,0:T(8,128)(2,1)}, u32[]{:S(2)}, u32[]{:S(2)}) %collective-permute-start.1) | collective-permute-done | bytes 3145760 | tf_op jit(solution)/shard_map/ppermute | solution.py:106
  144.2 63.5 %all-to-all-done.3 = bf16[8,128,3072]{2,1,0:T(8,128)(2,1)} async-done(((bf16[8,128,3072]{2,1,0:T(8,128)(2,1)}), bf16[8,128,3072]{2,1,0:T(8,128)(2,1)}, u32[]{:S(2)}, u32[]{:S(2)}) %all-to-all-start.3) | async-done | bytes 6291488 | tf_op jit(solution)/shard_map/all_to_all | solution.py:111
  207.7 0.0 copy-start.4
  207.7 10.7 %fusion = f32[1024,1024]{1,0:T(8,128)S(1)} fusion(bf16[1024,3072]{1,0:T(8,128)(2,1)} %bitcast.28, bf16[3072,512]{1,0:T(8,128)(2,1)} %collective-permute-done.1, bf16[3072,512]{1,0:T(8,128)(2,1)} %param.21), kind=kOutput, calls=%fused_computation.1 | convolution fusion | flops 6455033856 | bytes 16777216 | tf_op jit(solution)/shard_map/dot_general | solution.py:114
  218.5 0.0 copy-start.5
  218.5 0.0 collective-permute-done.2
  218.5 0.0 copy-done.4
  218.5 9.9 %fusion.4 = f32[1024,1024]{1,0:T(8,128)S(1)} fusion(bf16[1024,3072]{1,0:T(8,128)(2,1)} %bitcast.28, bf16[3072,512]{1,0:T(8,128)(2,1)} %collective-permute-done.2, bf16[3072,512]{1,0:T(8,128)(2,1)S(1)} %copy-done.4), kind=kOutput, calls=%fused_computation.5 | convolution fusion | flops 6455033856 | bytes 16777216 | tf_op jit(solution)/shard_map/dot_general | solution.py:115
  228.4 0.0 collective-permute-done.3
  228.4 0.0 copy-done.5
  228.4 10.6 %fusion.12 = bf16[1024,3072]{1,0:T(8,128)(2,1)} fusion(bf16[512,3072]{1,0:T(8,128)(2,1)} %collective-permute-done.3, bf16[512,3072]{1,0:T(8,128)(2,1)S(1)} %copy-done.5, f32[1024,1024]{1,0:T(8,128)S(1)} %fusion.4, f32[1024,1024]{1,0:T(8,128)S(1)} %fusion), kind=kOutput, calls=%fused_computation.14 | convolution fusion | flops 6464471040 | bytes 20971520 | tf_op jit(solution)/shard_map/dot_general | solution.py:117
  239.0 5.2 %all-to-all-start.4 = ((bf16[8,128,3072]{2,1,0:T(8,128)(2,1)}), bf16[8,128,3072]{2,1,0:T(8,128)(2,1)}, u32[]{:S(2)}, u32[]{:S(2)}) async-start(bf16[8,128,3072]{2,1,0:T(8,128)(2,1)} %bitcast.107), calls=%async_computation.4 | async-start | bytes 12582912 | tf_op jit(solution)/shard_map/all_to_all | solution.py:118
  244.9 70.6 %all-to-all-done.4 = bf16[8,128,3072]{2,1,0:T(8,128)(2,1)} async-done(((bf16[8,128,3072]{2,1,0:T(8,128)(2,1)}), bf16[8,128,3072]{2,1,0:T(8,128)(2,1)}, u32[]{:S(2)}, u32[]{:S(2)}) %all-to-all-start.4) | async-done | bytes 6291488 | tf_op jit(solution)/shard_map/all_to_all | solution.py:118
  315.4 4.0 %convert_reduce_fusion = f32[128,3072]{1,0:T(8,128)S(1)} fusion(bf16[8,128,3072]{2,1,0:T(8,128)(2,1)} %all-to-all-done.4), kind=kLoop, calls=%fused_computation | loop fusion | flops 5898240 | bytes 7864320 | tf_op jit(solution)/shard_map/reduce_sum | solution.py:121
  319.5 1.3 select_convert_fusion
  (13 shorter events, 0.1 us)
Async XLA Ops:
  0.0 12.9 %copy-start.2 = (bf16[128,2048]{1,0:T(8,128)(2,1)S(1)}, bf16[128,2048]{1,0:T(8,128)(2,1)}, u32[]{:S(2)}) copy-start(bf16[128,2048]{1,0:T(8,128)(2,1)} %param.14) | copy-start | bytes 1572868
  2.0 25.5 %all-to-all-start = ((bf16[16,16,2048]{2,1,0:T(8,128)(2,1)}), bf16[16,16,2048]{2,1,0:T(8,128)(2,1)S(1)}, u32[]{:S(2)}, u32[]{:S(2)}) async-start(bf16[16,16,2048]{2,1,0:T(8,128)(2,1)} %broadcast_in_dim.85), calls=%async_computation | async-start | bytes 2097152 | tf_op jit(solution)/shard_map/all_to_all | solution.py:75
  10.4 63.5 %collective-permute-start = (bf16[384,3072]{1,0:T(8,128)(2,1)}, bf16[384,3072]{1,0:T(8,128)(2,1)}, u32[]{:S(2)}, u32[]{:S(2)}) collective-permute-start(bf16[384,3072]{1,0:T(8,128)(2,1)} %param.19), channel_id=1, source_target_pairs={{0,16},{16,0},{1,17},{17,1},{2,18},{18,2},{3,19},{19,3},{4,20},{20... | collective-permute-start | bytes 7077896 | tf_op jit(solution)/shard_map/ppermute | solution.py:89
  28.7 5.2 %slice-start = ((s8[4718592]{0:T(1024)(128)(4,1)}), s8[524288]{0:T(1024)(128)(4,1)S(1)}, s32[]{:S(2)}) async-start(s8[4718592]{0:T(1024)(128)(4,1)} %bitcast.103), calls=%async_computation.5 | async-start | bytes 1048576
  32.2 2.2 slice-start.1
  33.0 1.8 copy-start.1
  80.6 5.2 %copy-start.3 = (bf16[3072]{0:T(1024)(128)(2,1)S(1)}, bf16[3072]{0:T(1024)(128)(2,1)}, u32[]{:S(2)}) copy-start(bf16[3072]{0:T(1024)(128)(2,1)} %param.20) | copy-start | bytes 18436
  80.6 42.9 %all-to-all-start.2 = ((bf16[4,128,3072]{2,1,0:T(8,128)(2,1)}), bf16[4,128,3072]{2,1,0:T(8,128)(2,1)}, u32[]{:S(2)}, u32[]{:S(2)}) async-start(bf16[4,128,3072]{2,1,0:T(8,128)(2,1)} %bitcast.27), calls=%async_computation.2 | async-start | bytes 6291456 | tf_op jit(solution)/shard_map/all_to_all | solution.py:98
  85.7 40.4 %copy-start = (bf16[128,3072]{1,0:T(8,128)(2,1)S(1)}, bf16[128,3072]{1,0:T(8,128)(2,1)}, u32[]{:S(2)}) copy-start(bf16[128,3072]{1,0:T(8,128)(2,1)} %param.12) | copy-start | bytes 2359300
  130.2 77.6 %all-to-all-start.3 = ((bf16[8,128,3072]{2,1,0:T(8,128)(2,1)}), bf16[8,128,3072]{2,1,0:T(8,128)(2,1)}, u32[]{:S(2)}, u32[]{:S(2)}) async-start(bf16[8,128,3072]{2,1,0:T(8,128)(2,1)} %broadcast_in_dim.88), calls=%async_computation.3 | async-start | bytes 12582912 | tf_op jit(solution)/shard_map/all_to_all | solution.py:111
  136.5 7.7 %collective-permute-start.1 = (bf16[3072,512]{1,0:T(8,128)(2,1)}, bf16[3072,512]{1,0:T(8,128)(2,1)}, u32[]{:S(2)}, u32[]{:S(2)}) collective-permute-start(bf16[3072,512]{1,0:T(8,128)(2,1)} %param.21), channel_id=1, source_target_pairs={{0,1},{1,0},{2,3},{3,2},{4,5},{5,4},{6,7},{7,6},{8,9},{9,8},{10,11... | collective-permute-start | bytes 9437192 | tf_op jit(solution)/shard_map/ppermute | solution.py:106
  138.6 79.9 %collective-permute-start.2 = (bf16[3072,512]{1,0:T(8,128)(2,1)}, bf16[3072,512]{1,0:T(8,128)(2,1)}, u32[]{:S(2)}, u32[]{:S(2)}) collective-permute-start(bf16[3072,512]{1,0:T(8,128)(2,1)} %param.22), channel_id=1, source_target_pairs={{0,1},{1,0},{2,3},{3,2},{4,5},{5,4},{6,7},{7,6},{8,9},{9,8},{10,11... | collective-permute-start | bytes 9437192 | tf_op jit(solution)/shard_map/ppermute | solution.py:107
  138.7 89.8 %collective-permute-start.3 = (bf16[512,3072]{1,0:T(8,128)(2,1)}, bf16[512,3072]{1,0:T(8,128)(2,1)}, u32[]{:S(2)}, u32[]{:S(2)}) collective-permute-start(bf16[512,3072]{1,0:T(8,128)(2,1)} %param.23), channel_id=1, source_target_pairs={{0,1},{1,0},{2,3},{3,2},{4,5},{5,4},{6,7},{7,6},{8,9},{9,8},{10,11... | collective-permute-start | bytes 9437192 | tf_op jit(solution)/shard_map/ppermute | solution.py:108
  207.7 10.8 %copy-start.4 = (bf16[3072,512]{1,0:T(8,128)(2,1)S(1)}, bf16[3072,512]{1,0:T(8,128)(2,1)}, u32[]{:S(2)}) copy-start(bf16[3072,512]{1,0:T(8,128)(2,1)} %param.22) | copy-start | bytes 9437188
  218.5 9.9 %copy-start.5 = (bf16[512,3072]{1,0:T(8,128)(2,1)S(1)}, bf16[512,3072]{1,0:T(8,128)(2,1)}, u32[]{:S(2)}) copy-start(bf16[512,3072]{1,0:T(8,128)(2,1)} %param.23) | copy-start | bytes 9437188
  239.0 76.4 %all-to-all-start.4 = ((bf16[8,128,3072]{2,1,0:T(8,128)(2,1)}), bf16[8,128,3072]{2,1,0:T(8,128)(2,1)}, u32[]{:S(2)}, u32[]{:S(2)}) async-start(bf16[8,128,3072]{2,1,0:T(8,128)(2,1)} %bitcast.107), calls=%async_computation.4 | async-start | bytes 12582912 | tf_op jit(solution)/shard_map/all_to_all | solution.py:118

commit v8 on v7

--- a/solution.py
+++ b/solution.py
@@ -108,17 +108,23 @@
     down_both = jnp.concatenate([down_weight, lax.ppermute(down_weight, "core", swap)], axis=0)
     feed_axes = ("x_hi", "y")
     n_feed = lax.axis_size(feed_axes)
-    gathered = lax.all_to_all(
-        jnp.broadcast_to(normed[None], (n_feed,) + normed.shape), feed_axes, 0, 0, tiled=False
-    ).reshape(n_feed * rows_here, normed.shape[1])
-    gate = jnp.dot(gathered, gate_both, preferred_element_type=jnp.float32)
-    upper = jnp.dot(gathered, up_both, preferred_element_type=jnp.float32)
-    hidden = (jax.nn.silu(gate) * upper).astype(jnp.bfloat16)
-    parts = jnp.dot(hidden, down_both, preferred_element_type=jnp.float32).astype(jnp.bfloat16)
-    parts = lax.all_to_all(
-        parts.reshape(n_feed, rows_here, parts.shape[1]), feed_axes, 0, 0, tiled=False
-    )
-    feed = jnp.sum(parts.astype(jnp.float32), axis=0)
+    chunks = 2
+    size = rows_here // chunks
+    feeds = []
+    for c in range(chunks):
+        rows = normed[c * size : (c + 1) * size]
+        gathered = lax.all_to_all(
+            jnp.broadcast_to(rows[None], (n_feed,) + rows.shape), feed_axes, 0, 0, tiled=False
+        ).reshape(n_feed * size, rows.shape[1])
+        gate = jnp.dot(gathered, gate_both, preferred_element_type=jnp.float32)
+        upper = jnp.dot(gathered, up_both, preferred_element_type=jnp.float32)
+        hidden = (jax.nn.silu(gate) * upper).astype(jnp.bfloat16)
+        parts = jnp.dot(hidden, down_both, preferred_element_type=jnp.float32).astype(jnp.bfloat16)
+        parts = lax.all_to_all(
+            parts.reshape(n_feed, size, parts.shape[1]), feed_axes, 0, 0, tiled=False
+        )
+        feeds.append(jnp.sum(parts.astype(jnp.float32), axis=0))
+    feed = jnp.concatenate(feeds, axis=0)
     live = offsets < suffix_len[0]
     return jnp.where(live[:, None], mixed + feed, 0.0).astype(jnp.bfloat16)
 

time: 321 us -> 307 us (0.956)
  waiting for transfers between devices: 207 us -> 148 us
  local copies, waits for them, and re-layouts: 10.4 us -> 30.5 us
  matrix products: 44 us -> 58.8 us
  starting transfers between devices: 28 us -> 37.1 us
    all_to_all x2 -> x4, waiting for transfers between devices: 134 us -> 80.7 us  [the longest x2 48.9 us: shards(): lax.all_to_all(parts.reshape(n_feed, size, parts.shape[1]), feed_axes, 0,...]
    dot_general x1 -> x2, matrix products: 10.6 us -> 28.9 us  [shards(): jnp.dot(hidden, down_both, preferred_element_type=jnp.float32)]
    concatenate x0 -> x3, local copies, waits for them, and re-layouts: none -> 11.5 us  [the longest x1 3.87 us: shards(): jnp.concatenate([gate_weight, lax.ppermute(gate_weight, 'core', swap)], a...]
    all_to_all x2 -> x4, starting transfers between devices: 11.5 us -> 21.8 us  [the longest x2 11.5 us: shards(): lax.all_to_all(jnp.broadcast_to(rows[None], (n_feed,) + rows.shape), feed...]
    dot_general x1 -> x0, matrix products: 9.89 us -> none  [shards(): upper = jnp.dot(gathered, up_both, preferred_element_type=jnp.float32)]
    unnamed x19 -> x24, local copies, waits for them, and re-layouts: 4.19 us -> 11.9 us
    dot_general x1 -> x2, matrix products: 10.7 us -> 17 us  [shards(): gate = jnp.dot(gathered, gate_both, preferred_element_type=jnp.float32)]
    ppermute x1, waiting for transfers between devices: 5.12 us -> 0.01 us  [shards(): lax.ppermute(gate_weight, 'core', swap)]
  transfers between devices with their start and end apart: 8 -> 10, of which waited for: 6 -> 7; matrix products, arithmetic and copies ran while one was open for 11% -> 29% of each run, Pallas kernels for 0% -> 0%
where the time goes in v8:
time: 307 us; the launch traced here: 306 us
  waiting for transfers between devices  148 us (48%)
  matrix products  58.8 us (19%)
  starting transfers between devices  37.1 us (12%)
  local copies, waits for them, and re-layouts  30.5 us (10%)
  blocking collectives  15.4 us (5%)
  other arithmetic  15.3 us (5%)
    all_to_all x2, waiting for transfers between devices, shards(): lax.all_to_all(parts.reshape(n_feed, size, parts.shape[1]), feed_axes, 0,...  48.9 us
    all_to_all x1, waiting for transfers between devices, shards(): lax.all_to_all(partial.reshape(n_z, rows_here, partial.shape[1]), 'z', 0,...  36 us
    all_to_all x2, waiting for transfers between devices, shards(): lax.all_to_all(jnp.broadcast_to(rows[None], (n_feed,) + rows.shape), feed...  31.8 us
    dot_general x2, matrix products, shards(): jnp.dot(hidden, down_both, preferred_element_type=jnp.float32)  28.9 us
    ppermute x1, waiting for transfers between devices, shards(): lax.ppermute(out_weight, 'x_lo', [(0, 1), (1, 0)])  21.7 us
    dot_general x2, matrix products, shards(): gate = jnp.dot(gathered, gate_both, preferred_element_type=jnp.float32)  17 us
    all_to_all x1, blocking collectives, shards(): lax.all_to_all(halves.reshape(rows_here, n_z, block), 'z', 1, 0, tiled=Fa...  15.4 us
    unnamed x24, local copies, waits for them, and re-layouts  11.9 us
  transfers between devices with their start and end apart: 10, of which 7 were waited for; matrix products, arithmetic and copies ran while one was open for 29% of the time, Pallas kernels for 0%

profile of v8, /device:TPU:1, one launch (start us, length us, event | category | flops | bytes accessed | tf_op | source)
XLA Modules:
  0.0 306.5 jit_solution(2199251099168579147)
XLA Ops:
  0.0 2.0 broadcast_in_dim.91
  2.1 8.4 %all-to-all-start = ((bf16[16,16,2048]{2,1,0:T(8,128)(2,1)}), bf16[16,16,2048]{2,1,0:T(8,128)(2,1)S(1)}, u32[]{:S(2)}, u32[]{:S(2)}) async-start(bf16[16,16,2048]{2,1,0:T(8,128)(2,1)} %broadcast_in_dim.91), calls=%async_computation | async-start | bytes 2097152 | tf_op jit(solution)/shard_map/all_to_all | solution.py:75
  10.5 0.3 collective-permute-start
  11.5 0.3 copy.32
  11.8 0.4 copy.33
  12.2 1.5 copy.31
  13.7 1.0 pad_maximum_fusion
  14.7 0.1 fusion.39
  14.9 0.2 fusion.38
  15.1 3.0 fusion.7
  18.1 9.4 %all-to-all-done = bf16[16,16,2048]{2,1,0:T(8,128)(2,1)S(1)} async-done(((bf16[16,16,2048]{2,1,0:T(8,128)(2,1)}), bf16[16,16,2048]{2,1,0:T(8,128)(2,1)S(1)}, u32[]{:S(2)}, u32[]{:S(2)}) %all-to-all-start) | async-done | bytes 1048608 | tf_op jit(solution)/shard_map/all_to_all | solution.py:75
  27.6 0.1 fusion.56
  27.7 0.2 copy.37
  27.9 0.2 copy.40
  28.1 0.7 fusion.10
  28.7 0.0 slice-start
  28.8 3.5 %fusion.8 = f32[8,3,128]{2,1,0:T(4,128)S(1)} fusion(f32[8,384,128,3]{2,1,3,0:T(8,128)} %get-tuple-element.17, f32[8,3,128]{2,1,0:T(4,128)S(1)} %get-tuple-element.14, pred[128,384]{0,1:T(8,128)(4,1)S(1)} %fusion.38), kind=kLoop, calls=%fused_computation.13 | loop fusion | flops 5895168 | bytes 4792320 | tf_op jit(solution)/shard_map/reduce_sum | solution.py:33
  32.3 0.8 fusion.18
  33.1 0.0 copy-start.4
  33.1 0.8 fusion.20
  34.0 0.5 slice-done.1
  34.5 0.4 copy-done.4
  34.9 1.6 fusion.25
  36.4 0.2 reverse_select_fusion
  36.6 0.3 copy.55
  36.9 15.4 %all_to_all.45 = bf16[1,128,4,768]{3,1,0,2:T(8,128)(2,1)S(1)} all-to-all(bf16[1,128,4,768]{3,1,0,2:T(8,128)(2,1)S(1)} %copy.55), channel_id=1, replica_groups=mesh['z'=4,'x_lo'=2,'x_hi'=2,'y'=4,'core'=2] {'z'}, dimensions={2} | all-to-all | bytes 1572864 | tf_op jit(solution)/shard_map/all_to_all | solution.py:94
  52.3 21.7 %collective-permute-done = bf16[384,3072]{1,0:T(8,128)(2,1)} collective-permute-done((bf16[384,3072]{1,0:T(8,128)(2,1)}, bf16[384,3072]{1,0:T(8,128)(2,1)}, u32[]{:S(2)}, u32[]{:S(2)}) %collective-permute-start) | collective-permute-done | bytes 2359328 | tf_op jit(solution)/shard_map/ppermute | solution.py:89
  74.0 6.7 %fusion.4 = bf16[512,3072]{1,0:T(8,128)(2,1)} fusion(bf16[512,768]{1,0:T(8,128)(2,1)S(1)} %bitcast.124, bf16[384,3072]{1,0:T(8,128)(2,1)} %collective-permute-done, bf16[384,3072]{1,0:T(8,128)(2,1)} %param.19), kind=kOutput, calls=%fused_computation.9 | convolution fusion | flops 2426929152 | bytes 8650752 | tf_op jit(solution)/shard_map/dot_general | solution.py:97
  80.7 5.2 %all-to-all-start.2 = ((bf16[4,128,3072]{2,1,0:T(8,128)(2,1)}), bf16[4,128,3072]{2,1,0:T(8,128)(2,1)}, u32[]{:S(2)}, u32[]{:S(2)}) async-start(bf16[4,128,3072]{2,1,0:T(8,128)(2,1)} %bitcast.27), calls=%async_computation.2 | async-start | bytes 6291456 | tf_op jit(solution)/shard_map/all_to_all | solution.py:98
  85.9 0.9 collective-permute-start.1
  86.8 0.1 collective-permute-start.2
  86.8 0.4 collective-permute-start.3
  87.3 36.0 %all-to-all-done.2 = bf16[4,128,3072]{2,1,0:T(8,128)(2,1)} async-done(((bf16[4,128,3072]{2,1,0:T(8,128)(2,1)}), bf16[4,128,3072]{2,1,0:T(8,128)(2,1)}, u32[]{:S(2)}, u32[]{:S(2)}) %all-to-all-start.2) | async-done | bytes 3145760 | tf_op jit(solution)/shard_map/all_to_all | solution.py:98
  123.2 2.6 convert_reduce_fusion.2
  125.8 0.3 multiply_reduce_fusion
  126.2 0.3 multiply_convert_fusion.2
  126.5 0.1 fusion.57
  126.5 2.1 broadcast_in_dim.95
  128.6 6.3 %all-to-all-start.5 = ((bf16[8,64,3072]{2,1,0:T(8,128)(2,1)}), bf16[8,64,3072]{2,1,0:T(8,128)(2,1)}, u32[]{:S(2)}, u32[]{:S(2)}) async-start(bf16[8,64,3072]{2,1,0:T(8,128)(2,1)} %broadcast_in_dim.95), calls=%async_computation.5 | async-start | bytes 6291456 | tf_op jit(solution)/shard_map/all_to_all | solution.py:116
  135.0 4.0 %constant_dynamic-update-slice_fusion.1 = bf16[3072,1024]{1,0:T(8,128)(2,1)} fusion(bf16[3072,512]{1,0:T(8,128)(2,1)} %param.21), kind=kLoop, calls=%fused_computation.68 | loop fusion | bytes 6291456
  138.9 1.9 constant_dynamic-update-slice_fusion.3
  140.9 1.1 copy-done.2
  142.0 1.8 constant_dynamic-update-slice_fusion.5
  143.8 0.0 collective-permute-done.1
  143.8 3.9 %constant_dynamic-update-slice_fusion = bf16[3072,1024]{1,0:T(8,128)(2,1)} fusion(bf16[3072,1024]{1,0:T(8,128)(2,1)} %constant_dynamic-update-slice_fusion.1, bf16[3072,512]{1,0:T(8,128)(2,1)} %collective-permute-done.1), kind=kLoop, calls=%fused_computation.67 | loop fusion | bytes 6291456 | tf_op jit(solution)/shard_map/concatenate | solution.py:106
  147.7 0.0 collective-permute-done.2
  147.7 3.9 %constant_dynamic-update-slice_fusion.2 = bf16[3072,1024]{1,0:T(8,128)(2,1)} fusion(bf16[3072,1024]{1,0:T(8,128)(2,1)} %constant_dynamic-update-slice_fusion.3, bf16[3072,512]{1,0:T(8,128)(2,1)} %collective-permute-done.2), kind=kLoop, calls=%fused_computation.69 | loop fusion | bytes 6291456 | tf_op jit(solution)/shard_map/concatenate | solution.py:107
  151.5 21.0 %all-to-all-done.5 = bf16[8,64,3072]{2,1,0:T(8,128)(2,1)} async-done(((bf16[8,64,3072]{2,1,0:T(8,128)(2,1)}), bf16[8,64,3072]{2,1,0:T(8,128)(2,1)}, u32[]{:S(2)}, u32[]{:S(2)}) %all-to-all-start.5) | async-done | bytes 3145760 | tf_op jit(solution)/shard_map/all_to_all | solution.py:116
  172.5 2.1 broadcast_in_dim.94
  174.7 5.2 %all-to-all-start.3 = ((bf16[8,64,3072]{2,1,0:T(8,128)(2,1)}), bf16[8,64,3072]{2,1,0:T(8,128)(2,1)}, u32[]{:S(2)}, u32[]{:S(2)}) async-start(bf16[8,64,3072]{2,1,0:T(8,128)(2,1)} %broadcast_in_dim.94), calls=%async_computation.3 | async-start | bytes 6291456 | tf_op jit(solution)/shard_map/all_to_all | solution.py:116
  179.8 0.0 collective-permute-done.3
  179.8 3.8 %constant_dynamic-update-slice_fusion.4 = bf16[1024,3072]{1,0:T(8,128)(2,1)} fusion(bf16[1024,3072]{1,0:T(8,128)(2,1)} %constant_dynamic-update-slice_fusion.5, bf16[512,3072]{1,0:T(8,128)(2,1)} %collective-permute-done.3), kind=kLoop, calls=%fused_computation.71 | loop fusion | bytes 6291456 | tf_op jit(solution)/shard_map/concatenate | solution.py:108
  183.6 8.5 %fusion.63 = f32[512,1024]{1,0:T(8,128)} fusion(bf16[512,3072]{1,0:T(8,128)(2,1)} %bitcast.30, bf16[3072,1024]{1,0:T(8,128)(2,1)} %constant_dynamic-update-slice_fusion), kind=kOutput, calls=%fused_computation.97 | convolution fusion | flops 3221225472 | bytes 11534336 | tf_op jit(solution)/shard_map/dot_general | solution.py:119
  192.0 14.5 %convolution_convert_fusion = bf16[512,3072]{1,0:T(8,128)(2,1)} fusion(bf16[1024,3072]{1,0:T(8,128)(2,1)} %constant_dynamic-update-slice_fusion.4, f32[512,1024]{1,0:T(8,128)} %fusion.63, bf16[512,3072]{1,0:T(8,128)(2,1)} %bitcast.30, bf16[3072,1024]{1,0:T(8,128)(2,1)} %constant_dynamic-update-slice_fusion.2), kind=kOutput, calls=%fused_computation.10 | convolution fusion | flops 6447169536 | bytes 20971520 | tf_op jit(solution)/shard_map/dot_general | solution.py:122
  206.5 10.8 %all-to-all-done.3 = bf16[8,64,3072]{2,1,0:T(8,128)(2,1)} async-done(((bf16[8,64,3072]{2,1,0:T(8,128)(2,1)}), bf16[8,64,3072]{2,1,0:T(8,128)(2,1)}, u32[]{:S(2)}, u32[]{:S(2)}) %all-to-all-start.3) | async-done | bytes 3145760 | tf_op jit(solution)/shard_map/all_to_all | solution.py:116
  217.3 5.2 %all-to-all-start.6 = ((bf16[8,64,3072]{2,1,0:T(8,128)(2,1)}), bf16[8,64,3072]{2,1,0:T(8,128)(2,1)}, u32[]{:S(2)}, u32[]{:S(2)}) async-start(bf16[8,64,3072]{2,1,0:T(8,128)(2,1)} %bitcast.118), calls=%async_computation.6 | async-start | bytes 6291456 | tf_op jit(solution)/shard_map/all_to_all | solution.py:123
  222.5 8.6 %fusion.62 = f32[512,1024]{1,0:T(8,128)} fusion(bf16[512,3072]{1,0:T(8,128)(2,1)} %bitcast.28, bf16[3072,1024]{1,0:T(8,128)(2,1)} %constant_dynamic-update-slice_fusion), kind=kOutput, calls=%fused_computation.96 | convolution fusion | flops 3221225472 | bytes 11534336 | tf_op jit(solution)/shard_map/dot_general | solution.py:119
  231.1 14.5 %convolution_convert_fusion.1 = bf16[512,3072]{1,0:T(8,128)(2,1)} fusion(bf16[1024,3072]{1,0:T(8,128)(2,1)} %constant_dynamic-update-slice_fusion.4, f32[512,1024]{1,0:T(8,128)} %fusion.62, bf16[512,3072]{1,0:T(8,128)(2,1)} %bitcast.28, bf16[3072,1024]{1,0:T(8,128)(2,1)} %constant_dynamic-update-slice_fusion.2), kind=kOutput, calls=%fused_computation.11 | convolution fusion | flops 6447169536 | bytes 20971520 | tf_op jit(solution)/shard_map/dot_general | solution.py:122
  245.5 14.5 %all-to-all-done.6 = bf16[8,64,3072]{2,1,0:T(8,128)(2,1)} async-done(((bf16[8,64,3072]{2,1,0:T(8,128)(2,1)}), bf16[8,64,3072]{2,1,0:T(8,128)(2,1)}, u32[]{:S(2)}, u32[]{:S(2)}) %all-to-all-start.6) | async-done | bytes 3145760 | tf_op jit(solution)/shard_map/all_to_all | solution.py:123
  260.0 5.2 %all-to-all-start.4 = ((bf16[8,64,3072]{2,1,0:T(8,128)(2,1)}), bf16[8,64,3072]{2,1,0:T(8,128)(2,1)}, u32[]{:S(2)}, u32[]{:S(2)}) async-start(bf16[8,64,3072]{2,1,0:T(8,128)(2,1)} %bitcast.119), calls=%async_computation.4 | async-start | bytes 6291456 | tf_op jit(solution)/shard_map/all_to_all | solution.py:123
  265.9 2.5 convert_reduce_fusion
  268.3 34.4 %all-to-all-done.4 = bf16[8,64,3072]{2,1,0:T(8,128)(2,1)} async-done(((bf16[8,64,3072]{2,1,0:T(8,128)(2,1)}), bf16[8,64,3072]{2,1,0:T(8,128)(2,1)}, u32[]{:S(2)}, u32[]{:S(2)}) %all-to-all-start.4) | async-done | bytes 3145760 | tf_op jit(solution)/shard_map/all_to_all | solution.py:123
  302.7 2.5 convert_reduce_fusion.1
  305.3 1.2 fusion.23
  (26 shorter events, 0.1 us)
Async XLA Ops:
  0.0 11.5 %copy-start.5 = (bf16[128,2048]{1,0:T(8,128)(2,1)S(1)}, bf16[128,2048]{1,0:T(8,128)(2,1)}, u32[]{:S(2)}) copy-start(bf16[128,2048]{1,0:T(8,128)(2,1)} %param.14) | copy-start | bytes 1572868
  0.0 11.8 %copy-start.3 = (bf16[128,3072]{1,0:T(8,128)(2,1)S(1)}, bf16[128,3072]{1,0:T(8,128)(2,1)}, u32[]{:S(2)}) copy-start(bf16[128,3072]{1,0:T(8,128)(2,1)} %param.13) | copy-start | bytes 2359300
  2.1 25.5 %all-to-all-start = ((bf16[16,16,2048]{2,1,0:T(8,128)(2,1)}), bf16[16,16,2048]{2,1,0:T(8,128)(2,1)S(1)}, u32[]{:S(2)}, u32[]{:S(2)}) async-start(bf16[16,16,2048]{2,1,0:T(8,128)(2,1)} %broadcast_in_dim.91), calls=%async_computation | async-start | bytes 2097152 | tf_op jit(solution)/shard_map/all_to_all | solution.py:75
  10.5 63.5 %collective-permute-start = (bf16[384,3072]{1,0:T(8,128)(2,1)}, bf16[384,3072]{1,0:T(8,128)(2,1)}, u32[]{:S(2)}, u32[]{:S(2)}) collective-permute-start(bf16[384,3072]{1,0:T(8,128)(2,1)} %param.19), channel_id=1, source_target_pairs={{0,16},{16,0},{1,17},{17,1},{2,18},{18,2},{3,19},{19,3},{4,20},{20... | collective-permute-start | bytes 7077896 | tf_op jit(solution)/shard_map/ppermute | solution.py:89
  28.7 5.2 %slice-start = ((s8[4718592]{0:T(1024)(128)(4,1)}), s8[524288]{0:T(1024)(128)(4,1)S(1)}, s32[]{:S(2)}) async-start(s8[4718592]{0:T(1024)(128)(4,1)} %bitcast.113), calls=%async_computation.7 | async-start | bytes 1048576
  32.3 2.2 slice-start.1
  33.1 1.8 copy-start.4
  80.7 6.5 %copy-start.6 = (bf16[3072]{0:T(1024)(128)(2,1)S(1)}, bf16[3072]{0:T(1024)(128)(2,1)}, u32[]{:S(2)}) copy-start(bf16[3072]{0:T(1024)(128)(2,1)} %param.20) | copy-start | bytes 18436
  80.7 42.5 %all-to-all-start.2 = ((bf16[4,128,3072]{2,1,0:T(8,128)(2,1)}), bf16[4,128,3072]{2,1,0:T(8,128)(2,1)}, u32[]{:S(2)}, u32[]{:S(2)}) async-start(bf16[4,128,3072]{2,1,0:T(8,128)(2,1)} %bitcast.27), calls=%async_computation.2 | async-start | bytes 6291456 | tf_op jit(solution)/shard_map/all_to_all | solution.py:98
  85.9 39.9 %copy-start = (bf16[128,3072]{1,0:T(8,128)(2,1)S(1)}, bf16[128,3072]{1,0:T(8,128)(2,1)}, u32[]{:S(2)}) copy-start(bf16[128,3072]{1,0:T(8,128)(2,1)} %param.12) | copy-start | bytes 2359300
  85.9 57.9 %collective-permute-start.1 = (bf16[3072,512]{1,0:T(8,128)(2,1)}, bf16[3072,512]{1,0:T(8,128)(2,1)}, u32[]{:S(2)}, u32[]{:S(2)}) collective-permute-start(bf16[3072,512]{1,0:T(8,128)(2,1)} %param.21), channel_id=1, source_target_pairs={{0,1},{1,0},{2,3},{3,2},{4,5},{5,4},{6,7},{7,6},{8,9},{9,8},{10,11... | collective-permute-start | bytes 9437192 | tf_op jit(solution)/shard_map/ppermute | solution.py:106
  86.8 60.9 %collective-permute-start.2 = (bf16[3072,512]{1,0:T(8,128)(2,1)}, bf16[3072,512]{1,0:T(8,128)(2,1)}, u32[]{:S(2)}, u32[]{:S(2)}) collective-permute-start(bf16[3072,512]{1,0:T(8,128)(2,1)} %param.22), channel_id=1, source_target_pairs={{0,1},{1,0},{2,3},{3,2},{4,5},{5,4},{6,7},{7,6},{8,9},{9,8},{10,11... | collective-permute-start | bytes 9437192 | tf_op jit(solution)/shard_map/ppermute | solution.py:107
  86.8 93.0 %collective-permute-start.3 = (bf16[512,3072]{1,0:T(8,128)(2,1)}, bf16[512,3072]{1,0:T(8,128)(2,1)}, u32[]{:S(2)}, u32[]{:S(2)}) collective-permute-start(bf16[512,3072]{1,0:T(8,128)(2,1)} %param.23), channel_id=1, source_target_pairs={{0,1},{1,0},{2,3},{3,2},{4,5},{5,4},{6,7},{7,6},{8,9},{9,8},{10,11... | collective-permute-start | bytes 9437192 | tf_op jit(solution)/shard_map/ppermute | solution.py:108
  128.6 43.9 %all-to-all-start.5 = ((bf16[8,64,3072]{2,1,0:T(8,128)(2,1)}), bf16[8,64,3072]{2,1,0:T(8,128)(2,1)}, u32[]{:S(2)}, u32[]{:S(2)}) async-start(bf16[8,64,3072]{2,1,0:T(8,128)(2,1)} %broadcast_in_dim.95), calls=%async_computation.5 | async-start | bytes 6291456 | tf_op jit(solution)/shard_map/all_to_all | solution.py:116
  135.0 4.0 %copy-start.1 = (bf16[3072,512]{1,0:T(8,128)(2,1)S(1)}, bf16[3072,512]{1,0:T(8,128)(2,1)}, u32[]{:S(2)}) copy-start(bf16[3072,512]{1,0:T(8,128)(2,1)} %param.22) | copy-start | bytes 9437188
  138.9 3.0 copy-start.2
  174.7 42.7 %all-to-all-start.3 = ((bf16[8,64,3072]{2,1,0:T(8,128)(2,1)}), bf16[8,64,3072]{2,1,0:T(8,128)(2,1)}, u32[]{:S(2)}, u32[]{:S(2)}) async-start(bf16[8,64,3072]{2,1,0:T(8,128)(2,1)} %broadcast_in_dim.94), calls=%async_computation.3 | async-start | bytes 6291456 | tf_op jit(solution)/shard_map/all_to_all | solution.py:116
  217.3 42.7 %all-to-all-start.6 = ((bf16[8,64,3072]{2,1,0:T(8,128)(2,1)}), bf16[8,64,3072]{2,1,0:T(8,128)(2,1)}, u32[]{:S(2)}, u32[]{:S(2)}) async-start(bf16[8,64,3072]{2,1,0:T(8,128)(2,1)} %bitcast.118), calls=%async_computation.6 | async-start | bytes 6291456 | tf_op jit(solution)/shard_map/all_to_all | solution.py:123
  260.0 42.7 %all-to-all-start.4 = ((bf16[8,64,3072]{2,1,0:T(8,128)(2,1)}), bf16[8,64,3072]{2,1,0:T(8,128)(2,1)}, u32[]{:S(2)}, u32[]{:S(2)}) async-start(bf16[8,64,3072]{2,1,0:T(8,128)(2,1)} %bitcast.119), calls=%async_computation.4 | async-start | bytes 6291456 | tf_op jit(solution)/shard_map/all_to_all | solution.py:123

commit v9 on v8

--- a/solution.py
+++ b/solution.py
@@ -86,14 +86,23 @@
         .reshape(rows_here, HEADS * HEAD)
         .astype(jnp.bfloat16)
     )
-    pair = jnp.concatenate([out_weight, lax.ppermute(out_weight, "x_lo", [(0, 1), (1, 0)])])
+    swap = [(0, 1), (1, 0)]
+    core = lax.axis_index("core")
+    width = out_weight.shape[0] // 2
+    fetched = lax.ppermute(
+        lax.dynamic_slice_in_dim(out_weight, core * width, width, 0), "x_lo", swap
+    )
+    pair = jnp.concatenate([out_weight, fetched, lax.ppermute(fetched, "core", swap)])
     n_z = lax.axis_size("z")
     block = pair.shape[0]
     halves = attended.reshape(rows_here, n_z, 2, out_weight.shape[0])
     halves = jnp.where(lax.axis_index("x_lo") == 0, halves, halves[:, :, ::-1])
-    columns = lax.all_to_all(
-        halves.reshape(rows_here, n_z, block), "z", 1, 0, tiled=False
-    ).reshape(n_z * rows_here, block)
+    other = halves[:, :, 1].reshape(rows_here, n_z, 2, width)
+    other = jnp.where(core == 0, other, other[:, :, ::-1])
+    ordered = jnp.concatenate(
+        [halves[:, :, 0], other.reshape(rows_here, n_z, 2 * width)], axis=-1
+    ).transpose(1, 0, 2)
+    columns = lax.all_to_all(ordered, "z", 0, 0, tiled=False).reshape(n_z * rows_here, block)
     partial = jnp.dot(columns, pair, preferred_element_type=jnp.float32).astype(jnp.bfloat16)
     returned = lax.all_to_all(
         partial.reshape(n_z, rows_here, partial.shape[1]), "z", 0, 0, tiled=False
@@ -102,7 +111,6 @@
     mixed = layer_input.astype(jnp.float32) + projected
     scale = lax.rsqrt(jnp.mean(mixed * mixed, axis=-1, keepdims=True) + 1e-05)
     normed = (mixed * scale * norm_gain.astype(jnp.float32)).astype(jnp.bfloat16)
-    swap = [(0, 1), (1, 0)]
     gate_both = jnp.concatenate([gate_weight, lax.ppermute(gate_weight, "core", swap)], axis=1)
     up_both = jnp.concatenate([up_weight, lax.ppermute(up_weight, "core", swap)], axis=1)
     down_both = jnp.concatenate([down_weight, lax.ppermute(down_weight, "core", swap)], axis=0)

time: 307 us -> 299 us (0.974)
  waiting for transfers between devices: 148 us -> 138 us
    ppermute x1 -> x2, waiting for transfers between devices: 21.7 us -> 15.2 us  [the longest x1 15.2 us: shards(): lax.ppermute(lax.dynamic_slice_in_dim(out_weight, core * width, width, 0)...]
  transfers between devices with their start and end apart: 10 -> 11, of which waited for: 7 -> 7; matrix products, arithmetic and copies ran while one was open for 29% -> 30% of each run, Pallas kernels for 0% -> 0%
where the time goes in v9:
time: 299 us; the launch traced here: 298 us
  waiting for transfers between devices  138 us (46%)
  matrix products  58.5 us (20%)
  starting transfers between devices  38.4 us (13%)
  local copies, waits for them, and re-layouts  32.1 us (11%)
  blocking collectives  16.9 us (6%)
  other arithmetic  13.1 us (4%)
    all_to_all x2, waiting for transfers between devices, shards(): lax.all_to_all(parts.reshape(n_feed, size, parts.shape[1]), feed_axes, 0,...  48.9 us
    all_to_all x1, waiting for transfers between devices, shards(): lax.all_to_all(partial.reshape(n_z, rows_here, partial.shape[1]), 'z', 0,...  34.8 us
    all_to_all x2, waiting for transfers between devices, shards(): lax.all_to_all(jnp.broadcast_to(rows[None], (n_feed,) + rows.shape), feed...  31.9 us
    dot_general x2, matrix products, shards(): jnp.dot(hidden, down_both, preferred_element_type=jnp.float32)  29 us
    dot_general x2, matrix products, shards(): gate = jnp.dot(gathered, gate_both, preferred_element_type=jnp.float32)  17 us
    all_to_all x1, blocking collectives, shards(): lax.all_to_all(ordered, 'z', 0, 0, tiled=False)  16.9 us
    ppermute x1, waiting for transfers between devices, shards(): lax.ppermute(lax.dynamic_slice_in_dim(out_weight, core * width, width, 0)...  15.2 us
    all_to_all x2, starting transfers between devices, shards(): lax.all_to_all(jnp.broadcast_to(rows[None], (n_feed,) + rows.shape), feed...  12.3 us
  transfers between devices with their start and end apart: 11, of which 7 were waited for; matrix products, arithmetic and copies ran while one was open for 30% of the time, Pallas kernels for 0%

profile of v9, /device:TPU:1, one launch (start us, length us, event | category | flops | bytes accessed | tf_op | source)
XLA Modules:
  0.0 298.4 jit_solution(12332911981455707496)
XLA Ops:
  0.0 2.0 broadcast_in_dim.91
  2.0 8.4 %all-to-all-start = ((bf16[16,16,2048]{2,1,0:T(8,128)(2,1)}), bf16[16,16,2048]{2,1,0:T(8,128)(2,1)S(1)}, u32[]{:S(2)}, u32[]{:S(2)}) async-start(bf16[16,16,2048]{2,1,0:T(8,128)(2,1)} %broadcast_in_dim.91), calls=%async_computation | async-start | bytes 2097152 | tf_op jit(solution)/shard_map/all_to_all | solution.py:75
  10.5 2.4 constant_dynamic-slice_fusion
  12.9 0.3 collective-permute-start
  13.9 0.3 copy.33
  14.2 0.4 copy.34
  14.6 1.5 copy.32
  16.1 1.0 pad_maximum_fusion
  17.2 0.1 fusion.41
  17.3 0.2 fusion.40
  17.5 3.0 %fusion.9 = (f32[8,3,128]{2,1,0:T(4,128)S(1)}, f32[8,384,128,3]{2,1,3,0:T(8,128)}) fusion(pred[128,384]{0,1:T(8,128)(4,1)S(1)} %fusion.40, bf16[384,8,128,1]{0,2,3,1:T(8,128)(2,1)S(1)} %bitcast.121, bf16[128,8,3,128]{0,3,2,1:T(8,128)(2,1)S(1)} %bitcast.116), kind=kOutput, calls=%fused_computation.14 | convolution fusion | flops 305525760 | bytes 6352896 | tf_op jit(solution)/shard_map/skgh,nkh->kgsn/dot_general | solution.py:20
  20.5 7.0 %all-to-all-done = bf16[16,16,2048]{2,1,0:T(8,128)(2,1)S(1)} async-done(((bf16[16,16,2048]{2,1,0:T(8,128)(2,1)}), bf16[16,16,2048]{2,1,0:T(8,128)(2,1)S(1)}, u32[]{:S(2)}, u32[]{:S(2)}) %all-to-all-start) | async-done | bytes 1048608 | tf_op jit(solution)/shard_map/all_to_all | solution.py:75
  27.6 0.1 fusion.58
  27.6 0.2 copy.38
  27.8 0.2 copy.41
  28.1 0.7 fusion.12
  28.8 0.8 fusion.20
  29.6 0.8 fusion.22
  30.4 0.1 slice-done.1
  30.5 1.2 fusion.10
  31.7 1.6 fusion.27
  33.3 0.1 copy.44
  33.4 0.2 reverse_select_fusion
  33.5 15.2 %collective-permute-done = bf16[192,3072]{1,0:T(8,128)(2,1)} collective-permute-done((bf16[192,3072]{1,0:T(8,128)(2,1)}, bf16[192,3072]{1,0:T(8,128)(2,1)}, u32[]{:S(2)}, u32[]{:S(2)}) %collective-permute-start) | collective-permute-done | bytes 1179680 | tf_op jit(solution)/shard_map/ppermute | solution.py:92
  48.7 0.6 collective-permute-start.1
  49.3 0.1 slice_bitcast_fusion
  49.3 0.1 reverse_select_fusion.1
  49.4 0.1 maximum_bitcast_fusion
  49.5 16.9 %all_to_all.35 = bf16[4,128,768]{1,2,0:T(8,128)(2,1)S(1)} all-to-all(bf16[4,128,768]{1,2,0:T(8,128)(2,1)S(1)} %maximum_bitcast_fusion), channel_id=1, replica_groups=mesh['z'=4,'x_lo'=2,'x_hi'=2,'y'=4,'core'=2] {'z'}, dimensions={0} | all-to-all | bytes 1572864 | tf_op jit(solution)/shard_map/all_to_all | solution.py:105
  66.4 0.3 copy.45
  66.7 6.4 %fusion.6 = bf16[512,3072]{1,0:T(8,128)(2,1)} fusion(bf16[512,768]{1,0:T(8,128)(2,1)S(1)} %bitcast.126, bf16[192,3072]{1,0:T(8,128)(2,1)S(1)} %collective-permute-done.1, bf16[192,3072]{1,0:T(8,128)(2,1)} %collective-permute-done, bf16[384,3072]{1,0:T(8,128)(2,1)} %param.19), kind=kOutput, calls=%fused_computation.11 | convolution fusion | flops 2431647744 | bytes 8650752 | tf_op jit(solution)/shard_map/dot_general | solution.py:106
  73.1 4.8 %all-to-all-start.2 = ((bf16[4,128,3072]{2,1,0:T(8,128)(2,1)}), bf16[4,128,3072]{2,1,0:T(8,128)(2,1)}, u32[]{:S(2)}, u32[]{:S(2)}) async-start(bf16[4,128,3072]{2,1,0:T(8,128)(2,1)} %bitcast.28), calls=%async_computation.2 | async-start | bytes 6291456 | tf_op jit(solution)/shard_map/all_to_all | solution.py:107
  77.9 1.2 collective-permute-start.2
  79.1 0.1 collective-permute-start.3
  79.2 0.4 collective-permute-start.4
  79.6 34.8 %all-to-all-done.2 = bf16[4,128,3072]{2,1,0:T(8,128)(2,1)} async-done(((bf16[4,128,3072]{2,1,0:T(8,128)(2,1)}), bf16[4,128,3072]{2,1,0:T(8,128)(2,1)}, u32[]{:S(2)}, u32[]{:S(2)}) %all-to-all-start.2) | async-done | bytes 3145760 | tf_op jit(solution)/shard_map/all_to_all | solution.py:107
  114.5 2.6 convert_reduce_fusion.2
  117.1 0.3 multiply_reduce_fusion
  117.4 0.3 multiply_convert_fusion.2
  117.7 0.1 fusion.59
  117.7 2.1 broadcast_in_dim.95
  119.8 7.1 %all-to-all-start.5 = ((bf16[8,64,3072]{2,1,0:T(8,128)(2,1)}), bf16[8,64,3072]{2,1,0:T(8,128)(2,1)}, u32[]{:S(2)}, u32[]{:S(2)}) async-start(bf16[8,64,3072]{2,1,0:T(8,128)(2,1)} %broadcast_in_dim.95), calls=%async_computation.5 | async-start | bytes 6291456 | tf_op jit(solution)/shard_map/all_to_all | solution.py:124
  127.0 3.9 %constant_dynamic-update-slice_fusion.1 = bf16[3072,1024]{1,0:T(8,128)(2,1)} fusion(bf16[3072,512]{1,0:T(8,128)(2,1)} %param.21), kind=kLoop, calls=%fused_computation.73 | loop fusion | bytes 6291456
  130.9 1.9 constant_dynamic-update-slice_fusion.3
  132.8 1.1 copy-done.2
  133.9 1.8 constant_dynamic-update-slice_fusion.5
  135.8 3.9 %constant_dynamic-update-slice_fusion = bf16[3072,1024]{1,0:T(8,128)(2,1)} fusion(bf16[3072,1024]{1,0:T(8,128)(2,1)} %constant_dynamic-update-slice_fusion.1, bf16[3072,512]{1,0:T(8,128)(2,1)} %collective-permute-done.2), kind=kLoop, calls=%fused_computation.72 | loop fusion | bytes 6291456 | tf_op jit(solution)/shard_map/concatenate | solution.py:114
  139.6 3.9 %constant_dynamic-update-slice_fusion.2 = bf16[3072,1024]{1,0:T(8,128)(2,1)} fusion(bf16[3072,1024]{1,0:T(8,128)(2,1)} %constant_dynamic-update-slice_fusion.3, bf16[3072,512]{1,0:T(8,128)(2,1)} %collective-permute-done.3), kind=kLoop, calls=%fused_computation.74 | loop fusion | bytes 6291456 | tf_op jit(solution)/shard_map/concatenate | solution.py:115
  143.5 21.0 %all-to-all-done.5 = bf16[8,64,3072]{2,1,0:T(8,128)(2,1)} async-done(((bf16[8,64,3072]{2,1,0:T(8,128)(2,1)}), bf16[8,64,3072]{2,1,0:T(8,128)(2,1)}, u32[]{:S(2)}, u32[]{:S(2)}) %all-to-all-start.5) | async-done | bytes 3145760 | tf_op jit(solution)/shard_map/all_to_all | solution.py:124
  164.5 2.1 broadcast_in_dim.94
  166.6 5.2 %all-to-all-start.3 = ((bf16[8,64,3072]{2,1,0:T(8,128)(2,1)}), bf16[8,64,3072]{2,1,0:T(8,128)(2,1)}, u32[]{:S(2)}, u32[]{:S(2)}) async-start(bf16[8,64,3072]{2,1,0:T(8,128)(2,1)} %broadcast_in_dim.94), calls=%async_computation.3 | async-start | bytes 6291456 | tf_op jit(solution)/shard_map/all_to_all | solution.py:124
  171.8 3.8 %constant_dynamic-update-slice_fusion.4 = bf16[1024,3072]{1,0:T(8,128)(2,1)} fusion(bf16[1024,3072]{1,0:T(8,128)(2,1)} %constant_dynamic-update-slice_fusion.5, bf16[512,3072]{1,0:T(8,128)(2,1)} %collective-permute-done.4), kind=kLoop, calls=%fused_computation.76 | loop fusion | bytes 6291456 | tf_op jit(solution)/shard_map/concatenate | solution.py:116
  175.5 8.4 %fusion.65 = f32[512,1024]{1,0:T(8,128)} fusion(bf16[512,3072]{1,0:T(8,128)(2,1)} %bitcast.31, bf16[3072,1024]{1,0:T(8,128)(2,1)} %constant_dynamic-update-slice_fusion), kind=kOutput, calls=%fused_computation.103 | convolution fusion | flops 3221225472 | bytes 11534336 | tf_op jit(solution)/shard_map/dot_general | solution.py:127
  184.0 14.5 %convolution_convert_fusion = bf16[512,3072]{1,0:T(8,128)(2,1)} fusion(bf16[1024,3072]{1,0:T(8,128)(2,1)} %constant_dynamic-update-slice_fusion.4, f32[512,1024]{1,0:T(8,128)} %fusion.65, bf16[512,3072]{1,0:T(8,128)(2,1)} %bitcast.31, bf16[3072,1024]{1,0:T(8,128)(2,1)} %constant_dynamic-update-slice_fusion.2), kind=kOutput, calls=%fused_computation.12 | convolution fusion | flops 6447169536 | bytes 20971520 | tf_op jit(solution)/shard_map/dot_general | solution.py:130
  198.5 10.8 %all-to-all-done.3 = bf16[8,64,3072]{2,1,0:T(8,128)(2,1)} async-done(((bf16[8,64,3072]{2,1,0:T(8,128)(2,1)}), bf16[8,64,3072]{2,1,0:T(8,128)(2,1)}, u32[]{:S(2)}, u32[]{:S(2)}) %all-to-all-start.3) | async-done | bytes 3145760 | tf_op jit(solution)/shard_map/all_to_all | solution.py:124
  209.3 5.2 %all-to-all-start.6 = ((bf16[8,64,3072]{2,1,0:T(8,128)(2,1)}), bf16[8,64,3072]{2,1,0:T(8,128)(2,1)}, u32[]{:S(2)}, u32[]{:S(2)}) async-start(bf16[8,64,3072]{2,1,0:T(8,128)(2,1)} %bitcast.119), calls=%async_computation.6 | async-start | bytes 6291456 | tf_op jit(solution)/shard_map/all_to_all | solution.py:131
  214.5 8.6 %fusion.64 = f32[512,1024]{1,0:T(8,128)} fusion(bf16[512,3072]{1,0:T(8,128)(2,1)} %bitcast.29, bf16[3072,1024]{1,0:T(8,128)(2,1)} %constant_dynamic-update-slice_fusion), kind=kOutput, calls=%fused_computation.102 | convolution fusion | flops 3221225472 | bytes 11534336 | tf_op jit(solution)/shard_map/dot_general | solution.py:127
  223.1 14.5 %convolution_convert_fusion.1 = bf16[512,3072]{1,0:T(8,128)(2,1)} fusion(bf16[1024,3072]{1,0:T(8,128)(2,1)} %constant_dynamic-update-slice_fusion.4, f32[512,1024]{1,0:T(8,128)} %fusion.64, bf16[512,3072]{1,0:T(8,128)(2,1)} %bitcast.29, bf16[3072,1024]{1,0:T(8,128)(2,1)} %constant_dynamic-update-slice_fusion.2), kind=kOutput, calls=%fused_computation.13 | convolution fusion | flops 6447169536 | bytes 20971520 | tf_op jit(solution)/shard_map/dot_general | solution.py:130
  237.5 14.5 %all-to-all-done.6 = bf16[8,64,3072]{2,1,0:T(8,128)(2,1)} async-done(((bf16[8,64,3072]{2,1,0:T(8,128)(2,1)}), bf16[8,64,3072]{2,1,0:T(8,128)(2,1)}, u32[]{:S(2)}, u32[]{:S(2)}) %all-to-all-start.6) | async-done | bytes 3145760 | tf_op jit(solution)/shard_map/all_to_all | solution.py:131
  252.0 5.2 %all-to-all-start.4 = ((bf16[8,64,3072]{2,1,0:T(8,128)(2,1)}), bf16[8,64,3072]{2,1,0:T(8,128)(2,1)}, u32[]{:S(2)}, u32[]{:S(2)}) async-start(bf16[8,64,3072]{2,1,0:T(8,128)(2,1)} %bitcast.120), calls=%async_computation.4 | async-start | bytes 6291456 | tf_op jit(solution)/shard_map/all_to_all | solution.py:131
  257.8 2.5 convert_reduce_fusion
  260.3 34.4 %all-to-all-done.4 = bf16[8,64,3072]{2,1,0:T(8,128)(2,1)} async-done(((bf16[8,64,3072]{2,1,0:T(8,128)(2,1)}), bf16[8,64,3072]{2,1,0:T(8,128)(2,1)}, u32[]{:S(2)}, u32[]{:S(2)}) %all-to-all-start.4) | async-done | bytes 3145760 | tf_op jit(solution)/shard_map/all_to_all | solution.py:131
  294.7 2.5 convert_reduce_fusion.1
  297.2 1.2 fusion.25
  (33 shorter events, 0.1 us)
Async XLA Ops:
  0.0 13.9 %copy-start.5 = (bf16[128,2048]{1,0:T(8,128)(2,1)S(1)}, bf16[128,2048]{1,0:T(8,128)(2,1)}, u32[]{:S(2)}) copy-start(bf16[128,2048]{1,0:T(8,128)(2,1)} %param.14) | copy-start | bytes 1572868
  0.0 14.2 %copy-start.3 = (bf16[128,3072]{1,0:T(8,128)(2,1)S(1)}, bf16[128,3072]{1,0:T(8,128)(2,1)}, u32[]{:S(2)}) copy-start(bf16[128,3072]{1,0:T(8,128)(2,1)} %param.13) | copy-start | bytes 2359300
  2.0 25.5 %all-to-all-start = ((bf16[16,16,2048]{2,1,0:T(8,128)(2,1)}), bf16[16,16,2048]{2,1,0:T(8,128)(2,1)S(1)}, u32[]{:S(2)}, u32[]{:S(2)}) async-start(bf16[16,16,2048]{2,1,0:T(8,128)(2,1)} %broadcast_in_dim.91), calls=%async_computation | async-start | bytes 2097152 | tf_op jit(solution)/shard_map/all_to_all | solution.py:75
  12.9 35.8 %collective-permute-start = (bf16[192,3072]{1,0:T(8,128)(2,1)}, bf16[192,3072]{1,0:T(8,128)(2,1)}, u32[]{:S(2)}, u32[]{:S(2)}) collective-permute-start(bf16[192,3072]{1,0:T(8,128)(2,1)} %constant_dynamic-slice_fusion), channel_id=1, source_target_pairs={{0,16},{16,0},{1,17},{17,1},{2,18},{18,2},{3,19},{19,3},{4,20},{20... | collective-permute-start | bytes 3538952 | tf_op jit(solution)/shard_map/ppermute | solution.py:92
  28.1 2.4 slice-start
  28.7 1.8 slice-start.1
  30.4 1.3 copy-start.4
  48.7 18.0 %collective-permute-start.1 = (bf16[192,3072]{1,0:T(8,128)(2,1)}, bf16[192,3072]{1,0:T(8,128)(2,1)S(1)}, u32[]{:S(2)}, u32[]{:S(2)}) collective-permute-start(bf16[192,3072]{1,0:T(8,128)(2,1)} %collective-permute-done), channel_id=1, source_target_pairs={{0,1},{1,0},{2,3},{3,2},{4,5},{5,4},{6,7},{7,6},{8,9},{9,8},{10,11... | collective-permute-start | bytes 3538952 | tf_op jit(solution)/shard_map/ppermute | solution.py:95
  73.1 6.5 %copy-start.6 = (bf16[3072]{0:T(1024)(128)(2,1)S(1)}, bf16[3072]{0:T(1024)(128)(2,1)}, u32[]{:S(2)}) copy-start(bf16[3072]{0:T(1024)(128)(2,1)} %param.20) | copy-start | bytes 18436
  73.1 41.4 %all-to-all-start.2 = ((bf16[4,128,3072]{2,1,0:T(8,128)(2,1)}), bf16[4,128,3072]{2,1,0:T(8,128)(2,1)}, u32[]{:S(2)}, u32[]{:S(2)}) async-start(bf16[4,128,3072]{2,1,0:T(8,128)(2,1)} %bitcast.28), calls=%async_computation.2 | async-start | bytes 6291456 | tf_op jit(solution)/shard_map/all_to_all | solution.py:107
  77.9 39.2 %copy-start = (bf16[128,3072]{1,0:T(8,128)(2,1)S(1)}, bf16[128,3072]{1,0:T(8,128)(2,1)}, u32[]{:S(2)}) copy-start(bf16[128,3072]{1,0:T(8,128)(2,1)} %param.12) | copy-start | bytes 2359300
  77.9 57.9 %collective-permute-start.2 = (bf16[3072,512]{1,0:T(8,128)(2,1)}, bf16[3072,512]{1,0:T(8,128)(2,1)}, u32[]{:S(2)}, u32[]{:S(2)}) collective-permute-start(bf16[3072,512]{1,0:T(8,128)(2,1)} %param.21), channel_id=1, source_target_pairs={{0,1},{1,0},{2,3},{3,2},{4,5},{5,4},{6,7},{7,6},{8,9},{9,8},{10,11... | collective-permute-start | bytes 9437192 | tf_op jit(solution)/shard_map/ppermute | solution.py:114
  79.1 60.5 %collective-permute-start.3 = (bf16[3072,512]{1,0:T(8,128)(2,1)}, bf16[3072,512]{1,0:T(8,128)(2,1)}, u32[]{:S(2)}, u32[]{:S(2)}) collective-permute-start(bf16[3072,512]{1,0:T(8,128)(2,1)} %param.22), channel_id=1, source_target_pairs={{0,1},{1,0},{2,3},{3,2},{4,5},{5,4},{6,7},{7,6},{8,9},{9,8},{10,11... | collective-permute-start | bytes 9437192 | tf_op jit(solution)/shard_map/ppermute | solution.py:115
  79.2 92.6 %collective-permute-start.4 = (bf16[512,3072]{1,0:T(8,128)(2,1)}, bf16[512,3072]{1,0:T(8,128)(2,1)}, u32[]{:S(2)}, u32[]{:S(2)}) collective-permute-start(bf16[512,3072]{1,0:T(8,128)(2,1)} %param.23), channel_id=1, source_target_pairs={{0,1},{1,0},{2,3},{3,2},{4,5},{5,4},{6,7},{7,6},{8,9},{9,8},{10,11... | collective-permute-start | bytes 9437192 | tf_op jit(solution)/shard_map/ppermute | solution.py:116
  119.8 44.7 %all-to-all-start.5 = ((bf16[8,64,3072]{2,1,0:T(8,128)(2,1)}), bf16[8,64,3072]{2,1,0:T(8,128)(2,1)}, u32[]{:S(2)}, u32[]{:S(2)}) async-start(bf16[8,64,3072]{2,1,0:T(8,128)(2,1)} %broadcast_in_dim.95), calls=%async_computation.5 | async-start | bytes 6291456 | tf_op jit(solution)/shard_map/all_to_all | solution.py:124
  127.0 4.0 %copy-start.1 = (bf16[3072,512]{1,0:T(8,128)(2,1)S(1)}, bf16[3072,512]{1,0:T(8,128)(2,1)}, u32[]{:S(2)}) copy-start(bf16[3072,512]{1,0:T(8,128)(2,1)} %param.22) | copy-start | bytes 9437188
  130.9 3.0 %copy-start.2 = (bf16[512,3072]{1,0:T(8,128)(2,1)S(1)}, bf16[512,3072]{1,0:T(8,128)(2,1)}, u32[]{:S(2)}) copy-start(bf16[512,3072]{1,0:T(8,128)(2,1)} %param.23) | copy-start | bytes 9437188
  166.6 42.7 %all-to-all-start.3 = ((bf16[8,64,3072]{2,1,0:T(8,128)(2,1)}), bf16[8,64,3072]{2,1,0:T(8,128)(2,1)}, u32[]{:S(2)}, u32[]{:S(2)}) async-start(bf16[8,64,3072]{2,1,0:T(8,128)(2,1)} %broadcast_in_dim.94), calls=%async_computation.3 | async-start | bytes 6291456 | tf_op jit(solution)/shard_map/all_to_all | solution.py:124
  209.3 42.7 %all-to-all-start.6 = ((bf16[8,64,3072]{2,1,0:T(8,128)(2,1)}), bf16[8,64,3072]{2,1,0:T(8,128)(2,1)}, u32[]{:S(2)}, u32[]{:S(2)}) async-start(bf16[8,64,3072]{2,1,0:T(8,128)(2,1)} %bitcast.119), calls=%async_computation.6 | async-start | bytes 6291456 | tf_op jit(solution)/shard_map/all_to_all | solution.py:131
  252.0 42.7 %all-to-all-start.4 = ((bf16[8,64,3072]{2,1,0:T(8,128)(2,1)}), bf16[8,64,3072]{2,1,0:T(8,128)(2,1)}, u32[]{:S(2)}, u32[]{:S(2)}) async-start(bf16[8,64,3072]{2,1,0:T(8,128)(2,1)} %bitcast.120), calls=%async_computation.4 | async-start | bytes 6291456 | tf_op jit(solution)/shard_map/all_to_all | solution.py:131

commit v10 on v9

--- a/solution.py
+++ b/solution.py
@@ -102,7 +102,18 @@
     ordered = jnp.concatenate(
         [halves[:, :, 0], other.reshape(rows_here, n_z, 2 * width)], axis=-1
     ).transpose(1, 0, 2)
-    columns = lax.all_to_all(ordered, "z", 0, 0, tiled=False).reshape(n_z * rows_here, block)
+    z = lax.axis_index("z")
+    received = [jnp.take(ordered, z, axis=0)]
+    for shift in range(1, n_z):
+        received.append(
+            lax.ppermute(
+                jnp.take(ordered, (z + shift) % n_z, axis=0),
+                "z",
+                [(i, (i + shift) % n_z) for i in range(n_z)],
+            )
+        )
+    sources = (z - jnp.arange(n_z, dtype=jnp.int32)) % n_z
+    columns = jnp.take(jnp.stack(received), sources, axis=0).reshape(n_z * rows_here, block)
     partial = jnp.dot(columns, pair, preferred_element_type=jnp.float32).astype(jnp.bfloat16)
     returned = lax.all_to_all(
         partial.reshape(n_z, rows_here, partial.shape[1]), "z", 0, 0, tiled=False

time: 299 us -> 300 us (level)
  blocking collectives: 16.9 us -> 0 us
  waiting for transfers between devices: 138 us -> 149 us
  starting transfers between devices: 38.4 us -> 42.6 us
    all_to_all x1 -> x0, blocking collectives: 16.9 us -> none  [shards(): lax.all_to_all(ordered, 'z', 0, 0, tiled=False)]
    ppermute x0 -> x3, waiting for transfers between devices: none -> 11.2 us  [shards(): lax.ppermute(jnp.take(ordered, (z + shift) % n_z, axis=0), 'z', [(i, (i +...]
    ppermute x0 -> x3, starting transfers between devices: none -> 4.53 us  [shards(): lax.ppermute(jnp.take(ordered, (z + shift) % n_z, axis=0), 'z', [(i, (i +...]
  transfers between devices with their start and end apart: 11 -> 14, of which waited for: 7 -> 9; matrix products, arithmetic and copies ran while one was open for 30% -> 31% of each run, Pallas kernels for 0% -> 0%
where the time goes in v10:
time: 300 us; the launch traced here: 299 us
  waiting for transfers between devices  149 us (50%)
  matrix products  58.5 us (20%)
  starting transfers between devices  42.6 us (14%)
  local copies, waits for them, and re-layouts  33.4 us (11%)
  other arithmetic  13.5 us (4%)
    all_to_all x2, waiting for transfers between devices, shards(): lax.all_to_all(parts.reshape(n_feed, size, parts.shape[1]), feed_axes, 0,...  48.9 us
    all_to_all x1, waiting for transfers between devices, shards(): lax.all_to_all(partial.reshape(n_z, rows_here, partial.shape[1]), 'z', 0,...  35.5 us
    all_to_all x2, waiting for transfers between devices, shards(): lax.all_to_all(jnp.broadcast_to(rows[None], (n_feed,) + rows.shape), feed...  31.8 us
    dot_general x2, matrix products, shards(): jnp.dot(hidden, down_both, preferred_element_type=jnp.float32)  29 us
    dot_general x2, matrix products, shards(): gate = jnp.dot(gathered, gate_both, preferred_element_type=jnp.float32)  17 us
    ppermute x1, waiting for transfers between devices, shards(): lax.ppermute(lax.dynamic_slice_in_dim(out_weight, core * width, width, 0)...  14.9 us
    all_to_all x2, starting transfers between devices, shards(): lax.all_to_all(jnp.broadcast_to(rows[None], (n_feed,) + rows.shape), feed...  12.3 us
    ppermute x3, waiting for transfers between devices, shards(): lax.ppermute(jnp.take(ordered, (z + shift) % n_z, axis=0), 'z', [(i, (i +...  11.2 us
  transfers between devices with their start and end apart: 14, of which 9 were waited for; matrix products, arithmetic and copies ran while one was open for 31% of the time, Pallas kernels for 0%

profile of v10, /device:TPU:1, one launch (start us, length us, event | category | flops | bytes accessed | tf_op | source)
XLA Modules:
  0.0 298.9 jit_solution(7021692861142562275)
XLA Ops:
  0.0 2.1 broadcast_in_dim.117
  2.1 8.4 %all-to-all-start = ((bf16[16,16,2048]{2,1,0:T(8,128)(2,1)}), bf16[16,16,2048]{2,1,0:T(8,128)(2,1)S(1)}, u32[]{:S(2)}, u32[]{:S(2)}) async-start(bf16[16,16,2048]{2,1,0:T(8,128)(2,1)} %broadcast_in_dim.117), calls=%async_computation | async-start | bytes 2097152 | tf_op jit(solution)/shard_map/all_to_all | solution.py:75
  10.5 2.4 constant_dynamic-slice_fusion
  12.9 0.3 collective-permute-start.3
  14.0 0.3 copy.44
  14.3 0.4 copy.45
  14.6 1.5 copy.43
  16.2 1.0 pad_maximum_fusion
  17.2 0.1 fusion.41
  17.3 0.2 fusion.40
  17.5 3.0 %fusion.9 = (f32[8,3,128]{2,1,0:T(4,128)S(1)}, f32[8,384,128,3]{2,1,3,0:T(8,128)}) fusion(pred[128,384]{0,1:T(8,128)(4,1)S(1)} %fusion.40, bf16[384,8,128,1]{0,2,3,1:T(8,128)(2,1)S(1)} %bitcast.136, bf16[128,8,3,128]{0,3,2,1:T(8,128)(2,1)S(1)} %bitcast.131), kind=kOutput, calls=%fused_computation.15 | convolution fusion | flops 305525760 | bytes 6352896 | tf_op jit(solution)/shard_map/skgh,nkh->kgsn/dot_general | solution.py:20
  20.6 7.0 %all-to-all-done = bf16[16,16,2048]{2,1,0:T(8,128)(2,1)S(1)} async-done(((bf16[16,16,2048]{2,1,0:T(8,128)(2,1)}), bf16[16,16,2048]{2,1,0:T(8,128)(2,1)S(1)}, u32[]{:S(2)}, u32[]{:S(2)}) %all-to-all-start) | async-done | bytes 1048608 | tf_op jit(solution)/shard_map/all_to_all | solution.py:75
  27.7 0.2 copy.49
  27.9 0.2 copy.52
  28.1 0.7 fusion.12
  28.8 0.8 fusion.20
  29.6 0.8 fusion.22
  30.5 1.2 fusion.10
  31.8 1.6 fusion.27
  33.3 0.4 copy.55
  33.7 0.1 reverse_select_fusion
  33.8 14.9 %collective-permute-done.3 = bf16[192,3072]{1,0:T(8,128)(2,1)} collective-permute-done((bf16[192,3072]{1,0:T(8,128)(2,1)}, bf16[192,3072]{1,0:T(8,128)(2,1)}, u32[]{:S(2)}, u32[]{:S(2)}) %collective-permute-start.3) | collective-permute-done | bytes 1179680 | tf_op jit(solution)/shard_map/ppermute | solution.py:92
  48.7 0.6 collective-permute-start.4
  49.4 0.2 copy.56
  49.7 0.2 copy.57
  50.1 3.8 %collective-permute-start.2 = (bf16[128,768]{1,0:T(8,128)(2,1)S(1)}, bf16[128,768]{1,0:T(8,128)(2,1)S(1)}, u32[]{:S(2)}, u32[]{:S(2)}) collective-permute-start(bf16[128,768]{1,0:T(8,128)(2,1)S(1)} %get-tuple-element.26), channel_id=1, source_target_pairs={{0,96},{32,0},{64,32},{96,64},{1,97},{33,1},{65,33},{97,65},{2,98}... | collective-permute-start | bytes 589832 | tf_op jit(solution)/shard_map/ppermute | solution.py:109
  53.9 0.7 collective-permute-start
  54.7 7.7 %collective-permute-done.2 = bf16[128,768]{1,0:T(8,128)(2,1)S(1)} collective-permute-done((bf16[128,768]{1,0:T(8,128)(2,1)S(1)}, bf16[128,768]{1,0:T(8,128)(2,1)S(1)}, u32[]{:S(2)}, u32[]{:S(2)}) %collective-permute-start.2) | collective-permute-done | bytes 196640 | tf_op jit(solution)/shard_map/ppermute | solution.py:109
  62.4 3.5 %collective-permute-done = bf16[128,768]{1,0:T(8,128)(2,1)S(1)} collective-permute-done((bf16[128,768]{1,0:T(8,128)(2,1)S(1)}, bf16[128,768]{1,0:T(8,128)(2,1)S(1)}, u32[]{:S(2)}, u32[]{:S(2)}) %collective-permute-start) | collective-permute-done | bytes 196640 | tf_op jit(solution)/shard_map/ppermute | solution.py:109
  65.9 0.1 pad_maximum_fusion.1
  66.0 0.6 gather_fusion
  66.6 0.2 bitcast_select_fusion.2
  66.8 6.4 %fusion.6 = bf16[512,3072]{1,0:T(8,128)(2,1)} fusion(bf16[512,768]{1,0:T(8,128)(2,1)S(1)} %bitcast_select_fusion.2, bf16[192,3072]{1,0:T(8,128)(2,1)S(1)} %collective-permute-done.4, bf16[192,3072]{1,0:T(8,128)(2,1)} %collective-permute-done.3, bf16[384,3072]{1,0:T(8,128)(2,1)} %param.21), kind=kOutput, calls=%fused_computation.12 | convolution fusion | flops 2431647744 | bytes 8650752 | tf_op jit(solution)/shard_map/dot_general | solution.py:117
  73.2 4.8 %all-to-all-start.1 = ((bf16[4,128,3072]{2,1,0:T(8,128)(2,1)}), bf16[4,128,3072]{2,1,0:T(8,128)(2,1)}, u32[]{:S(2)}, u32[]{:S(2)}) async-start(bf16[4,128,3072]{2,1,0:T(8,128)(2,1)} %bitcast.37), calls=%async_computation.1 | async-start | bytes 6291456 | tf_op jit(solution)/shard_map/all_to_all | solution.py:118
  78.0 0.9 collective-permute-start.5
  79.0 0.4 collective-permute-start.7
  79.4 35.5 %all-to-all-done.1 = bf16[4,128,3072]{2,1,0:T(8,128)(2,1)} async-done(((bf16[4,128,3072]{2,1,0:T(8,128)(2,1)}), bf16[4,128,3072]{2,1,0:T(8,128)(2,1)}, u32[]{:S(2)}, u32[]{:S(2)}) %all-to-all-start.1) | async-done | bytes 3145760 | tf_op jit(solution)/shard_map/all_to_all | solution.py:118
  114.9 2.6 convert_reduce_fusion.2
  117.5 0.3 multiply_reduce_fusion
  117.8 0.3 multiply_convert_fusion.2
  118.2 2.1 broadcast_in_dim.122
  120.3 7.1 %all-to-all-start.4 = ((bf16[8,64,3072]{2,1,0:T(8,128)(2,1)}), bf16[8,64,3072]{2,1,0:T(8,128)(2,1)}, u32[]{:S(2)}, u32[]{:S(2)}) async-start(bf16[8,64,3072]{2,1,0:T(8,128)(2,1)} %broadcast_in_dim.122), calls=%async_computation.4 | async-start | bytes 6291456 | tf_op jit(solution)/shard_map/all_to_all | solution.py:135
  127.5 4.0 %constant_dynamic-update-slice_fusion.1 = bf16[3072,1024]{1,0:T(8,128)(2,1)} fusion(bf16[3072,512]{1,0:T(8,128)(2,1)} %param.23), kind=kLoop, calls=%fused_computation.80 | loop fusion | bytes 6291456
  131.4 1.9 constant_dynamic-update-slice_fusion.3
  133.3 1.1 copy-done.2
  134.4 1.9 constant_dynamic-update-slice_fusion.5
  136.3 3.9 %constant_dynamic-update-slice_fusion = bf16[3072,1024]{1,0:T(8,128)(2,1)} fusion(bf16[3072,1024]{1,0:T(8,128)(2,1)} %constant_dynamic-update-slice_fusion.1, bf16[3072,512]{1,0:T(8,128)(2,1)} %collective-permute-done.5), kind=kLoop, calls=%fused_computation.79 | loop fusion | bytes 6291456 | tf_op jit(solution)/shard_map/concatenate | solution.py:125
  140.2 3.8 %constant_dynamic-update-slice_fusion.2 = bf16[3072,1024]{1,0:T(8,128)(2,1)} fusion(bf16[3072,1024]{1,0:T(8,128)(2,1)} %constant_dynamic-update-slice_fusion.3, bf16[3072,512]{1,0:T(8,128)(2,1)} %collective-permute-done.6), kind=kLoop, calls=%fused_computation.81 | loop fusion | bytes 6291456 | tf_op jit(solution)/shard_map/concatenate | solution.py:126
  144.0 21.0 %all-to-all-done.4 = bf16[8,64,3072]{2,1,0:T(8,128)(2,1)} async-done(((bf16[8,64,3072]{2,1,0:T(8,128)(2,1)}), bf16[8,64,3072]{2,1,0:T(8,128)(2,1)}, u32[]{:S(2)}, u32[]{:S(2)}) %all-to-all-start.4) | async-done | bytes 3145760 | tf_op jit(solution)/shard_map/all_to_all | solution.py:135
  165.0 2.1 broadcast_in_dim.121
  167.1 5.2 %all-to-all-start.2 = ((bf16[8,64,3072]{2,1,0:T(8,128)(2,1)}), bf16[8,64,3072]{2,1,0:T(8,128)(2,1)}, u32[]{:S(2)}, u32[]{:S(2)}) async-start(bf16[8,64,3072]{2,1,0:T(8,128)(2,1)} %broadcast_in_dim.121), calls=%async_computation.2 | async-start | bytes 6291456 | tf_op jit(solution)/shard_map/all_to_all | solution.py:135
  172.3 3.8 %constant_dynamic-update-slice_fusion.4 = bf16[1024,3072]{1,0:T(8,128)(2,1)} fusion(bf16[1024,3072]{1,0:T(8,128)(2,1)} %constant_dynamic-update-slice_fusion.5, bf16[512,3072]{1,0:T(8,128)(2,1)} %collective-permute-done.7), kind=kLoop, calls=%fused_computation.83 | loop fusion | bytes 6291456 | tf_op jit(solution)/shard_map/concatenate | solution.py:127
  176.1 8.4 %fusion.68 = f32[512,1024]{1,0:T(8,128)} fusion(bf16[512,3072]{1,0:T(8,128)(2,1)} %bitcast.40, bf16[3072,1024]{1,0:T(8,128)(2,1)} %constant_dynamic-update-slice_fusion), kind=kOutput, calls=%fused_computation.124 | convolution fusion | flops 3221225472 | bytes 11534336 | tf_op jit(solution)/shard_map/dot_general | solution.py:138
  184.5 14.5 %convolution_convert_fusion = bf16[512,3072]{1,0:T(8,128)(2,1)} fusion(bf16[1024,3072]{1,0:T(8,128)(2,1)} %constant_dynamic-update-slice_fusion.4, f32[512,1024]{1,0:T(8,128)} %fusion.68, bf16[512,3072]{1,0:T(8,128)(2,1)} %bitcast.40, bf16[3072,1024]{1,0:T(8,128)(2,1)} %constant_dynamic-update-slice_fusion.2), kind=kOutput, calls=%fused_computation.13 | convolution fusion | flops 6447169536 | bytes 20971520 | tf_op jit(solution)/shard_map/dot_general | solution.py:141
  199.0 10.8 %all-to-all-done.2 = bf16[8,64,3072]{2,1,0:T(8,128)(2,1)} async-done(((bf16[8,64,3072]{2,1,0:T(8,128)(2,1)}), bf16[8,64,3072]{2,1,0:T(8,128)(2,1)}, u32[]{:S(2)}, u32[]{:S(2)}) %all-to-all-start.2) | async-done | bytes 3145760 | tf_op jit(solution)/shard_map/all_to_all | solution.py:135
  209.8 5.2 %all-to-all-start.5 = ((bf16[8,64,3072]{2,1,0:T(8,128)(2,1)}), bf16[8,64,3072]{2,1,0:T(8,128)(2,1)}, u32[]{:S(2)}, u32[]{:S(2)}) async-start(bf16[8,64,3072]{2,1,0:T(8,128)(2,1)} %bitcast.134), calls=%async_computation.5 | async-start | bytes 6291456 | tf_op jit(solution)/shard_map/all_to_all | solution.py:142
  215.0 8.6 %fusion.67 = f32[512,1024]{1,0:T(8,128)} fusion(bf16[512,3072]{1,0:T(8,128)(2,1)} %bitcast.38, bf16[3072,1024]{1,0:T(8,128)(2,1)} %constant_dynamic-update-slice_fusion), kind=kOutput, calls=%fused_computation.123 | convolution fusion | flops 3221225472 | bytes 11534336 | tf_op jit(solution)/shard_map/dot_general | solution.py:138
  223.6 14.5 %convolution_convert_fusion.1 = bf16[512,3072]{1,0:T(8,128)(2,1)} fusion(bf16[1024,3072]{1,0:T(8,128)(2,1)} %constant_dynamic-update-slice_fusion.4, f32[512,1024]{1,0:T(8,128)} %fusion.67, bf16[512,3072]{1,0:T(8,128)(2,1)} %bitcast.38, bf16[3072,1024]{1,0:T(8,128)(2,1)} %constant_dynamic-update-slice_fusion.2), kind=kOutput, calls=%fused_computation.14 | convolution fusion | flops 6447169536 | bytes 20971520 | tf_op jit(solution)/shard_map/dot_general | solution.py:141
  238.0 14.5 %all-to-all-done.5 = bf16[8,64,3072]{2,1,0:T(8,128)(2,1)} async-done(((bf16[8,64,3072]{2,1,0:T(8,128)(2,1)}), bf16[8,64,3072]{2,1,0:T(8,128)(2,1)}, u32[]{:S(2)}, u32[]{:S(2)}) %all-to-all-start.5) | async-done | bytes 3145760 | tf_op jit(solution)/shard_map/all_to_all | solution.py:142
  252.5 5.2 %all-to-all-start.3 = ((bf16[8,64,3072]{2,1,0:T(8,128)(2,1)}), bf16[8,64,3072]{2,1,0:T(8,128)(2,1)}, u32[]{:S(2)}, u32[]{:S(2)}) async-start(bf16[8,64,3072]{2,1,0:T(8,128)(2,1)} %bitcast.135), calls=%async_computation.3 | async-start | bytes 6291456 | tf_op jit(solution)/shard_map/all_to_all | solution.py:142
  258.3 2.5 convert_reduce_fusion
  260.8 34.4 %all-to-all-done.3 = bf16[8,64,3072]{2,1,0:T(8,128)(2,1)} async-done(((bf16[8,64,3072]{2,1,0:T(8,128)(2,1)}), bf16[8,64,3072]{2,1,0:T(8,128)(2,1)}, u32[]{:S(2)}, u32[]{:S(2)}) %all-to-all-start.3) | async-done | bytes 3145760 | tf_op jit(solution)/shard_map/all_to_all | solution.py:142
  295.2 2.5 convert_reduce_fusion.1
  297.7 1.2 fusion.25
  (47 shorter events, 0.9 us)
Async XLA Ops:
  0.0 14.0 %copy-start.5 = (bf16[128,2048]{1,0:T(8,128)(2,1)S(1)}, bf16[128,2048]{1,0:T(8,128)(2,1)}, u32[]{:S(2)}) copy-start(bf16[128,2048]{1,0:T(8,128)(2,1)} %param.16) | copy-start | bytes 1572868
  0.0 14.3 %copy-start.3 = (bf16[128,3072]{1,0:T(8,128)(2,1)S(1)}, bf16[128,3072]{1,0:T(8,128)(2,1)}, u32[]{:S(2)}) copy-start(bf16[128,3072]{1,0:T(8,128)(2,1)} %param.15) | copy-start | bytes 2359300
  2.1 25.5 %all-to-all-start = ((bf16[16,16,2048]{2,1,0:T(8,128)(2,1)}), bf16[16,16,2048]{2,1,0:T(8,128)(2,1)S(1)}, u32[]{:S(2)}, u32[]{:S(2)}) async-start(bf16[16,16,2048]{2,1,0:T(8,128)(2,1)} %broadcast_in_dim.117), calls=%async_computation | async-start | bytes 2097152 | tf_op jit(solution)/shard_map/all_to_all | solution.py:75
  12.9 35.8 %collective-permute-start.3 = (bf16[192,3072]{1,0:T(8,128)(2,1)}, bf16[192,3072]{1,0:T(8,128)(2,1)}, u32[]{:S(2)}, u32[]{:S(2)}) collective-permute-start(bf16[192,3072]{1,0:T(8,128)(2,1)} %constant_dynamic-slice_fusion), channel_id=1, source_target_pairs={{0,16},{16,0},{1,17},{17,1},{2,18},{18,2},{3,19},{19,3},{4,20},{20... | collective-permute-start | bytes 3538952 | tf_op jit(solution)/shard_map/ppermute | solution.py:92
  28.1 2.4 slice-start
  28.8 1.8 slice-start.1
  30.4 1.3 copy-start.4
  48.7 18.1 %collective-permute-start.4 = (bf16[192,3072]{1,0:T(8,128)(2,1)}, bf16[192,3072]{1,0:T(8,128)(2,1)S(1)}, u32[]{:S(2)}, u32[]{:S(2)}) collective-permute-start(bf16[192,3072]{1,0:T(8,128)(2,1)} %collective-permute-done.3), channel_id=1, source_target_pairs={{0,1},{1,0},{2,3},{3,2},{4,5},{5,4},{6,7},{7,6},{8,9},{9,8},{10,11... | collective-permute-start | bytes 3538952 | tf_op jit(solution)/shard_map/ppermute | solution.py:95
  50.1 12.3 %collective-permute-start.2 = (bf16[128,768]{1,0:T(8,128)(2,1)S(1)}, bf16[128,768]{1,0:T(8,128)(2,1)S(1)}, u32[]{:S(2)}, u32[]{:S(2)}) collective-permute-start(bf16[128,768]{1,0:T(8,128)(2,1)S(1)} %get-tuple-element.26), channel_id=1, source_target_pairs={{0,96},{32,0},{64,32},{96,64},{1,97},{33,1},{65,33},{97,65},{2,98}... | collective-permute-start | bytes 589832 | tf_op jit(solution)/shard_map/ppermute | solution.py:109
  53.9 8.5 %collective-permute-start.1 = (bf16[128,768]{1,0:T(8,128)(2,1)S(1)}, bf16[128,768]{1,0:T(8,128)(2,1)S(1)}, u32[]{:S(2)}, u32[]{:S(2)}) collective-permute-start(bf16[128,768]{1,0:T(8,128)(2,1)S(1)} %get-tuple-element.27), channel_id=1, source_target_pairs={{0,64},{32,96},{64,0},{96,32},{1,65},{33,97},{65,1},{97,33},{2,66}... | collective-permute-start | bytes 589832 | tf_op jit(solution)/shard_map/ppermute | solution.py:109
  53.9 12.0 %collective-permute-start = (bf16[128,768]{1,0:T(8,128)(2,1)S(1)}, bf16[128,768]{1,0:T(8,128)(2,1)S(1)}, u32[]{:S(2)}, u32[]{:S(2)}) collective-permute-start(bf16[128,768]{1,0:T(8,128)(2,1)S(1)} %get-tuple-element.28), channel_id=1, source_target_pairs={{0,32},{32,64},{64,96},{96,0},{1,33},{33,65},{65,97},{97,1},{2,34}... | collective-permute-start | bytes 589832 | tf_op jit(solution)/shard_map/ppermute | solution.py:109
  73.2 6.2 %copy-start.6 = (bf16[3072]{0:T(1024)(128)(2,1)S(1)}, bf16[3072]{0:T(1024)(128)(2,1)}, u32[]{:S(2)}) copy-start(bf16[3072]{0:T(1024)(128)(2,1)} %param.22) | copy-start | bytes 18436
  73.2 41.7 %all-to-all-start.1 = ((bf16[4,128,3072]{2,1,0:T(8,128)(2,1)}), bf16[4,128,3072]{2,1,0:T(8,128)(2,1)}, u32[]{:S(2)}, u32[]{:S(2)}) async-start(bf16[4,128,3072]{2,1,0:T(8,128)(2,1)} %bitcast.37), calls=%async_computation.1 | async-start | bytes 6291456 | tf_op jit(solution)/shard_map/all_to_all | solution.py:118
  78.0 39.5 %copy-start = (bf16[128,3072]{1,0:T(8,128)(2,1)S(1)}, bf16[128,3072]{1,0:T(8,128)(2,1)}, u32[]{:S(2)}) copy-start(bf16[128,3072]{1,0:T(8,128)(2,1)} %param.14) | copy-start | bytes 2359300
  78.0 58.3 %collective-permute-start.5 = (bf16[3072,512]{1,0:T(8,128)(2,1)}, bf16[3072,512]{1,0:T(8,128)(2,1)}, u32[]{:S(2)}, u32[]{:S(2)}) collective-permute-start(bf16[3072,512]{1,0:T(8,128)(2,1)} %param.23), channel_id=1, source_target_pairs={{0,1},{1,0},{2,3},{3,2},{4,5},{5,4},{6,7},{7,6},{8,9},{9,8},{10,11... | collective-permute-start | bytes 9437192 | tf_op jit(solution)/shard_map/ppermute | solution.py:125
  78.9 61.3 %collective-permute-start.6 = (bf16[3072,512]{1,0:T(8,128)(2,1)}, bf16[3072,512]{1,0:T(8,128)(2,1)}, u32[]{:S(2)}, u32[]{:S(2)}) collective-permute-start(bf16[3072,512]{1,0:T(8,128)(2,1)} %param.24), channel_id=1, source_target_pairs={{0,1},{1,0},{2,3},{3,2},{4,5},{5,4},{6,7},{7,6},{8,9},{9,8},{10,11... | collective-permute-start | bytes 9437192 | tf_op jit(solution)/shard_map/ppermute | solution.py:126
  79.0 93.3 %collective-permute-start.7 = (bf16[512,3072]{1,0:T(8,128)(2,1)}, bf16[512,3072]{1,0:T(8,128)(2,1)}, u32[]{:S(2)}, u32[]{:S(2)}) collective-permute-start(bf16[512,3072]{1,0:T(8,128)(2,1)} %param.25), channel_id=1, source_target_pairs={{0,1},{1,0},{2,3},{3,2},{4,5},{5,4},{6,7},{7,6},{8,9},{9,8},{10,11... | collective-permute-start | bytes 9437192 | tf_op jit(solution)/shard_map/ppermute | solution.py:127
  120.3 44.7 %all-to-all-start.4 = ((bf16[8,64,3072]{2,1,0:T(8,128)(2,1)}), bf16[8,64,3072]{2,1,0:T(8,128)(2,1)}, u32[]{:S(2)}, u32[]{:S(2)}) async-start(bf16[8,64,3072]{2,1,0:T(8,128)(2,1)} %broadcast_in_dim.122), calls=%async_computation.4 | async-start | bytes 6291456 | tf_op jit(solution)/shard_map/all_to_all | solution.py:135
  127.4 4.0 %copy-start.1 = (bf16[3072,512]{1,0:T(8,128)(2,1)S(1)}, bf16[3072,512]{1,0:T(8,128)(2,1)}, u32[]{:S(2)}) copy-start(bf16[3072,512]{1,0:T(8,128)(2,1)} %param.24) | copy-start | bytes 9437188
  131.4 3.0 %copy-start.2 = (bf16[512,3072]{1,0:T(8,128)(2,1)S(1)}, bf16[512,3072]{1,0:T(8,128)(2,1)}, u32[]{:S(2)}) copy-start(bf16[512,3072]{1,0:T(8,128)(2,1)} %param.25) | copy-start | bytes 9437188
  167.1 42.7 %all-to-all-start.2 = ((bf16[8,64,3072]{2,1,0:T(8,128)(2,1)}), bf16[8,64,3072]{2,1,0:T(8,128)(2,1)}, u32[]{:S(2)}, u32[]{:S(2)}) async-start(bf16[8,64,3072]{2,1,0:T(8,128)(2,1)} %broadcast_in_dim.121), calls=%async_computation.2 | async-start | bytes 6291456 | tf_op jit(solution)/shard_map/all_to_all | solution.py:135
  209.8 42.7 %all-to-all-start.5 = ((bf16[8,64,3072]{2,1,0:T(8,128)(2,1)}), bf16[8,64,3072]{2,1,0:T(8,128)(2,1)}, u32[]{:S(2)}, u32[]{:S(2)}) async-start(bf16[8,64,3072]{2,1,0:T(8,128)(2,1)} %bitcast.134), calls=%async_computation.5 | async-start | bytes 6291456 | tf_op jit(solution)/shard_map/all_to_all | solution.py:142
  252.5 42.7 %all-to-all-start.3 = ((bf16[8,64,3072]{2,1,0:T(8,128)(2,1)}), bf16[8,64,3072]{2,1,0:T(8,128)(2,1)}, u32[]{:S(2)}, u32[]{:S(2)}) async-start(bf16[8,64,3072]{2,1,0:T(8,128)(2,1)} %bitcast.135), calls=%async_computation.3 | async-start | bytes 6291456 | tf_op jit(solution)/shard_map/all_to_all | solution.py:142

commit v11 on v9

--- a/solution.py
+++ b/solution.py
@@ -111,9 +111,10 @@
     mixed = layer_input.astype(jnp.float32) + projected
     scale = lax.rsqrt(jnp.mean(mixed * mixed, axis=-1, keepdims=True) + 1e-05)
     normed = (mixed * scale * norm_gain.astype(jnp.float32)).astype(jnp.bfloat16)
-    gate_both = jnp.concatenate([gate_weight, lax.ppermute(gate_weight, "core", swap)], axis=1)
-    up_both = jnp.concatenate([up_weight, lax.ppermute(up_weight, "core", swap)], axis=1)
-    down_both = jnp.concatenate([down_weight, lax.ppermute(down_weight, "core", swap)], axis=0)
+    weights = [
+        (gate_weight, up_weight, down_weight),
+        tuple(lax.ppermute(w, "core", swap) for w in (gate_weight, up_weight, down_weight)),
+    ]
     feed_axes = ("x_hi", "y")
     n_feed = lax.axis_size(feed_axes)
     chunks = 2
@@ -124,10 +125,13 @@
         gathered = lax.all_to_all(
             jnp.broadcast_to(rows[None], (n_feed,) + rows.shape), feed_axes, 0, 0, tiled=False
         ).reshape(n_feed * size, rows.shape[1])
-        gate = jnp.dot(gathered, gate_both, preferred_element_type=jnp.float32)
-        upper = jnp.dot(gathered, up_both, preferred_element_type=jnp.float32)
-        hidden = (jax.nn.silu(gate) * upper).astype(jnp.bfloat16)
-        parts = jnp.dot(hidden, down_both, preferred_element_type=jnp.float32).astype(jnp.bfloat16)
+        parts = 0.0
+        for gate_w, up_w, down_w in weights:
+            gate = jnp.dot(gathered, gate_w, preferred_element_type=jnp.float32)
+            upper = jnp.dot(gathered, up_w, preferred_element_type=jnp.float32)
+            hidden = (jax.nn.silu(gate) * upper).astype(jnp.bfloat16)
+            parts = parts + jnp.dot(hidden, down_w, preferred_element_type=jnp.float32)
+        parts = parts.astype(jnp.bfloat16)
         parts = lax.all_to_all(
             parts.reshape(n_feed, size, parts.shape[1]), feed_axes, 0, 0, tiled=False
         )

time: 299 us -> 299 us (level)
  local copies, waits for them, and re-layouts: 32.1 us -> 12.7 us
  matrix products: 58.5 us -> 74.9 us
    dot_general x4 -> x8, matrix products: 46 us -> 62.5 us  [the longest x4 41.9 us: shards(): parts = parts + jnp.dot(hidden, down_w, preferred_element_type=jnp.float32)]
    concatenate x3 -> x0, local copies, waits for them, and re-layouts: 11.5 us -> none  [the longest x1 3.86 us: shards(): jnp.concatenate([gate_weight, lax.ppermute(gate_weight, 'core', swap)], a...]
    all_to_all x2, waiting for transfers between devices: 31.9 us -> 41.1 us  [shards(): lax.all_to_all(jnp.broadcast_to(rows[None], (n_feed,) + rows.shape), feed...]
    all_to_all x2, waiting for transfers between devices: 48.9 us -> 40.6 us  [shards(): lax.all_to_all(parts.reshape(n_feed, size, parts.shape[1]), feed_axes, 0,...]
    unnamed x24 -> x15, local copies, waits for them, and re-layouts: 11 us -> 4.42 us
  transfers between devices with their start and end apart: 11 -> 11, of which waited for: 7 -> 7; matrix products, arithmetic and copies ran while one was open for 30% -> 28% of each run, Pallas kernels for 0% -> 0%
where the time goes in v11:
time: 299 us; the launch traced here: 298 us
  waiting for transfers between devices  139 us (46%)
  matrix products  74.9 us (25%)
  starting transfers between devices  39.7 us (13%)
  blocking collectives  16.9 us (6%)
  other arithmetic  13.2 us (4%)
  local copies, waits for them, and re-layouts  12.7 us (4%)
    dot_general x4, matrix products, shards(): parts = parts + jnp.dot(hidden, down_w, preferred_element_type=jnp.float32)  41.9 us
    all_to_all x2, waiting for transfers between devices, shards(): lax.all_to_all(jnp.broadcast_to(rows[None], (n_feed,) + rows.shape), feed...  41.1 us
    all_to_all x2, waiting for transfers between devices, shards(): lax.all_to_all(parts.reshape(n_feed, size, parts.shape[1]), feed_axes, 0,...  40.6 us
    all_to_all x1, waiting for transfers between devices, shards(): lax.all_to_all(partial.reshape(n_z, rows_here, partial.shape[1]), 'z', 0,...  36.4 us
    dot_general x4, matrix products, shards(): gate = jnp.dot(gathered, gate_w, preferred_element_type=jnp.float32)  20.5 us
    all_to_all x1, blocking collectives, shards(): lax.all_to_all(ordered, 'z', 0, 0, tiled=False)  16.9 us
    ppermute x1, waiting for transfers between devices, shards(): lax.ppermute(lax.dynamic_slice_in_dim(out_weight, core * width, width, 0)...  15.2 us
    all_to_all x2, starting transfers between devices, shards(): lax.all_to_all(jnp.broadcast_to(rows[None], (n_feed,) + rows.shape), feed...  12.3 us
  transfers between devices with their start and end apart: 11, of which 7 were waited for; matrix products, arithmetic and copies ran while one was open for 28% of the time, Pallas kernels for 0%

profile of v11, /device:TPU:1, one launch (start us, length us, event | category | flops | bytes accessed | tf_op | source)
XLA Modules:
  0.0 298.4 jit_solution(16856651100731996263)
XLA Ops:
  0.0 2.1 broadcast_in_dim.91
  2.1 8.4 %all-to-all-start = ((bf16[16,16,2048]{2,1,0:T(8,128)(2,1)}), bf16[16,16,2048]{2,1,0:T(8,128)(2,1)S(1)}, u32[]{:S(2)}, u32[]{:S(2)}) async-start(bf16[16,16,2048]{2,1,0:T(8,128)(2,1)} %broadcast_in_dim.91), calls=%async_computation | async-start | bytes 2097152 | tf_op jit(solution)/shard_map/all_to_all | solution.py:75
  10.5 1.1 constant_dynamic-slice_fusion
  11.7 0.3 collective-permute-start
  12.7 1.5 copy.32
  14.2 1.3 copy.33
  15.5 1.5 copy.34
  17.0 1.0 pad_maximum_fusion
  18.1 0.1 fusion.47
  18.2 0.2 fusion.46
  18.4 3.0 %fusion.9 = (f32[8,3,128]{2,1,0:T(4,128)S(1)}, f32[8,384,128,3]{2,1,3,0:T(8,128)}) fusion(pred[128,384]{0,1:T(8,128)(4,1)S(1)} %fusion.46, bf16[384,8,128,1]{0,2,3,1:T(8,128)(2,1)S(1)} %bitcast.131, bf16[128,8,3,128]{0,3,2,1:T(8,128)(2,1)S(1)} %bitcast.126), kind=kOutput, calls=%fused_computation.14 | convolution fusion | flops 305525760 | bytes 6352896 | tf_op jit(solution)/shard_map/skgh,nkh->kgsn/dot_general | solution.py:20
  21.4 6.2 %all-to-all-done = bf16[16,16,2048]{2,1,0:T(8,128)(2,1)S(1)} async-done(((bf16[16,16,2048]{2,1,0:T(8,128)(2,1)}), bf16[16,16,2048]{2,1,0:T(8,128)(2,1)S(1)}, u32[]{:S(2)}, u32[]{:S(2)}) %all-to-all-start) | async-done | bytes 1048608 | tf_op jit(solution)/shard_map/all_to_all | solution.py:75
  27.6 0.1 fusion.66
  27.7 0.2 copy.38
  27.9 0.2 copy.41
  28.1 0.0 slice-start
  28.1 0.7 fusion.12
  28.8 0.8 fusion.20
  29.6 0.8 fusion.22
  30.4 0.0 copy-start.1
  30.5 0.1 slice-done.1
  30.6 1.2 fusion.10
  31.8 1.6 fusion.27
  33.3 0.1 copy.44
  33.4 0.2 reverse_select_fusion
  33.6 15.2 %collective-permute-done = bf16[192,3072]{1,0:T(8,128)(2,1)} collective-permute-done((bf16[192,3072]{1,0:T(8,128)(2,1)}, bf16[192,3072]{1,0:T(8,128)(2,1)}, u32[]{:S(2)}, u32[]{:S(2)}) %collective-permute-start) | collective-permute-done | bytes 1179680 | tf_op jit(solution)/shard_map/ppermute | solution.py:92
  48.7 0.6 collective-permute-start.1
  49.3 0.1 slice_bitcast_fusion
  49.4 0.1 reverse_select_fusion.1
  49.5 0.1 maximum_bitcast_fusion
  49.5 16.9 %all_to_all.35 = bf16[4,128,768]{1,2,0:T(8,128)(2,1)S(1)} all-to-all(bf16[4,128,768]{1,2,0:T(8,128)(2,1)S(1)} %maximum_bitcast_fusion), channel_id=1, replica_groups=mesh['z'=4,'x_lo'=2,'x_hi'=2,'y'=4,'core'=2] {'z'}, dimensions={0} | all-to-all | bytes 1572864 | tf_op jit(solution)/shard_map/all_to_all | solution.py:105
  66.5 0.3 copy.45
  66.8 6.3 %fusion.6 = bf16[512,3072]{1,0:T(8,128)(2,1)} fusion(bf16[512,768]{1,0:T(8,128)(2,1)S(1)} %bitcast.136, bf16[192,3072]{1,0:T(8,128)(2,1)S(1)} %collective-permute-done.1, bf16[192,3072]{1,0:T(8,128)(2,1)} %collective-permute-done, bf16[384,3072]{1,0:T(8,128)(2,1)} %param.19), kind=kOutput, calls=%fused_computation.13 | convolution fusion | flops 2431647744 | bytes 8650752 | tf_op jit(solution)/shard_map/dot_general | solution.py:106
  73.0 5.0 %all-to-all-start.2 = ((bf16[4,128,3072]{2,1,0:T(8,128)(2,1)}), bf16[4,128,3072]{2,1,0:T(8,128)(2,1)}, u32[]{:S(2)}, u32[]{:S(2)}) async-start(bf16[4,128,3072]{2,1,0:T(8,128)(2,1)} %bitcast.28), calls=%async_computation.2 | async-start | bytes 6291456 | tf_op jit(solution)/shard_map/all_to_all | solution.py:107
  78.0 0.0 copy-start
  78.0 36.4 %all-to-all-done.2 = bf16[4,128,3072]{2,1,0:T(8,128)(2,1)} async-done(((bf16[4,128,3072]{2,1,0:T(8,128)(2,1)}), bf16[4,128,3072]{2,1,0:T(8,128)(2,1)}, u32[]{:S(2)}, u32[]{:S(2)}) %all-to-all-start.2) | async-done | bytes 3145760 | tf_op jit(solution)/shard_map/all_to_all | solution.py:107
  114.4 2.6 convert_reduce_fusion.2
  117.0 0.3 multiply_reduce_fusion
  117.3 0.3 multiply_convert_fusion
  117.6 0.1 fusion.67
  117.7 2.0 broadcast_in_dim.94
  119.7 7.1 %all-to-all-start.3 = ((bf16[8,64,3072]{2,1,0:T(8,128)(2,1)}), bf16[8,64,3072]{2,1,0:T(8,128)(2,1)}, u32[]{:S(2)}, u32[]{:S(2)}) async-start(bf16[8,64,3072]{2,1,0:T(8,128)(2,1)} %broadcast_in_dim.94), calls=%async_computation.3 | async-start | bytes 6291456 | tf_op jit(solution)/shard_map/all_to_all | solution.py:125
  126.8 2.3 collective-permute-start.2
  129.1 0.1 collective-permute-start.3
  129.2 0.4 collective-permute-start.4
  129.6 34.8 %all-to-all-done.3 = bf16[8,64,3072]{2,1,0:T(8,128)(2,1)} async-done(((bf16[8,64,3072]{2,1,0:T(8,128)(2,1)}), bf16[8,64,3072]{2,1,0:T(8,128)(2,1)}, u32[]{:S(2)}, u32[]{:S(2)}) %all-to-all-start.3) | async-done | bytes 3145760 | tf_op jit(solution)/shard_map/all_to_all | solution.py:125
  164.4 2.1 broadcast_in_dim.95
  166.5 5.2 %all-to-all-start.5 = ((bf16[8,64,3072]{2,1,0:T(8,128)(2,1)}), bf16[8,64,3072]{2,1,0:T(8,128)(2,1)}, u32[]{:S(2)}, u32[]{:S(2)}) async-start(bf16[8,64,3072]{2,1,0:T(8,128)(2,1)} %broadcast_in_dim.95), calls=%async_computation.5 | async-start | bytes 6291456 | tf_op jit(solution)/shard_map/all_to_all | solution.py:125
  171.6 5.6 %fusion.72 = f32[512,512]{1,0:T(8,128)} fusion(bf16[512,3072]{1,0:T(8,128)(2,1)} %bitcast.29, bf16[3072,512]{1,0:T(8,128)(2,1)} %param.21), kind=kOutput, calls=%fused_computation.106 | convolution fusion | flops 1610612736 | bytes 7340032 | tf_op jit(solution)/shard_map/dot_general | solution.py:130
  177.2 4.6 %fusion.73 = f32[512,512]{1,0:T(8,128)S(1)} fusion(bf16[512,3072]{1,0:T(8,128)(2,1)} %bitcast.29, bf16[3072,512]{1,0:T(8,128)(2,1)} %collective-permute-done.2), kind=kOutput, calls=%fused_computation.107 | convolution fusion | flops 1610612736 | bytes 7340032 | tf_op jit(solution)/shard_map/dot_general | solution.py:130
  181.9 10.2 %fusion.39 = f32[512,3072]{1,0:T(8,128)} fusion(bf16[512,3072]{1,0:T(8,128)(2,1)} %param.23, bf16[512,3072]{1,0:T(8,128)(2,1)} %bitcast.29, bf16[3072,512]{1,0:T(8,128)(2,1)} %param.22, f32[512,512]{1,0:T(8,128)} %fusion.72), kind=kOutput, calls=%fused_computation.55 | convolution fusion | flops 3222798336 | bytes 16777216 | tf_op jit(solution)/shard_map/dot_general | solution.py:133
  192.1 10.7 %add_convert_fusion.1 = bf16[512,3072]{1,0:T(8,128)(2,1)} fusion(f32[512,3072]{1,0:T(8,128)} %fusion.39, bf16[512,3072]{1,0:T(8,128)(2,1)} %collective-permute-done.4, f32[512,512]{1,0:T(8,128)S(1)} %fusion.73, bf16[512,3072]{1,0:T(8,128)(2,1)} %bitcast.29, bf16[3072,512]{1,0:T(8,128)(2,1)} %collective-permute-done.3), kind=kOutput, calls=%fused_computation.3 | convolution fusion | flops 3225944064 | bytes 19922944 | tf_op jit(solution)/shard_map/dot_general | solution.py:133
  202.9 6.3 %all-to-all-done.5 = bf16[8,64,3072]{2,1,0:T(8,128)(2,1)} async-done(((bf16[8,64,3072]{2,1,0:T(8,128)(2,1)}), bf16[8,64,3072]{2,1,0:T(8,128)(2,1)}, u32[]{:S(2)}, u32[]{:S(2)}) %all-to-all-start.5) | async-done | bytes 3145760 | tf_op jit(solution)/shard_map/all_to_all | solution.py:125
  209.2 5.2 %all-to-all-start.4 = ((bf16[8,64,3072]{2,1,0:T(8,128)(2,1)}), bf16[8,64,3072]{2,1,0:T(8,128)(2,1)}, u32[]{:S(2)}, u32[]{:S(2)}) async-start(bf16[8,64,3072]{2,1,0:T(8,128)(2,1)} %bitcast.129), calls=%async_computation.4 | async-start | bytes 6291456 | tf_op jit(solution)/shard_map/all_to_all | solution.py:135
  214.3 5.7 %fusion.74 = f32[512,512]{1,0:T(8,128)} fusion(bf16[512,3072]{1,0:T(8,128)(2,1)} %bitcast.31, bf16[3072,512]{1,0:T(8,128)(2,1)} %param.21), kind=kOutput, calls=%fused_computation.108 | convolution fusion | flops 1610612736 | bytes 7340032 | tf_op jit(solution)/shard_map/dot_general | solution.py:130
  220.0 4.6 %fusion.75 = f32[512,512]{1,0:T(8,128)S(1)} fusion(bf16[512,3072]{1,0:T(8,128)(2,1)} %bitcast.31, bf16[3072,512]{1,0:T(8,128)(2,1)} %collective-permute-done.2), kind=kOutput, calls=%fused_computation.109 | convolution fusion | flops 1610612736 | bytes 7340032 | tf_op jit(solution)/shard_map/dot_general | solution.py:130
  224.6 10.2 %fusion.38 = f32[512,3072]{1,0:T(8,128)} fusion(bf16[512,3072]{1,0:T(8,128)(2,1)} %param.23, bf16[512,3072]{1,0:T(8,128)(2,1)} %bitcast.31, bf16[3072,512]{1,0:T(8,128)(2,1)} %param.22, f32[512,512]{1,0:T(8,128)} %fusion.74), kind=kOutput, calls=%fused_computation.54 | convolution fusion | flops 3222798336 | bytes 16777216 | tf_op jit(solution)/shard_map/dot_general | solution.py:133
  234.9 10.7 %add_convert_fusion = bf16[512,3072]{1,0:T(8,128)(2,1)} fusion(f32[512,3072]{1,0:T(8,128)} %fusion.38, bf16[512,3072]{1,0:T(8,128)(2,1)} %collective-permute-done.4, f32[512,512]{1,0:T(8,128)S(1)} %fusion.75, bf16[512,3072]{1,0:T(8,128)(2,1)} %bitcast.31, bf16[3072,512]{1,0:T(8,128)(2,1)} %collective-permute-done.3), kind=kOutput, calls=%fused_computation.1 | convolution fusion | flops 3225944064 | bytes 19922944 | tf_op jit(solution)/shard_map/dot_general | solution.py:133
  245.6 6.2 %all-to-all-done.4 = bf16[8,64,3072]{2,1,0:T(8,128)(2,1)} async-done(((bf16[8,64,3072]{2,1,0:T(8,128)(2,1)}), bf16[8,64,3072]{2,1,0:T(8,128)(2,1)}, u32[]{:S(2)}, u32[]{:S(2)}) %all-to-all-start.4) | async-done | bytes 3145760 | tf_op jit(solution)/shard_map/all_to_all | solution.py:135
  251.9 5.2 %all-to-all-start.6 = ((bf16[8,64,3072]{2,1,0:T(8,128)(2,1)}), bf16[8,64,3072]{2,1,0:T(8,128)(2,1)}, u32[]{:S(2)}, u32[]{:S(2)}) async-start(bf16[8,64,3072]{2,1,0:T(8,128)(2,1)} %bitcast.130), calls=%async_computation.6 | async-start | bytes 6291456 | tf_op jit(solution)/shard_map/all_to_all | solution.py:135
  257.7 2.5 convert_reduce_fusion.1
  260.2 34.4 %all-to-all-done.6 = bf16[8,64,3072]{2,1,0:T(8,128)(2,1)} async-done(((bf16[8,64,3072]{2,1,0:T(8,128)(2,1)}), bf16[8,64,3072]{2,1,0:T(8,128)(2,1)}, u32[]{:S(2)}, u32[]{:S(2)}) %all-to-all-start.6) | async-done | bytes 3145760 | tf_op jit(solution)/shard_map/all_to_all | solution.py:135
  294.6 2.5 convert_reduce_fusion
  297.1 1.3 fusion.25
  (25 shorter events, 0.1 us)
Async XLA Ops:
  0.0 10.5 %copy-start.2 = (bf16[384,3072]{1,0:T(8,128)(2,1)S(1)}, bf16[384,3072]{1,0:T(8,128)(2,1)}, u32[]{:S(2)}) copy-start(bf16[384,3072]{1,0:T(8,128)(2,1)} %param.19) | copy-start | bytes 7077892
  2.1 25.5 %all-to-all-start = ((bf16[16,16,2048]{2,1,0:T(8,128)(2,1)}), bf16[16,16,2048]{2,1,0:T(8,128)(2,1)S(1)}, u32[]{:S(2)}, u32[]{:S(2)}) async-start(bf16[16,16,2048]{2,1,0:T(8,128)(2,1)} %broadcast_in_dim.91), calls=%async_computation | async-start | bytes 2097152 | tf_op jit(solution)/shard_map/all_to_all | solution.py:75
  11.7 37.1 %collective-permute-start = (bf16[192,3072]{1,0:T(8,128)(2,1)}, bf16[192,3072]{1,0:T(8,128)(2,1)}, u32[]{:S(2)}, u32[]{:S(2)}) collective-permute-start(bf16[192,3072]{1,0:T(8,128)(2,1)} %constant_dynamic-slice_fusion), channel_id=1, source_target_pairs={{0,16},{16,0},{1,17},{17,1},{2,18},{18,2},{3,19},{19,3},{4,20},{20... | collective-permute-start | bytes 3538952 | tf_op jit(solution)/shard_map/ppermute | solution.py:92
  28.1 2.4 slice-start
  28.8 1.8 slice-start.1
  30.4 1.3 copy-start.1
  48.7 18.0 %collective-permute-start.1 = (bf16[192,3072]{1,0:T(8,128)(2,1)}, bf16[192,3072]{1,0:T(8,128)(2,1)S(1)}, u32[]{:S(2)}, u32[]{:S(2)}) collective-permute-start(bf16[192,3072]{1,0:T(8,128)(2,1)} %collective-permute-done), channel_id=1, source_target_pairs={{0,1},{1,0},{2,3},{3,2},{4,5},{5,4},{6,7},{7,6},{8,9},{9,8},{10,11... | collective-permute-start | bytes 3538952 | tf_op jit(solution)/shard_map/ppermute | solution.py:95
  73.0 5.0 %copy-start.3 = (bf16[3072]{0:T(1024)(128)(2,1)S(1)}, bf16[3072]{0:T(1024)(128)(2,1)}, u32[]{:S(2)}) copy-start(bf16[3072]{0:T(1024)(128)(2,1)} %param.20) | copy-start | bytes 18436
  73.0 41.4 %all-to-all-start.2 = ((bf16[4,128,3072]{2,1,0:T(8,128)(2,1)}), bf16[4,128,3072]{2,1,0:T(8,128)(2,1)}, u32[]{:S(2)}, u32[]{:S(2)}) async-start(bf16[4,128,3072]{2,1,0:T(8,128)(2,1)} %bitcast.28), calls=%async_computation.2 | async-start | bytes 6291456 | tf_op jit(solution)/shard_map/all_to_all | solution.py:107
  78.0 39.0 %copy-start = (bf16[128,3072]{1,0:T(8,128)(2,1)S(1)}, bf16[128,3072]{1,0:T(8,128)(2,1)}, u32[]{:S(2)}) copy-start(bf16[128,3072]{1,0:T(8,128)(2,1)} %param.12) | copy-start | bytes 2359300
  119.7 44.7 %all-to-all-start.3 = ((bf16[8,64,3072]{2,1,0:T(8,128)(2,1)}), bf16[8,64,3072]{2,1,0:T(8,128)(2,1)}, u32[]{:S(2)}, u32[]{:S(2)}) async-start(bf16[8,64,3072]{2,1,0:T(8,128)(2,1)} %broadcast_in_dim.94), calls=%async_computation.3 | async-start | bytes 6291456 | tf_op jit(solution)/shard_map/all_to_all | solution.py:125
  126.8 50.4 %collective-permute-start.2 = (bf16[3072,512]{1,0:T(8,128)(2,1)}, bf16[3072,512]{1,0:T(8,128)(2,1)}, u32[]{:S(2)}, u32[]{:S(2)}) collective-permute-start(bf16[3072,512]{1,0:T(8,128)(2,1)} %param.21), channel_id=1, source_target_pairs={{0,1},{1,0},{2,3},{3,2},{4,5},{5,4},{6,7},{7,6},{8,9},{9,8},{10,11... | collective-permute-start | bytes 9437192 | tf_op jit(solution)/shard_map/ppermute | solution.py:116
  129.1 63.0 %collective-permute-start.3 = (bf16[3072,512]{1,0:T(8,128)(2,1)}, bf16[3072,512]{1,0:T(8,128)(2,1)}, u32[]{:S(2)}, u32[]{:S(2)}) collective-permute-start(bf16[3072,512]{1,0:T(8,128)(2,1)} %param.22), channel_id=1, source_target_pairs={{0,1},{1,0},{2,3},{3,2},{4,5},{5,4},{6,7},{7,6},{8,9},{9,8},{10,11... | collective-permute-start | bytes 9437192 | tf_op jit(solution)/shard_map/ppermute | solution.py:116
  129.2 62.9 %collective-permute-start.4 = (bf16[512,3072]{1,0:T(8,128)(2,1)}, bf16[512,3072]{1,0:T(8,128)(2,1)}, u32[]{:S(2)}, u32[]{:S(2)}) collective-permute-start(bf16[512,3072]{1,0:T(8,128)(2,1)} %param.23), channel_id=1, source_target_pairs={{0,1},{1,0},{2,3},{3,2},{4,5},{5,4},{6,7},{7,6},{8,9},{9,8},{10,11... | collective-permute-start | bytes 9437192 | tf_op jit(solution)/shard_map/ppermute | solution.py:116
  166.5 42.7 %all-to-all-start.5 = ((bf16[8,64,3072]{2,1,0:T(8,128)(2,1)}), bf16[8,64,3072]{2,1,0:T(8,128)(2,1)}, u32[]{:S(2)}, u32[]{:S(2)}) async-start(bf16[8,64,3072]{2,1,0:T(8,128)(2,1)} %broadcast_in_dim.95), calls=%async_computation.5 | async-start | bytes 6291456 | tf_op jit(solution)/shard_map/all_to_all | solution.py:125
  209.2 42.7 %all-to-all-start.4 = ((bf16[8,64,3072]{2,1,0:T(8,128)(2,1)}), bf16[8,64,3072]{2,1,0:T(8,128)(2,1)}, u32[]{:S(2)}, u32[]{:S(2)}) async-start(bf16[8,64,3072]{2,1,0:T(8,128)(2,1)} %bitcast.129), calls=%async_computation.4 | async-start | bytes 6291456 | tf_op jit(solution)/shard_map/all_to_all | solution.py:135
  251.9 42.7 %all-to-all-start.6 = ((bf16[8,64,3072]{2,1,0:T(8,128)(2,1)}), bf16[8,64,3072]{2,1,0:T(8,128)(2,1)}, u32[]{:S(2)}, u32[]{:S(2)}) async-start(bf16[8,64,3072]{2,1,0:T(8,128)(2,1)} %bitcast.130), calls=%async_computation.6 | async-start | bytes 6291456 | tf_op jit(solution)/shard_map/all_to_all | solution.py:135

commit v12 on v11

--- a/solution.py
+++ b/solution.py
@@ -117,11 +117,12 @@
     ]
     feed_axes = ("x_hi", "y")
     n_feed = lax.axis_size(feed_axes)
-    chunks = 2
-    size = rows_here // chunks
+    edge = rows_here // 4
+    bounds = [0, edge, rows_here - edge, rows_here]
     feeds = []
-    for c in range(chunks):
-        rows = normed[c * size : (c + 1) * size]
+    for c in range(len(bounds) - 1):
+        rows = normed[bounds[c] : bounds[c + 1]]
+        size = rows.shape[0]
         gathered = lax.all_to_all(
             jnp.broadcast_to(rows[None], (n_feed,) + rows.shape), feed_axes, 0, 0, tiled=False
         ).reshape(n_feed * size, rows.shape[1])

time: 299 us -> 318 us (1.064)
  waiting for transfers between devices: 139 us -> 110 us
  blocking collectives: 16.9 us -> 43.8 us
  matrix products: 74.9 us -> 85.7 us
  starting transfers between devices: 39.7 us -> 50 us
    all_to_all x2, waiting for transfers between devices: 41.1 us -> 8.71 us  [shards(): lax.all_to_all(jnp.broadcast_to(rows[None], (n_feed,) + rows.shape), feed...]
    all_to_all x0 -> x1, blocking collectives: none -> 26.9 us  [shards(): lax.all_to_all(jnp.broadcast_to(rows[None], (n_feed,) + rows.shape), feed...]
    dot_general x4 -> x6, matrix products: 41.9 us -> 49.4 us  [shards(): parts = parts + jnp.dot(hidden, down_w, preferred_element_type=jnp.float32)]
    all_to_all x2 -> x3, starting transfers between devices: 10.3 us -> 17.5 us  [shards(): lax.all_to_all(parts.reshape(n_feed, size, parts.shape[1]), feed_axes, 0,...]
    all_to_all x2 -> x3, waiting for transfers between devices: 40.6 us -> 44.3 us  [shards(): lax.all_to_all(parts.reshape(n_feed, size, parts.shape[1]), feed_axes, 0,...]
    dot_general x4 -> x6, matrix products: 20.5 us -> 24 us  [shards(): gate = jnp.dot(gathered, gate_w, preferred_element_type=jnp.float32)]
  transfers between devices with their start and end apart: 11 -> 12, of which waited for: 7 -> 7; matrix products, arithmetic and copies ran while one was open for 28% -> 31% of each run, Pallas kernels for 0% -> 0%
where the time goes in v12:
time: 318 us; the launch traced here: 317 us
  waiting for transfers between devices  110 us (35%)
  matrix products  85.7 us (27%)
  starting transfers between devices  50 us (16%)
  blocking collectives  43.8 us (14%)
  other arithmetic  14 us (4%)
  local copies, waits for them, and re-layouts  11.1 us (3%)
    dot_general x6, matrix products, shards(): parts = parts + jnp.dot(hidden, down_w, preferred_element_type=jnp.float32)  49.4 us
    all_to_all x3, waiting for transfers between devices, shards(): lax.all_to_all(parts.reshape(n_feed, size, parts.shape[1]), feed_axes, 0,...  44.3 us
    all_to_all x1, waiting for transfers between devices, shards(): lax.all_to_all(partial.reshape(n_z, rows_here, partial.shape[1]), 'z', 0,...  35.2 us
    all_to_all x1, blocking collectives, shards(): lax.all_to_all(jnp.broadcast_to(rows[None], (n_feed,) + rows.shape), feed...  26.9 us
    dot_general x6, matrix products, shards(): gate = jnp.dot(gathered, gate_w, preferred_element_type=jnp.float32)  24 us
    all_to_all x3, starting transfers between devices, shards(): lax.all_to_all(parts.reshape(n_feed, size, parts.shape[1]), feed_axes, 0,...  17.5 us
    all_to_all x1, blocking collectives, shards(): lax.all_to_all(ordered, 'z', 0, 0, tiled=False)  16.9 us
    ppermute x1, waiting for transfers between devices, shards(): lax.ppermute(lax.dynamic_slice_in_dim(out_weight, core * width, width, 0)...  15.2 us
  transfers between devices with their start and end apart: 12, of which 7 were waited for; matrix products, arithmetic and copies ran while one was open for 31% of the time, Pallas kernels for 0%

profile of v12, /device:TPU:1, one launch (start us, length us, event | category | flops | bytes accessed | tf_op | source)
XLA Modules:
  0.0 316.7 jit_solution(11002409043919487515)
XLA Ops:
  0.0 2.0 broadcast_in_dim.97
  2.0 8.4 %all-to-all-start = ((bf16[16,16,2048]{2,1,0:T(8,128)(2,1)}), bf16[16,16,2048]{2,1,0:T(8,128)(2,1)S(1)}, u32[]{:S(2)}, u32[]{:S(2)}) async-start(bf16[16,16,2048]{2,1,0:T(8,128)(2,1)} %broadcast_in_dim.97), calls=%async_computation | async-start | bytes 2097152 | tf_op jit(solution)/shard_map/all_to_all | solution.py:75
  10.5 2.4 constant_dynamic-slice_fusion
  12.9 0.3 collective-permute-start
  13.9 0.3 copy.33
  14.2 0.4 copy.34
  14.6 1.5 copy.32
  16.1 1.0 pad_maximum_fusion
  17.1 0.1 fusion.63
  17.2 0.2 fusion.62
  17.5 3.0 fusion.9
  20.5 7.1 %all-to-all-done = bf16[16,16,2048]{2,1,0:T(8,128)(2,1)S(1)} async-done(((bf16[16,16,2048]{2,1,0:T(8,128)(2,1)}), bf16[16,16,2048]{2,1,0:T(8,128)(2,1)S(1)}, u32[]{:S(2)}, u32[]{:S(2)}) %all-to-all-start) | async-done | bytes 1048608 | tf_op jit(solution)/shard_map/all_to_all | solution.py:75
  27.6 0.2 copy.38
  27.8 0.2 copy.41
  28.1 0.7 fusion.14
  28.8 0.8 fusion.22
  29.6 0.8 fusion.24
  30.4 0.1 slice-done.1
  30.5 1.2 fusion.12
  31.7 1.6 fusion.29
  33.4 0.2 reverse_select_fusion
  33.5 15.2 %collective-permute-done = bf16[192,3072]{1,0:T(8,128)(2,1)} collective-permute-done((bf16[192,3072]{1,0:T(8,128)(2,1)}, bf16[192,3072]{1,0:T(8,128)(2,1)}, u32[]{:S(2)}, u32[]{:S(2)}) %collective-permute-start) | collective-permute-done | bytes 1179680 | tf_op jit(solution)/shard_map/ppermute | solution.py:92
  48.7 0.6 collective-permute-start.1
  49.3 0.1 reverse_select_fusion.1
  49.5 16.9 %all_to_all.45 = bf16[4,128,768]{1,2,0:T(8,128)(2,1)S(1)} all-to-all(bf16[4,128,768]{1,2,0:T(8,128)(2,1)S(1)} %maximum_bitcast_fusion), channel_id=1, replica_groups=mesh['z'=4,'x_lo'=2,'x_hi'=2,'y'=4,'core'=2] {'z'}, dimensions={0} | all-to-all | bytes 1572864 | tf_op jit(solution)/shard_map/all_to_all | solution.py:105
  66.4 0.3 copy.45
  66.7 6.3 %fusion.6 = bf16[512,3072]{1,0:T(8,128)(2,1)} fusion(bf16[512,768]{1,0:T(8,128)(2,1)S(1)} %bitcast.153, bf16[192,3072]{1,0:T(8,128)(2,1)S(1)} %collective-permute-done.1, bf16[192,3072]{1,0:T(8,128)(2,1)} %collective-permute-done, bf16[384,3072]{1,0:T(8,128)(2,1)} %param.19), kind=kOutput, calls=%fused_computation.11 | convolution fusion | flops 2431647744 | bytes 8650752 | tf_op jit(solution)/shard_map/dot_general | solution.py:106
  73.0 4.8 %all-to-all-start.2 = ((bf16[4,128,3072]{2,1,0:T(8,128)(2,1)}), bf16[4,128,3072]{2,1,0:T(8,128)(2,1)}, u32[]{:S(2)}, u32[]{:S(2)}) async-start(bf16[4,128,3072]{2,1,0:T(8,128)(2,1)} %bitcast.28), calls=%async_computation.2 | async-start | bytes 6291456 | tf_op jit(solution)/shard_map/all_to_all | solution.py:107
  77.8 1.4 collective-permute-start.2
  79.2 35.2 %all-to-all-done.2 = bf16[4,128,3072]{2,1,0:T(8,128)(2,1)} async-done(((bf16[4,128,3072]{2,1,0:T(8,128)(2,1)}), bf16[4,128,3072]{2,1,0:T(8,128)(2,1)}, u32[]{:S(2)}, u32[]{:S(2)}) %all-to-all-start.2) | async-done | bytes 3145760 | tf_op jit(solution)/shard_map/all_to_all | solution.py:107
  114.4 2.6 convert_reduce_fusion.1
  117.0 0.3 multiply_reduce_fusion
  117.3 0.3 multiply_convert_fusion
  117.6 0.2 broadcast_in_dim.100
  117.8 26.9 %all_to_all.46 = bf16[8,32,3072]{2,1,0:T(8,128)(2,1)} all-to-all(bf16[8,32,3072]{2,1,0:T(8,128)(2,1)S(1)} %broadcast_in_dim.100), channel_id=1, replica_groups=mesh['z'=4,'x_lo'=2,'x_hi'=2,'y'=4,'core'=2] {'x_hi','y'}, dimensions={0} | all-to-all | bytes 3145728 | tf_op jit(solution)/shard_map/all_to_all | solution.py:126
  144.7 1.3 broadcast_in_dim.102
  146.1 4.3 %all-to-all-start.7 = ((bf16[8,32,3072]{2,1,0:T(8,128)(2,1)}), bf16[8,32,3072]{2,1,0:T(8,128)(2,1)}, u32[]{:S(2)}, u32[]{:S(2)}) async-start(bf16[8,32,3072]{2,1,0:T(8,128)(2,1)} %broadcast_in_dim.102), calls=%async_computation.7 | async-start | bytes 3145728 | tf_op jit(solution)/shard_map/all_to_all | solution.py:126
  150.4 3.9 %collective-permute-start.3 = (bf16[3072,512]{1,0:T(8,128)(2,1)}, bf16[3072,512]{1,0:T(8,128)(2,1)}, u32[]{:S(2)}, u32[]{:S(2)}) collective-permute-start(bf16[3072,512]{1,0:T(8,128)(2,1)} %param.22), channel_id=1, source_target_pairs={{0,1},{1,0},{2,3},{3,2},{4,5},{5,4},{6,7},{7,6},{8,9},{9,8},{10,11... | collective-permute-start | bytes 9437192 | tf_op jit(solution)/shard_map/ppermute | solution.py:116
  154.3 0.1 collective-permute-start.4
  154.4 4.2 %fusion.92 = f32[256,512]{1,0:T(8,128)} fusion(bf16[256,3072]{1,0:T(8,128)(2,1)} %bitcast.140, bf16[3072,512]{1,0:T(8,128)(2,1)} %param.21), kind=kOutput, calls=%fused_computation.129 | convolution fusion | flops 805306368 | bytes 5242880 | tf_op jit(solution)/shard_map/dot_general | solution.py:131
  158.6 8.7 %all-to-all-done.7 = bf16[8,32,3072]{2,1,0:T(8,128)(2,1)} async-done(((bf16[8,32,3072]{2,1,0:T(8,128)(2,1)}), bf16[8,32,3072]{2,1,0:T(8,128)(2,1)}, u32[]{:S(2)}, u32[]{:S(2)}) %all-to-all-start.7) | async-done | bytes 1572896 | tf_op jit(solution)/shard_map/all_to_all | solution.py:126
  167.3 2.0 broadcast_in_dim.101
  169.3 8.6 %all-to-all-start.5 = ((bf16[8,64,3072]{2,1,0:T(8,128)(2,1)}), bf16[8,64,3072]{2,1,0:T(8,128)(2,1)}, u32[]{:S(2)}, u32[]{:S(2)}) async-start(bf16[8,64,3072]{2,1,0:T(8,128)(2,1)} %broadcast_in_dim.101), calls=%async_computation.5 | async-start | bytes 6291456 | tf_op jit(solution)/shard_map/all_to_all | solution.py:126
  177.9 4.3 %fusion.96 = f32[256,512]{1,0:T(8,128)} fusion(bf16[256,3072]{1,0:T(8,128)(2,1)} %bitcast.33, bf16[3072,512]{1,0:T(8,128)(2,1)} %param.21), kind=kOutput, calls=%fused_computation.133 | convolution fusion | flops 805306368 | bytes 5242880 | tf_op jit(solution)/shard_map/dot_general | solution.py:131
  182.2 2.9 fusion.93
  185.1 3.3 %fusion.97 = f32[256,512]{1,0:T(8,128)S(1)} fusion(bf16[256,3072]{1,0:T(8,128)(2,1)} %bitcast.33, bf16[3072,512]{1,0:T(8,128)(2,1)} %collective-permute-done.2), kind=kOutput, calls=%fused_computation.134 | convolution fusion | flops 805306368 | bytes 5242880 | tf_op jit(solution)/shard_map/dot_general | solution.py:131
  188.4 7.0 %fusion.41 = f32[256,3072]{1,0:T(8,128)} fusion(bf16[512,3072]{1,0:T(8,128)(2,1)} %param.23, bf16[256,3072]{1,0:T(8,128)(2,1)} %bitcast.33, bf16[3072,512]{1,0:T(8,128)(2,1)} %param.22, f32[256,512]{1,0:T(8,128)} %fusion.96), kind=kOutput, calls=%fused_computation.59 | convolution fusion | flops 1611399168 | bytes 11534336 | tf_op jit(solution)/shard_map/dot_general | solution.py:134
  195.5 7.0 %fusion.42 = f32[256,3072]{1,0:T(8,128)} fusion(bf16[512,3072]{1,0:T(8,128)(2,1)} %param.23, bf16[256,3072]{1,0:T(8,128)(2,1)} %bitcast.141, bf16[3072,512]{1,0:T(8,128)(2,1)} %param.22, f32[256,512]{1,0:T(8,128)} %fusion.92), kind=kOutput, calls=%fused_computation.60 | convolution fusion | flops 1611399168 | bytes 11534336 | tf_op jit(solution)/shard_map/dot_general | solution.py:134
  202.5 7.3 %fusion.11 = bf16[256,3072]{1,0:T(8,128)(2,1)} fusion(f32[256,3072]{1,0:T(8,128)} %fusion.41, bf16[512,3072]{1,0:T(8,128)(2,1)} %collective-permute-done.4, f32[256,512]{1,0:T(8,128)S(1)} %fusion.97, bf16[256,3072]{1,0:T(8,128)(2,1)} %bitcast.33, bf16[3072,512]{1,0:T(8,128)(2,1)} %collective-permute-done.3), kind=kOutput, calls=%fused_computation.16 | convolution fusion | flops 1612972032 | bytes 13107200 | tf_op jit(solution)/shard_map/dot_general | solution.py:134
  209.8 7.3 %fusion.10 = bf16[256,3072]{1,0:T(8,128)(2,1)} fusion(f32[256,3072]{1,0:T(8,128)} %fusion.42, bf16[512,3072]{1,0:T(8,128)(2,1)} %collective-permute-done.4, f32[256,512]{1,0:T(8,128)S(1)} %fusion.93, bf16[256,3072]{1,0:T(8,128)(2,1)} %bitcast.142, bf16[3072,512]{1,0:T(8,128)(2,1)} %collective-permute-done.3), kind=kOutput, calls=%fused_computation.15 | convolution fusion | flops 1612972032 | bytes 13107200 | tf_op jit(solution)/shard_map/dot_general | solution.py:134
  217.1 6.6 %all-to-all-start.8 = ((bf16[8,32,3072]{2,1,0:T(8,128)(2,1)}), bf16[8,32,3072]{2,1,0:T(8,128)(2,1)}, u32[]{:S(2)}, u32[]{:S(2)}) async-start(bf16[8,32,3072]{2,1,0:T(8,128)(2,1)} %bitcast.145), calls=%async_computation.8 | async-start | bytes 3145728 | tf_op jit(solution)/shard_map/all_to_all | solution.py:136
  223.8 4.6 %fusion.94 = f32[512,512]{1,0:T(8,128)S(1)} fusion(bf16[512,3072]{1,0:T(8,128)(2,1)} %bitcast.31, bf16[3072,512]{1,0:T(8,128)(2,1)} %param.21), kind=kOutput, calls=%fused_computation.131 | convolution fusion | flops 1610612736 | bytes 7340032 | tf_op jit(solution)/shard_map/dot_general | solution.py:131
  228.4 9.9 %fusion.43 = f32[512,3072]{1,0:T(8,128)} fusion(bf16[512,3072]{1,0:T(8,128)(2,1)} %param.23, bf16[512,3072]{1,0:T(8,128)(2,1)} %bitcast.31, bf16[3072,512]{1,0:T(8,128)(2,1)} %param.22, f32[512,512]{1,0:T(8,128)S(1)} %fusion.94), kind=kOutput, calls=%fused_computation.61 | convolution fusion | flops 3222798336 | bytes 16777216 | tf_op jit(solution)/shard_map/dot_general | solution.py:134
  238.3 5.5 %all-to-all-done.8 = bf16[8,32,3072]{2,1,0:T(8,128)(2,1)} async-done(((bf16[8,32,3072]{2,1,0:T(8,128)(2,1)}), bf16[8,32,3072]{2,1,0:T(8,128)(2,1)}, u32[]{:S(2)}, u32[]{:S(2)}) %all-to-all-start.8) | async-done | bytes 1572896 | tf_op jit(solution)/shard_map/all_to_all | solution.py:136
  243.8 5.8 %all-to-all-start.4 = ((bf16[8,32,3072]{2,1,0:T(8,128)(2,1)}), bf16[8,32,3072]{2,1,0:T(8,128)(2,1)}, u32[]{:S(2)}, u32[]{:S(2)}) async-start(bf16[8,32,3072]{2,1,0:T(8,128)(2,1)} %bitcast.144), calls=%async_computation.4 | async-start | bytes 3145728 | tf_op jit(solution)/shard_map/all_to_all | solution.py:136
  249.6 4.6 %fusion.95 = f32[512,512]{1,0:T(8,128)S(1)} fusion(bf16[512,3072]{1,0:T(8,128)(2,1)} %bitcast.31, bf16[3072,512]{1,0:T(8,128)(2,1)} %collective-permute-done.2), kind=kOutput, calls=%fused_computation.132 | convolution fusion | flops 1610612736 | bytes 7340032 | tf_op jit(solution)/shard_map/dot_general | solution.py:131
  254.2 10.8 %add_convert_fusion = bf16[512,3072]{1,0:T(8,128)(2,1)} fusion(f32[512,3072]{1,0:T(8,128)} %fusion.43, bf16[512,3072]{1,0:T(8,128)(2,1)} %collective-permute-done.4, f32[512,512]{1,0:T(8,128)S(1)} %fusion.95, bf16[512,3072]{1,0:T(8,128)(2,1)} %bitcast.31, bf16[3072,512]{1,0:T(8,128)(2,1)} %collective-permute-done.3), kind=kOutput, calls=%fused_computation.1 | convolution fusion | flops 3225944064 | bytes 19922944 | tf_op jit(solution)/shard_map/dot_general | solution.py:134
  265.0 5.3 %all-to-all-done.4 = bf16[8,32,3072]{2,1,0:T(8,128)(2,1)} async-done(((bf16[8,32,3072]{2,1,0:T(8,128)(2,1)}), bf16[8,32,3072]{2,1,0:T(8,128)(2,1)}, u32[]{:S(2)}, u32[]{:S(2)}) %all-to-all-start.4) | async-done | bytes 1572896 | tf_op jit(solution)/shard_map/all_to_all | solution.py:136
  270.3 5.2 %all-to-all-start.6 = ((bf16[8,64,3072]{2,1,0:T(8,128)(2,1)}), bf16[8,64,3072]{2,1,0:T(8,128)(2,1)}, u32[]{:S(2)}, u32[]{:S(2)}) async-start(bf16[8,64,3072]{2,1,0:T(8,128)(2,1)} %bitcast.147), calls=%async_computation.6 | async-start | bytes 6291456 | tf_op jit(solution)/shard_map/all_to_all | solution.py:136
  276.1 1.7 convert_reduce_fusion.2
  277.8 1.7 convert_reduce_fusion.3
  279.4 33.5 %all-to-all-done.6 = bf16[8,64,3072]{2,1,0:T(8,128)(2,1)} async-done(((bf16[8,64,3072]{2,1,0:T(8,128)(2,1)}), bf16[8,64,3072]{2,1,0:T(8,128)(2,1)}, u32[]{:S(2)}, u32[]{:S(2)}) %all-to-all-start.6) | async-done | bytes 3145760 | tf_op jit(solution)/shard_map/all_to_all | solution.py:136
  313.0 2.5 convert_reduce_fusion
  315.5 1.2 fusion.27
  (42 shorter events, 0.4 us)
Async XLA Ops:
  0.0 13.9 %copy-start.5 = (bf16[128,2048]{1,0:T(8,128)(2,1)S(1)}, bf16[128,2048]{1,0:T(8,128)(2,1)}, u32[]{:S(2)}) copy-start(bf16[128,2048]{1,0:T(8,128)(2,1)} %param.14) | copy-start | bytes 1572868
  0.0 14.2 %copy-start.3 = (bf16[128,3072]{1,0:T(8,128)(2,1)S(1)}, bf16[128,3072]{1,0:T(8,128)(2,1)}, u32[]{:S(2)}) copy-start(bf16[128,3072]{1,0:T(8,128)(2,1)} %param.13) | copy-start | bytes 2359300
  2.0 25.5 %all-to-all-start = ((bf16[16,16,2048]{2,1,0:T(8,128)(2,1)}), bf16[16,16,2048]{2,1,0:T(8,128)(2,1)S(1)}, u32[]{:S(2)}, u32[]{:S(2)}) async-start(bf16[16,16,2048]{2,1,0:T(8,128)(2,1)} %broadcast_in_dim.97), calls=%async_computation | async-start | bytes 2097152 | tf_op jit(solution)/shard_map/all_to_all | solution.py:75
  12.9 35.8 %collective-permute-start = (bf16[192,3072]{1,0:T(8,128)(2,1)}, bf16[192,3072]{1,0:T(8,128)(2,1)}, u32[]{:S(2)}, u32[]{:S(2)}) collective-permute-start(bf16[192,3072]{1,0:T(8,128)(2,1)} %constant_dynamic-slice_fusion), channel_id=1, source_target_pairs={{0,16},{16,0},{1,17},{17,1},{2,18},{18,2},{3,19},{19,3},{4,20},{20... | collective-permute-start | bytes 3538952 | tf_op jit(solution)/shard_map/ppermute | solution.py:92
  28.1 2.4 slice-start
  28.7 1.8 slice-start.1
  30.4 1.3 copy-start.4
  48.7 18.0 %collective-permute-start.1 = (bf16[192,3072]{1,0:T(8,128)(2,1)}, bf16[192,3072]{1,0:T(8,128)(2,1)S(1)}, u32[]{:S(2)}, u32[]{:S(2)}) collective-permute-start(bf16[192,3072]{1,0:T(8,128)(2,1)} %collective-permute-done), channel_id=1, source_target_pairs={{0,1},{1,0},{2,3},{3,2},{4,5},{5,4},{6,7},{7,6},{8,9},{9,8},{10,11... | collective-permute-start | bytes 3538952 | tf_op jit(solution)/shard_map/ppermute | solution.py:95
  73.0 6.2 %copy-start.6 = (bf16[3072]{0:T(1024)(128)(2,1)S(1)}, bf16[3072]{0:T(1024)(128)(2,1)}, u32[]{:S(2)}) copy-start(bf16[3072]{0:T(1024)(128)(2,1)} %param.20) | copy-start | bytes 18436
  73.0 41.4 %all-to-all-start.2 = ((bf16[4,128,3072]{2,1,0:T(8,128)(2,1)}), bf16[4,128,3072]{2,1,0:T(8,128)(2,1)}, u32[]{:S(2)}, u32[]{:S(2)}) async-start(bf16[4,128,3072]{2,1,0:T(8,128)(2,1)} %bitcast.28), calls=%async_computation.2 | async-start | bytes 6291456 | tf_op jit(solution)/shard_map/all_to_all | solution.py:107
  77.8 39.2 %copy-start = (bf16[128,3072]{1,0:T(8,128)(2,1)S(1)}, bf16[128,3072]{1,0:T(8,128)(2,1)}, u32[]{:S(2)}) copy-start(bf16[128,3072]{1,0:T(8,128)(2,1)} %param.12) | copy-start | bytes 2359300
  77.8 104.4 %collective-permute-start.2 = (bf16[3072,512]{1,0:T(8,128)(2,1)}, bf16[3072,512]{1,0:T(8,128)(2,1)}, u32[]{:S(2)}, u32[]{:S(2)}) collective-permute-start(bf16[3072,512]{1,0:T(8,128)(2,1)} %param.21), channel_id=1, source_target_pairs={{0,1},{1,0},{2,3},{3,2},{4,5},{5,4},{6,7},{7,6},{8,9},{9,8},{10,11... | collective-permute-start | bytes 9437192 | tf_op jit(solution)/shard_map/ppermute | solution.py:116
  117.6 36.8 %copy-start.2 = (bf16[128,3072]{1,0:T(8,128)(2,1)}, bf16[128,3072]{1,0:T(8,128)(2,1)S(1)}, u32[]{:S(2)}) copy-start(bf16[128,3072]{1,0:T(8,128)(2,1)S(1)} %multiply_convert_fusion) | copy-start | bytes 2359300
  146.1 21.3 %all-to-all-start.7 = ((bf16[8,32,3072]{2,1,0:T(8,128)(2,1)}), bf16[8,32,3072]{2,1,0:T(8,128)(2,1)}, u32[]{:S(2)}, u32[]{:S(2)}) async-start(bf16[8,32,3072]{2,1,0:T(8,128)(2,1)} %broadcast_in_dim.102), calls=%async_computation.7 | async-start | bytes 3145728 | tf_op jit(solution)/shard_map/all_to_all | solution.py:126
  150.4 52.2 %collective-permute-start.3 = (bf16[3072,512]{1,0:T(8,128)(2,1)}, bf16[3072,512]{1,0:T(8,128)(2,1)}, u32[]{:S(2)}, u32[]{:S(2)}) collective-permute-start(bf16[3072,512]{1,0:T(8,128)(2,1)} %param.22), channel_id=1, source_target_pairs={{0,1},{1,0},{2,3},{3,2},{4,5},{5,4},{6,7},{7,6},{8,9},{9,8},{10,11... | collective-permute-start | bytes 9437192 | tf_op jit(solution)/shard_map/ppermute | solution.py:116
  154.3 48.2 %collective-permute-start.4 = (bf16[512,3072]{1,0:T(8,128)(2,1)}, bf16[512,3072]{1,0:T(8,128)(2,1)}, u32[]{:S(2)}, u32[]{:S(2)}) collective-permute-start(bf16[512,3072]{1,0:T(8,128)(2,1)} %param.23), channel_id=1, source_target_pairs={{0,1},{1,0},{2,3},{3,2},{4,5},{5,4},{6,7},{7,6},{8,9},{9,8},{10,11... | collective-permute-start | bytes 9437192 | tf_op jit(solution)/shard_map/ppermute | solution.py:116
  154.4 12.9 %slice-start.2 = ((bf16[128,3072]{1,0:T(8,128)(2,1)}), bf16[64,3072]{1,0:T(8,128)(2,1)S(1)}, s32[]{:S(2)}) async-start(bf16[128,3072]{1,0:T(8,128)(2,1)} %copy-done.2), calls=%async_computation.11 | async-start | bytes 786432 | tf_op jit(solution)/shard_map/slice | solution.py:124
  169.3 47.8 %all-to-all-start.5 = ((bf16[8,64,3072]{2,1,0:T(8,128)(2,1)}), bf16[8,64,3072]{2,1,0:T(8,128)(2,1)}, u32[]{:S(2)}, u32[]{:S(2)}) async-start(bf16[8,64,3072]{2,1,0:T(8,128)(2,1)} %broadcast_in_dim.101), calls=%async_computation.5 | async-start | bytes 6291456 | tf_op jit(solution)/shard_map/all_to_all | solution.py:126
  177.9 4.3 %copy-start.1 = (bf16[8,32,3072]{2,1,0:T(8,128)(2,1)S(1)}, bf16[8,32,3072]{2,1,0:T(8,128)(2,1)}, u32[]{:S(2)}) copy-start(bf16[8,32,3072]{2,1,0:T(8,128)(2,1)} %all_to_all.46) | copy-start | bytes 4718596
  217.1 26.7 %all-to-all-start.8 = ((bf16[8,32,3072]{2,1,0:T(8,128)(2,1)}), bf16[8,32,3072]{2,1,0:T(8,128)(2,1)}, u32[]{:S(2)}, u32[]{:S(2)}) async-start(bf16[8,32,3072]{2,1,0:T(8,128)(2,1)} %bitcast.145), calls=%async_computation.8 | async-start | bytes 3145728 | tf_op jit(solution)/shard_map/all_to_all | solution.py:136
  243.8 26.4 %all-to-all-start.4 = ((bf16[8,32,3072]{2,1,0:T(8,128)(2,1)}), bf16[8,32,3072]{2,1,0:T(8,128)(2,1)}, u32[]{:S(2)}, u32[]{:S(2)}) async-start(bf16[8,32,3072]{2,1,0:T(8,128)(2,1)} %bitcast.144), calls=%async_computation.4 | async-start | bytes 3145728 | tf_op jit(solution)/shard_map/all_to_all | solution.py:136
  270.3 42.7 %all-to-all-start.6 = ((bf16[8,64,3072]{2,1,0:T(8,128)(2,1)}), bf16[8,64,3072]{2,1,0:T(8,128)(2,1)}, u32[]{:S(2)}, u32[]{:S(2)}) async-start(bf16[8,64,3072]{2,1,0:T(8,128)(2,1)} %bitcast.147), calls=%async_computation.6 | async-start | bytes 6291456 | tf_op jit(solution)/shard_map/all_to_all | solution.py:136

commit v13 on v9

--- a/solution.py
+++ b/solution.py
@@ -111,9 +111,9 @@
     mixed = layer_input.astype(jnp.float32) + projected
     scale = lax.rsqrt(jnp.mean(mixed * mixed, axis=-1, keepdims=True) + 1e-05)
     normed = (mixed * scale * norm_gain.astype(jnp.float32)).astype(jnp.bfloat16)
-    gate_both = jnp.concatenate([gate_weight, lax.ppermute(gate_weight, "core", swap)], axis=1)
-    up_both = jnp.concatenate([up_weight, lax.ppermute(up_weight, "core", swap)], axis=1)
-    down_both = jnp.concatenate([down_weight, lax.ppermute(down_weight, "core", swap)], axis=0)
+    gate_both = lax.all_gather(gate_weight, "core", axis=1, tiled=True)
+    up_both = lax.all_gather(up_weight, "core", axis=1, tiled=True)
+    down_both = lax.all_gather(down_weight, "core", axis=0, tiled=True)
     feed_axes = ("x_hi", "y")
     n_feed = lax.axis_size(feed_axes)
     chunks = 2

time: 299 us -> 309 us (1.033)
  blocking collectives: 16.9 us -> 60.7 us
  local copies, waits for them, and re-layouts: 32.1 us -> 9.22 us
  waiting for transfers between devices: 138 us -> 122 us
  between operations: 1.63 us -> 14.8 us
  starting transfers between devices: 38.4 us -> 29 us
    all_to_all x0 -> x1, blocking collectives: none -> 43.7 us  [shards(): lax.all_to_all(jnp.broadcast_to(rows[None], (n_feed,) + rows.shape), feed...]
    all_to_all x2 -> x1, waiting for transfers between devices: 31.9 us -> 14.5 us  [shards(): lax.all_to_all(jnp.broadcast_to(rows[None], (n_feed,) + rows.shape), feed...]
    concatenate x3 -> x0, local copies, waits for them, and re-layouts: 11.5 us -> none  [the longest x1 3.86 us: shards(): jnp.concatenate([gate_weight, lax.ppermute(gate_weight, 'core', swap)], a...]
    all_to_all x2 -> x1, starting transfers between devices: 12.3 us -> 4.44 us  [shards(): lax.all_to_all(jnp.broadcast_to(rows[None], (n_feed,) + rows.shape), feed...]
    unnamed x24 -> x19, local copies, waits for them, and re-layouts: 11 us -> 3.61 us
  transfers between devices with their start and end apart: 11 -> 10, of which waited for: 7 -> 6; matrix products, arithmetic and copies ran while one was open for 30% -> 25% of each run, Pallas kernels for 0% -> 0%
where the time goes in v13:
time: 309 us; the launch traced here: 308 us
  waiting for transfers between devices  122 us (39%)
  blocking collectives  60.7 us (20%)
  matrix products  58.5 us (19%)
  starting transfers between devices  29 us (9%)
  between operations  14.8 us (5%)
  other arithmetic  13.2 us (4%)
  local copies, waits for them, and re-layouts  9.22 us (3%)
    all_to_all x2, waiting for transfers between devices, shards(): lax.all_to_all(parts.reshape(n_feed, size, parts.shape[1]), feed_axes, 0,...  48.9 us
    all_to_all x1, blocking collectives, shards(): lax.all_to_all(jnp.broadcast_to(rows[None], (n_feed,) + rows.shape), feed...  43.7 us
    all_to_all x1, waiting for transfers between devices, shards(): lax.all_to_all(partial.reshape(n_z, rows_here, partial.shape[1]), 'z', 0,...  35.8 us
    dot_general x2, matrix products, shards(): jnp.dot(hidden, down_both, preferred_element_type=jnp.float32)  29 us
    dot_general x2, matrix products, shards(): gate = jnp.dot(gathered, gate_both, preferred_element_type=jnp.float32)  17.1 us
    all_to_all x1, blocking collectives, shards(): lax.all_to_all(ordered, 'z', 0, 0, tiled=False)  16.9 us
    ppermute x1, waiting for transfers between devices, shards(): lax.ppermute(lax.dynamic_slice_in_dim(out_weight, core * width, width, 0)...  15.2 us
    all_to_all x1, waiting for transfers between devices, shards(): lax.all_to_all(jnp.broadcast_to(rows[None], (n_feed,) + rows.shape), feed...  14.5 us
  transfers between devices with their start and end apart: 10, of which 6 were waited for; matrix products, arithmetic and copies ran while one was open for 25% of the time, Pallas kernels for 0%

profile of v13, /device:TPU:1, one launch (start us, length us, event | category | flops | bytes accessed | tf_op | source)
XLA Modules:
  0.0 307.8 jit_solution(17918657994379764970)
XLA Ops:
  6.5 0.7 all-gather.4.cloned.1.call-update
  7.3 0.1 copy-done.4
  7.4 1.1 broadcast_in_dim.91
  8.5 8.4 %all-to-all-start = ((bf16[16,16,2048]{2,1,0:T(8,128)(2,1)}), bf16[16,16,2048]{2,1,0:T(8,128)(2,1)S(1)}, u32[]{:S(2)}, u32[]{:S(2)}) async-start(bf16[16,16,2048]{2,1,0:T(8,128)(2,1)} %broadcast_in_dim.91), calls=%async_computation | async-start | bytes 2097152 | tf_op jit(solution)/shard_map/all_to_all | solution.py:75
  16.9 0.0 all-gather.6.cloned.1.call-start
  17.0 1.1 constant_dynamic-slice_fusion
  18.1 0.3 collective-permute-start
  18.4 0.0 all-gather.6.cloned.1.call-update
  19.2 1.5 copy.32
  20.6 0.3 copy.33
  20.9 1.6 copy.34
  22.6 1.0 pad_maximum_fusion
  23.6 0.1 fusion.39
  23.7 0.2 fusion.38
  23.9 3.1 %fusion.9 = (f32[8,3,128]{2,1,0:T(4,128)S(1)}, f32[8,384,128,3]{2,1,3,0:T(8,128)}) fusion(pred[128,384]{0,1:T(8,128)(4,1)S(1)} %fusion.38, bf16[384,8,128,1]{0,2,3,1:T(8,128)(2,1)S(1)} %bitcast.123, bf16[128,8,3,128]{0,3,2,1:T(8,128)(2,1)S(1)} %bitcast.116), kind=kOutput, calls=%fused_computation.14 | convolution fusion | flops 305525760 | bytes 6352896 | tf_op jit(solution)/shard_map/skgh,nkh->kgsn/dot_general | solution.py:20
  27.0 6.9 %all-to-all-done = bf16[16,16,2048]{2,1,0:T(8,128)(2,1)S(1)} async-done(((bf16[16,16,2048]{2,1,0:T(8,128)(2,1)}), bf16[16,16,2048]{2,1,0:T(8,128)(2,1)S(1)}, u32[]{:S(2)}, u32[]{:S(2)}) %all-to-all-start) | async-done | bytes 1048608 | tf_op jit(solution)/shard_map/all_to_all | solution.py:75
  34.0 0.1 fusion.56
  34.1 0.2 copy.38
  34.3 0.2 copy.41
  34.5 0.0 slice-start
  34.5 0.7 fusion.12
  35.2 0.8 fusion.20
  36.0 0.8 fusion.22
  36.8 0.0 copy-start.1
  36.9 0.1 slice-done.1
  37.0 1.2 fusion.10
  38.2 1.6 fusion.27
  39.7 0.1 copy.44
  39.8 0.2 reverse_select_fusion
  40.0 15.2 %collective-permute-done = bf16[192,3072]{1,0:T(8,128)(2,1)} collective-permute-done((bf16[192,3072]{1,0:T(8,128)(2,1)}, bf16[192,3072]{1,0:T(8,128)(2,1)}, u32[]{:S(2)}, u32[]{:S(2)}) %collective-permute-start) | collective-permute-done | bytes 1179680 | tf_op jit(solution)/shard_map/ppermute | solution.py:92
  55.1 0.6 collective-permute-start.1
  55.7 0.1 slice_bitcast_fusion
  55.8 0.1 reverse_select_fusion.1
  55.9 0.1 maximum_bitcast_fusion
  55.9 16.9 %all_to_all.35 = bf16[4,128,768]{1,2,0:T(8,128)(2,1)S(1)} all-to-all(bf16[4,128,768]{1,2,0:T(8,128)(2,1)S(1)} %maximum_bitcast_fusion), channel_id=1, replica_groups=mesh['z'=4,'x_lo'=2,'x_hi'=2,'y'=4,'core'=2] {'z'}, dimensions={0} | all-to-all | bytes 1572864 | tf_op jit(solution)/shard_map/all_to_all | solution.py:105
  72.9 0.3 copy.45
  73.1 6.3 %fusion.6 = bf16[512,3072]{1,0:T(8,128)(2,1)} fusion(bf16[512,768]{1,0:T(8,128)(2,1)S(1)} %bitcast.128, bf16[192,3072]{1,0:T(8,128)(2,1)S(1)} %collective-permute-done.1, bf16[192,3072]{1,0:T(8,128)(2,1)} %collective-permute-done, bf16[384,3072]{1,0:T(8,128)(2,1)} %param.19), kind=kOutput, calls=%fused_computation.11 | convolution fusion | flops 2431647744 | bytes 8650752 | tf_op jit(solution)/shard_map/dot_general | solution.py:106
  79.5 4.7 %all-to-all-start.2 = ((bf16[4,128,3072]{2,1,0:T(8,128)(2,1)}), bf16[4,128,3072]{2,1,0:T(8,128)(2,1)}, u32[]{:S(2)}, u32[]{:S(2)}) async-start(bf16[4,128,3072]{2,1,0:T(8,128)(2,1)} %bitcast.28), calls=%async_computation.2 | async-start | bytes 6291456 | tf_op jit(solution)/shard_map/all_to_all | solution.py:107
  84.2 0.0 copy-start.5
  84.2 0.2 all-gather.8.cloned.1.call-start
  84.4 0.5 all-gather.8.cloned.1.call-update
  84.9 0.0 copy-start
  85.0 35.8 %all-to-all-done.2 = bf16[4,128,3072]{2,1,0:T(8,128)(2,1)} async-done(((bf16[4,128,3072]{2,1,0:T(8,128)(2,1)}), bf16[4,128,3072]{2,1,0:T(8,128)(2,1)}, u32[]{:S(2)}, u32[]{:S(2)}) %all-to-all-start.2) | async-done | bytes 3145760 | tf_op jit(solution)/shard_map/all_to_all | solution.py:107
  120.8 2.6 convert_reduce_fusion.2
  123.4 0.3 multiply_reduce_fusion
  123.7 0.3 multiply_convert_fusion.2
  124.0 0.1 fusion.57
  124.0 0.4 broadcast_in_dim.94
  124.4 43.7 %all_to_all.36 = bf16[8,64,3072]{2,1,0:T(8,128)(2,1)} all-to-all(bf16[8,64,3072]{2,1,0:T(8,128)(2,1)S(1)} %broadcast_in_dim.94), channel_id=1, replica_groups=mesh['z'=4,'x_lo'=2,'x_hi'=2,'y'=4,'core'=2] {'x_hi','y'}, dimensions={0} | all-to-all | bytes 6291456 | tf_op jit(solution)/shard_map/all_to_all | solution.py:124
  168.2 2.1 broadcast_in_dim.95
  170.3 4.4 %all-to-all-start.5 = ((bf16[8,64,3072]{2,1,0:T(8,128)(2,1)}), bf16[8,64,3072]{2,1,0:T(8,128)(2,1)}, u32[]{:S(2)}, u32[]{:S(2)}) async-start(bf16[8,64,3072]{2,1,0:T(8,128)(2,1)} %broadcast_in_dim.95), calls=%async_computation.5 | async-start | bytes 6291456 | tf_op jit(solution)/shard_map/all_to_all | solution.py:124
  174.7 0.0 all-gather.4.cloned.1.call-done
  174.7 8.4 %fusion.58 = f32[512,1024]{1,0:T(8,128)} fusion(bf16[512,3072]{1,0:T(8,128)(2,1)} %bitcast.119, bf16[3072,1024]{1,0:T(8,128)(2,1)} %all-gather.4.cloned.1.call-done), kind=kOutput, calls=%fused_computation.92 | convolution fusion | flops 3221225472 | bytes 11534336 | tf_op jit(solution)/shard_map/dot_general | solution.py:127
  183.2 14.5 %convolution_convert_fusion.1 = bf16[512,3072]{1,0:T(8,128)(2,1)} fusion(bf16[1024,3072]{1,0:T(8,128)(2,1)} %all-gather.8.cloned.1.call-done, f32[512,1024]{1,0:T(8,128)} %fusion.58, bf16[512,3072]{1,0:T(8,128)(2,1)} %bitcast.120, bf16[3072,1024]{1,0:T(8,128)(2,1)} %all-gather.6.cloned.1.call-done), kind=kOutput, calls=%fused_computation.13 | convolution fusion | flops 6447169536 | bytes 20971520 | tf_op jit(solution)/shard_map/dot_general | solution.py:130
  197.7 14.5 %all-to-all-done.5 = bf16[8,64,3072]{2,1,0:T(8,128)(2,1)} async-done(((bf16[8,64,3072]{2,1,0:T(8,128)(2,1)}), bf16[8,64,3072]{2,1,0:T(8,128)(2,1)}, u32[]{:S(2)}, u32[]{:S(2)}) %all-to-all-start.5) | async-done | bytes 3145760 | tf_op jit(solution)/shard_map/all_to_all | solution.py:124
  212.1 5.1 %all-to-all-start.4 = ((bf16[8,64,3072]{2,1,0:T(8,128)(2,1)}), bf16[8,64,3072]{2,1,0:T(8,128)(2,1)}, u32[]{:S(2)}, u32[]{:S(2)}) async-start(bf16[8,64,3072]{2,1,0:T(8,128)(2,1)} %bitcast.121), calls=%async_computation.4 | async-start | bytes 6291456 | tf_op jit(solution)/shard_map/all_to_all | solution.py:131
  217.3 8.6 %fusion.59 = f32[512,1024]{1,0:T(8,128)} fusion(bf16[512,3072]{1,0:T(8,128)(2,1)} %bitcast.31, bf16[3072,1024]{1,0:T(8,128)(2,1)} %all-gather.4.cloned.1.call-done), kind=kOutput, calls=%fused_computation.93 | convolution fusion | flops 3221225472 | bytes 11534336 | tf_op jit(solution)/shard_map/dot_general | solution.py:127
  225.9 14.5 %convolution_convert_fusion = bf16[512,3072]{1,0:T(8,128)(2,1)} fusion(bf16[1024,3072]{1,0:T(8,128)(2,1)} %all-gather.8.cloned.1.call-done, f32[512,1024]{1,0:T(8,128)} %fusion.59, bf16[512,3072]{1,0:T(8,128)(2,1)} %bitcast.31, bf16[3072,1024]{1,0:T(8,128)(2,1)} %all-gather.6.cloned.1.call-done), kind=kOutput, calls=%fused_computation.12 | convolution fusion | flops 6447169536 | bytes 20971520 | tf_op jit(solution)/shard_map/dot_general | solution.py:130
  240.4 14.5 %all-to-all-done.4 = bf16[8,64,3072]{2,1,0:T(8,128)(2,1)} async-done(((bf16[8,64,3072]{2,1,0:T(8,128)(2,1)}), bf16[8,64,3072]{2,1,0:T(8,128)(2,1)}, u32[]{:S(2)}, u32[]{:S(2)}) %all-to-all-start.4) | async-done | bytes 3145760 | tf_op jit(solution)/shard_map/all_to_all | solution.py:131
  254.8 5.2 %all-to-all-start.6 = ((bf16[8,64,3072]{2,1,0:T(8,128)(2,1)}), bf16[8,64,3072]{2,1,0:T(8,128)(2,1)}, u32[]{:S(2)}, u32[]{:S(2)}) async-start(bf16[8,64,3072]{2,1,0:T(8,128)(2,1)} %bitcast.122), calls=%async_computation.6 | async-start | bytes 6291456 | tf_op jit(solution)/shard_map/all_to_all | solution.py:131
  260.6 2.5 convert_reduce_fusion.1
  263.1 34.4 %all-to-all-done.6 = bf16[8,64,3072]{2,1,0:T(8,128)(2,1)} async-done(((bf16[8,64,3072]{2,1,0:T(8,128)(2,1)}), bf16[8,64,3072]{2,1,0:T(8,128)(2,1)}, u32[]{:S(2)}, u32[]{:S(2)}) %all-to-all-start.6) | async-done | bytes 3145760 | tf_op jit(solution)/shard_map/all_to_all | solution.py:131
  297.5 2.5 convert_reduce_fusion
  300.0 1.3 fusion.25
  (27 shorter events, 0.1 us)
Async XLA Ops:
  6.5 0.8 copy-start.4
  6.5 10.4 %copy-start.2 = (bf16[384,3072]{1,0:T(8,128)(2,1)S(1)}, bf16[384,3072]{1,0:T(8,128)(2,1)}, u32[]{:S(2)}) copy-start(bf16[384,3072]{1,0:T(8,128)(2,1)} %param.19) | copy-start | bytes 7077892
  6.5 168.2 %all-gather.4.cloned.1.call-start = ((), (), s32[]{:S(2)}) async-start(), calls=%async_computation.7 | async-start | bytes 9437184 | tf_op jit(solution)/shard_map/all_gather | solution.py:114
  8.5 25.5 %all-to-all-start = ((bf16[16,16,2048]{2,1,0:T(8,128)(2,1)}), bf16[16,16,2048]{2,1,0:T(8,128)(2,1)S(1)}, u32[]{:S(2)}, u32[]{:S(2)}) async-start(bf16[16,16,2048]{2,1,0:T(8,128)(2,1)} %broadcast_in_dim.91), calls=%async_computation | async-start | bytes 2097152 | tf_op jit(solution)/shard_map/all_to_all | solution.py:75
  16.9 166.3 %all-gather.6.cloned.1.call-start = ((), (), s32[]{:S(2)}) async-start(), calls=%async_computation.8 | async-start | bytes 9437184 | tf_op jit(solution)/shard_map/all_gather | solution.py:115
  18.1 2.6 copy-start.3
  18.1 37.0 %collective-permute-start = (bf16[192,3072]{1,0:T(8,128)(2,1)}, bf16[192,3072]{1,0:T(8,128)(2,1)}, u32[]{:S(2)}, u32[]{:S(2)}) collective-permute-start(bf16[192,3072]{1,0:T(8,128)(2,1)} %constant_dynamic-slice_fusion), channel_id=1, source_target_pairs={{0,16},{16,0},{1,17},{17,1},{2,18},{18,2},{3,19},{19,3},{4,20},{20... | collective-permute-start | bytes 3538952 | tf_op jit(solution)/shard_map/ppermute | solution.py:92
  34.5 2.4 slice-start
  35.2 1.8 slice-start.1
  36.8 1.3 copy-start.1
  55.1 18.0 %collective-permute-start.1 = (bf16[192,3072]{1,0:T(8,128)(2,1)}, bf16[192,3072]{1,0:T(8,128)(2,1)S(1)}, u32[]{:S(2)}, u32[]{:S(2)}) collective-permute-start(bf16[192,3072]{1,0:T(8,128)(2,1)} %collective-permute-done), channel_id=1, source_target_pairs={{0,1},{1,0},{2,3},{3,2},{4,5},{5,4},{6,7},{7,6},{8,9},{9,8},{10,11... | collective-permute-start | bytes 3538952 | tf_op jit(solution)/shard_map/ppermute | solution.py:95
  79.5 41.3 %all-to-all-start.2 = ((bf16[4,128,3072]{2,1,0:T(8,128)(2,1)}), bf16[4,128,3072]{2,1,0:T(8,128)(2,1)}, u32[]{:S(2)}, u32[]{:S(2)}) async-start(bf16[4,128,3072]{2,1,0:T(8,128)(2,1)} %bitcast.28), calls=%async_computation.2 | async-start | bytes 6291456 | tf_op jit(solution)/shard_map/all_to_all | solution.py:107
  84.2 0.8 copy-start.5
  84.2 99.0 %all-gather.8.cloned.1.call-start = ((), (), s32[]{:S(2)}) async-start(), calls=%async_computation.9 | async-start | bytes 9437184 | tf_op jit(solution)/shard_map/all_gather | solution.py:116
  84.9 38.4 %copy-start = (bf16[128,3072]{1,0:T(8,128)(2,1)S(1)}, bf16[128,3072]{1,0:T(8,128)(2,1)}, u32[]{:S(2)}) copy-start(bf16[128,3072]{1,0:T(8,128)(2,1)} %param.12) | copy-start | bytes 2359300
  170.3 41.9 %all-to-all-start.5 = ((bf16[8,64,3072]{2,1,0:T(8,128)(2,1)}), bf16[8,64,3072]{2,1,0:T(8,128)(2,1)}, u32[]{:S(2)}, u32[]{:S(2)}) async-start(bf16[8,64,3072]{2,1,0:T(8,128)(2,1)} %broadcast_in_dim.95), calls=%async_computation.5 | async-start | bytes 6291456 | tf_op jit(solution)/shard_map/all_to_all | solution.py:124
  212.1 42.7 %all-to-all-start.4 = ((bf16[8,64,3072]{2,1,0:T(8,128)(2,1)}), bf16[8,64,3072]{2,1,0:T(8,128)(2,1)}, u32[]{:S(2)}, u32[]{:S(2)}) async-start(bf16[8,64,3072]{2,1,0:T(8,128)(2,1)} %bitcast.121), calls=%async_computation.4 | async-start | bytes 6291456 | tf_op jit(solution)/shard_map/all_to_all | solution.py:131
  254.8 42.7 %all-to-all-start.6 = ((bf16[8,64,3072]{2,1,0:T(8,128)(2,1)}), bf16[8,64,3072]{2,1,0:T(8,128)(2,1)}, u32[]{:S(2)}, u32[]{:S(2)}) async-start(bf16[8,64,3072]{2,1,0:T(8,128)(2,1)} %bitcast.122), calls=%async_computation.6 | async-start | bytes 6291456 | tf_op jit(solution)/shard_map/all_to_all | solution.py:131
Sparse Core Ops, SparseCore 0:
  9.0 23.0 all-gather.3
  33.8 20.7 all-gather.5
  86.7 22.6 all-gather.7

commit v14 on v11

--- a/solution.py
+++ b/solution.py
@@ -77,7 +77,7 @@
     ).reshape(prefix_total, prefix_kv.shape[1])
     count = piece.shape[0]
     positions = jnp.arange(count, dtype=jnp.int32)
-    maxima, totals, sums = absorb(
+    _, totals, sums = absorb(
         state, query_heads, piece, positions, jnp.ones((count,), bool), query_pos, window
     )
     attended = (
@@ -102,7 +102,8 @@
     ordered = jnp.concatenate(
         [halves[:, :, 0], other.reshape(rows_here, n_z, 2 * width)], axis=-1
     ).transpose(1, 0, 2)
-    columns = lax.all_to_all(ordered, "z", 0, 0, tiled=False).reshape(n_z * rows_here, block)
+    columns = lax.all_to_all(ordered, "z", 0, 0, tiled=False)
+    columns = columns.reshape(n_z * rows_here, block)
     partial = jnp.dot(columns, pair, preferred_element_type=jnp.float32).astype(jnp.bfloat16)
     returned = lax.all_to_all(
         partial.reshape(n_z, rows_here, partial.shape[1]), "z", 0, 0, tiled=False
@@ -159,4 +160,5 @@
         P(REQ, None),
     )
     out_specs = P(ALL, None)
+
     return jax.shard_map(shards, mesh=fine, in_specs=in_specs, out_specs=out_specs, check_vma=False)

time: 299 us -> 299 us (level)
  no operation moved by 1% of the time
where the time goes in v14:
time: 299 us; the launch traced here: 298 us
  waiting for transfers between devices  139 us (46%)
  matrix products  74.9 us (25%)
  starting transfers between devices  39.7 us (13%)
  blocking collectives  16.9 us (6%)
  other arithmetic  13.2 us (4%)
  local copies, waits for them, and re-layouts  12.7 us (4%)
    dot_general x4, matrix products, shards(): parts = parts + jnp.dot(hidden, down_w, preferred_element_type=jnp.float32)  41.9 us
    all_to_all x2, waiting for transfers between devices, shards(): lax.all_to_all(jnp.broadcast_to(rows[None], (n_feed,) + rows.shape), feed...  41.1 us
    all_to_all x2, waiting for transfers between devices, shards(): lax.all_to_all(parts.reshape(n_feed, size, parts.shape[1]), feed_axes, 0,...  40.6 us
    all_to_all x1, waiting for transfers between devices, shards(): lax.all_to_all(partial.reshape(n_z, rows_here, partial.shape[1]), 'z', 0,...  36.4 us
    dot_general x4, matrix products, shards(): gate = jnp.dot(gathered, gate_w, preferred_element_type=jnp.float32)  20.5 us
    all_to_all x1, blocking collectives, shards(): columns = lax.all_to_all(ordered, 'z', 0, 0, tiled=False)  16.9 us
    ppermute x1, waiting for transfers between devices, shards(): lax.ppermute(lax.dynamic_slice_in_dim(out_weight, core * width, width, 0)...  15.2 us
    all_to_all x2, starting transfers between devices, shards(): lax.all_to_all(jnp.broadcast_to(rows[None], (n_feed,) + rows.shape), feed...  12.3 us
  transfers between devices with their start and end apart: 11, of which 7 were waited for; matrix products, arithmetic and copies ran while one was open for 28% of the time, Pallas kernels for 0%

profile of v14, /device:TPU:1, one launch (start us, length us, event | category | flops | bytes accessed | tf_op | source)
XLA Modules:
  0.0 298.4 jit_solution(16856651100731996263)
XLA Ops:
  0.0 2.1 broadcast_in_dim.91
  2.1 8.4 %all-to-all-start = ((bf16[16,16,2048]{2,1,0:T(8,128)(2,1)}), bf16[16,16,2048]{2,1,0:T(8,128)(2,1)S(1)}, u32[]{:S(2)}, u32[]{:S(2)}) async-start(bf16[16,16,2048]{2,1,0:T(8,128)(2,1)} %broadcast_in_dim.91), calls=%async_computation | async-start | bytes 2097152 | tf_op jit(solution)/shard_map/all_to_all | solution.py:75
  10.5 1.1 constant_dynamic-slice_fusion
  11.7 0.3 collective-permute-start
  12.7 1.5 copy.32
  14.2 1.3 copy.33
  15.5 1.5 copy.34
  17.0 1.0 pad_maximum_fusion
  18.1 0.1 fusion.47
  18.2 0.2 fusion.46
  18.4 3.0 %fusion.9 = (f32[8,3,128]{2,1,0:T(4,128)S(1)}, f32[8,384,128,3]{2,1,3,0:T(8,128)}) fusion(pred[128,384]{0,1:T(8,128)(4,1)S(1)} %fusion.46, bf16[384,8,128,1]{0,2,3,1:T(8,128)(2,1)S(1)} %bitcast.131, bf16[128,8,3,128]{0,3,2,1:T(8,128)(2,1)S(1)} %bitcast.126), kind=kOutput, calls=%fused_computation.14 | convolution fusion | flops 305525760 | bytes 6352896 | tf_op jit(solution)/shard_map/skgh,nkh->kgsn/dot_general | solution.py:20
  21.4 6.2 %all-to-all-done = bf16[16,16,2048]{2,1,0:T(8,128)(2,1)S(1)} async-done(((bf16[16,16,2048]{2,1,0:T(8,128)(2,1)}), bf16[16,16,2048]{2,1,0:T(8,128)(2,1)S(1)}, u32[]{:S(2)}, u32[]{:S(2)}) %all-to-all-start) | async-done | bytes 1048608 | tf_op jit(solution)/shard_map/all_to_all | solution.py:75
  27.6 0.1 fusion.66
  27.7 0.2 copy.38
  27.9 0.2 copy.41
  28.1 0.0 slice-start
  28.1 0.7 fusion.12
  28.8 0.8 fusion.20
  29.6 0.8 fusion.22
  30.4 0.0 copy-start.1
  30.5 0.1 slice-done.1
  30.6 1.2 fusion.10
  31.8 1.6 fusion.27
  33.3 0.1 copy.44
  33.4 0.2 reverse_select_fusion
  33.6 15.2 %collective-permute-done = bf16[192,3072]{1,0:T(8,128)(2,1)} collective-permute-done((bf16[192,3072]{1,0:T(8,128)(2,1)}, bf16[192,3072]{1,0:T(8,128)(2,1)}, u32[]{:S(2)}, u32[]{:S(2)}) %collective-permute-start) | collective-permute-done | bytes 1179680 | tf_op jit(solution)/shard_map/ppermute | solution.py:92
  48.7 0.6 collective-permute-start.1
  49.3 0.1 slice_bitcast_fusion
  49.4 0.1 reverse_select_fusion.1
  49.5 0.1 maximum_bitcast_fusion
  49.5 16.9 %all_to_all.35 = bf16[4,128,768]{1,2,0:T(8,128)(2,1)S(1)} all-to-all(bf16[4,128,768]{1,2,0:T(8,128)(2,1)S(1)} %maximum_bitcast_fusion), channel_id=1, replica_groups=mesh['z'=4,'x_lo'=2,'x_hi'=2,'y'=4,'core'=2] {'z'}, dimensions={0} | all-to-all | bytes 1572864 | tf_op jit(solution)/shard_map/all_to_all | solution.py:105
  66.5 0.3 copy.45
  66.8 6.3 %fusion.6 = bf16[512,3072]{1,0:T(8,128)(2,1)} fusion(bf16[512,768]{1,0:T(8,128)(2,1)S(1)} %bitcast.136, bf16[192,3072]{1,0:T(8,128)(2,1)S(1)} %collective-permute-done.1, bf16[192,3072]{1,0:T(8,128)(2,1)} %collective-permute-done, bf16[384,3072]{1,0:T(8,128)(2,1)} %param.19), kind=kOutput, calls=%fused_computation.13 | convolution fusion | flops 2431647744 | bytes 8650752 | tf_op jit(solution)/shard_map/dot_general | solution.py:107
  73.0 5.0 %all-to-all-start.2 = ((bf16[4,128,3072]{2,1,0:T(8,128)(2,1)}), bf16[4,128,3072]{2,1,0:T(8,128)(2,1)}, u32[]{:S(2)}, u32[]{:S(2)}) async-start(bf16[4,128,3072]{2,1,0:T(8,128)(2,1)} %bitcast.28), calls=%async_computation.2 | async-start | bytes 6291456 | tf_op jit(solution)/shard_map/all_to_all | solution.py:108
  78.0 0.0 copy-start
  78.0 36.4 %all-to-all-done.2 = bf16[4,128,3072]{2,1,0:T(8,128)(2,1)} async-done(((bf16[4,128,3072]{2,1,0:T(8,128)(2,1)}), bf16[4,128,3072]{2,1,0:T(8,128)(2,1)}, u32[]{:S(2)}, u32[]{:S(2)}) %all-to-all-start.2) | async-done | bytes 3145760 | tf_op jit(solution)/shard_map/all_to_all | solution.py:108
  114.4 2.6 convert_reduce_fusion.2
  117.0 0.3 multiply_reduce_fusion
  117.3 0.3 multiply_convert_fusion
  117.6 0.1 fusion.67
  117.7 2.0 broadcast_in_dim.94
  119.7 7.1 %all-to-all-start.3 = ((bf16[8,64,3072]{2,1,0:T(8,128)(2,1)}), bf16[8,64,3072]{2,1,0:T(8,128)(2,1)}, u32[]{:S(2)}, u32[]{:S(2)}) async-start(bf16[8,64,3072]{2,1,0:T(8,128)(2,1)} %broadcast_in_dim.94), calls=%async_computation.3 | async-start | bytes 6291456 | tf_op jit(solution)/shard_map/all_to_all | solution.py:126
  126.8 2.3 collective-permute-start.2
  129.1 0.1 collective-permute-start.3
  129.2 0.4 collective-permute-start.4
  129.6 34.8 %all-to-all-done.3 = bf16[8,64,3072]{2,1,0:T(8,128)(2,1)} async-done(((bf16[8,64,3072]{2,1,0:T(8,128)(2,1)}), bf16[8,64,3072]{2,1,0:T(8,128)(2,1)}, u32[]{:S(2)}, u32[]{:S(2)}) %all-to-all-start.3) | async-done | bytes 3145760 | tf_op jit(solution)/shard_map/all_to_all | solution.py:126
  164.4 2.1 broadcast_in_dim.95
  166.5 5.2 %all-to-all-start.5 = ((bf16[8,64,3072]{2,1,0:T(8,128)(2,1)}), bf16[8,64,3072]{2,1,0:T(8,128)(2,1)}, u32[]{:S(2)}, u32[]{:S(2)}) async-start(bf16[8,64,3072]{2,1,0:T(8,128)(2,1)} %broadcast_in_dim.95), calls=%async_computation.5 | async-start | bytes 6291456 | tf_op jit(solution)/shard_map/all_to_all | solution.py:126
  171.6 5.6 %fusion.72 = f32[512,512]{1,0:T(8,128)} fusion(bf16[512,3072]{1,0:T(8,128)(2,1)} %bitcast.29, bf16[3072,512]{1,0:T(8,128)(2,1)} %param.21), kind=kOutput, calls=%fused_computation.106 | convolution fusion | flops 1610612736 | bytes 7340032 | tf_op jit(solution)/shard_map/dot_general | solution.py:131
  177.2 4.6 %fusion.73 = f32[512,512]{1,0:T(8,128)S(1)} fusion(bf16[512,3072]{1,0:T(8,128)(2,1)} %bitcast.29, bf16[3072,512]{1,0:T(8,128)(2,1)} %collective-permute-done.2), kind=kOutput, calls=%fused_computation.107 | convolution fusion | flops 1610612736 | bytes 7340032 | tf_op jit(solution)/shard_map/dot_general | solution.py:131
  181.9 10.2 %fusion.39 = f32[512,3072]{1,0:T(8,128)} fusion(bf16[512,3072]{1,0:T(8,128)(2,1)} %param.23, bf16[512,3072]{1,0:T(8,128)(2,1)} %bitcast.29, bf16[3072,512]{1,0:T(8,128)(2,1)} %param.22, f32[512,512]{1,0:T(8,128)} %fusion.72), kind=kOutput, calls=%fused_computation.55 | convolution fusion | flops 3222798336 | bytes 16777216 | tf_op jit(solution)/shard_map/dot_general | solution.py:134
  192.1 10.7 %add_convert_fusion.1 = bf16[512,3072]{1,0:T(8,128)(2,1)} fusion(f32[512,3072]{1,0:T(8,128)} %fusion.39, bf16[512,3072]{1,0:T(8,128)(2,1)} %collective-permute-done.4, f32[512,512]{1,0:T(8,128)S(1)} %fusion.73, bf16[512,3072]{1,0:T(8,128)(2,1)} %bitcast.29, bf16[3072,512]{1,0:T(8,128)(2,1)} %collective-permute-done.3), kind=kOutput, calls=%fused_computation.3 | convolution fusion | flops 3225944064 | bytes 19922944 | tf_op jit(solution)/shard_map/dot_general | solution.py:134
  202.9 6.3 %all-to-all-done.5 = bf16[8,64,3072]{2,1,0:T(8,128)(2,1)} async-done(((bf16[8,64,3072]{2,1,0:T(8,128)(2,1)}), bf16[8,64,3072]{2,1,0:T(8,128)(2,1)}, u32[]{:S(2)}, u32[]{:S(2)}) %all-to-all-start.5) | async-done | bytes 3145760 | tf_op jit(solution)/shard_map/all_to_all | solution.py:126
  209.2 5.2 %all-to-all-start.4 = ((bf16[8,64,3072]{2,1,0:T(8,128)(2,1)}), bf16[8,64,3072]{2,1,0:T(8,128)(2,1)}, u32[]{:S(2)}, u32[]{:S(2)}) async-start(bf16[8,64,3072]{2,1,0:T(8,128)(2,1)} %bitcast.129), calls=%async_computation.4 | async-start | bytes 6291456 | tf_op jit(solution)/shard_map/all_to_all | solution.py:136
  214.3 5.7 %fusion.74 = f32[512,512]{1,0:T(8,128)} fusion(bf16[512,3072]{1,0:T(8,128)(2,1)} %bitcast.31, bf16[3072,512]{1,0:T(8,128)(2,1)} %param.21), kind=kOutput, calls=%fused_computation.108 | convolution fusion | flops 1610612736 | bytes 7340032 | tf_op jit(solution)/shard_map/dot_general | solution.py:131
  220.0 4.6 %fusion.75 = f32[512,512]{1,0:T(8,128)S(1)} fusion(bf16[512,3072]{1,0:T(8,128)(2,1)} %bitcast.31, bf16[3072,512]{1,0:T(8,128)(2,1)} %collective-permute-done.2), kind=kOutput, calls=%fused_computation.109 | convolution fusion | flops 1610612736 | bytes 7340032 | tf_op jit(solution)/shard_map/dot_general | solution.py:131
  224.6 10.2 %fusion.38 = f32[512,3072]{1,0:T(8,128)} fusion(bf16[512,3072]{1,0:T(8,128)(2,1)} %param.23, bf16[512,3072]{1,0:T(8,128)(2,1)} %bitcast.31, bf16[3072,512]{1,0:T(8,128)(2,1)} %param.22, f32[512,512]{1,0:T(8,128)} %fusion.74), kind=kOutput, calls=%fused_computation.54 | convolution fusion | flops 3222798336 | bytes 16777216 | tf_op jit(solution)/shard_map/dot_general | solution.py:134
  234.9 10.7 %add_convert_fusion = bf16[512,3072]{1,0:T(8,128)(2,1)} fusion(f32[512,3072]{1,0:T(8,128)} %fusion.38, bf16[512,3072]{1,0:T(8,128)(2,1)} %collective-permute-done.4, f32[512,512]{1,0:T(8,128)S(1)} %fusion.75, bf16[512,3072]{1,0:T(8,128)(2,1)} %bitcast.31, bf16[3072,512]{1,0:T(8,128)(2,1)} %collective-permute-done.3), kind=kOutput, calls=%fused_computation.1 | convolution fusion | flops 3225944064 | bytes 19922944 | tf_op jit(solution)/shard_map/dot_general | solution.py:134
  245.6 6.2 %all-to-all-done.4 = bf16[8,64,3072]{2,1,0:T(8,128)(2,1)} async-done(((bf16[8,64,3072]{2,1,0:T(8,128)(2,1)}), bf16[8,64,3072]{2,1,0:T(8,128)(2,1)}, u32[]{:S(2)}, u32[]{:S(2)}) %all-to-all-start.4) | async-done | bytes 3145760 | tf_op jit(solution)/shard_map/all_to_all | solution.py:136
  251.9 5.2 %all-to-all-start.6 = ((bf16[8,64,3072]{2,1,0:T(8,128)(2,1)}), bf16[8,64,3072]{2,1,0:T(8,128)(2,1)}, u32[]{:S(2)}, u32[]{:S(2)}) async-start(bf16[8,64,3072]{2,1,0:T(8,128)(2,1)} %bitcast.130), calls=%async_computation.6 | async-start | bytes 6291456 | tf_op jit(solution)/shard_map/all_to_all | solution.py:136
  257.7 2.5 convert_reduce_fusion.1
  260.2 34.4 %all-to-all-done.6 = bf16[8,64,3072]{2,1,0:T(8,128)(2,1)} async-done(((bf16[8,64,3072]{2,1,0:T(8,128)(2,1)}), bf16[8,64,3072]{2,1,0:T(8,128)(2,1)}, u32[]{:S(2)}, u32[]{:S(2)}) %all-to-all-start.6) | async-done | bytes 3145760 | tf_op jit(solution)/shard_map/all_to_all | solution.py:136
  294.6 2.5 convert_reduce_fusion
  297.1 1.3 fusion.25
  (25 shorter events, 0.1 us)
Async XLA Ops:
  0.0 10.5 %copy-start.2 = (bf16[384,3072]{1,0:T(8,128)(2,1)S(1)}, bf16[384,3072]{1,0:T(8,128)(2,1)}, u32[]{:S(2)}) copy-start(bf16[384,3072]{1,0:T(8,128)(2,1)} %param.19) | copy-start | bytes 7077892
  2.1 25.5 %all-to-all-start = ((bf16[16,16,2048]{2,1,0:T(8,128)(2,1)}), bf16[16,16,2048]{2,1,0:T(8,128)(2,1)S(1)}, u32[]{:S(2)}, u32[]{:S(2)}) async-start(bf16[16,16,2048]{2,1,0:T(8,128)(2,1)} %broadcast_in_dim.91), calls=%async_computation | async-start | bytes 2097152 | tf_op jit(solution)/shard_map/all_to_all | solution.py:75
  11.7 37.1 %collective-permute-start = (bf16[192,3072]{1,0:T(8,128)(2,1)}, bf16[192,3072]{1,0:T(8,128)(2,1)}, u32[]{:S(2)}, u32[]{:S(2)}) collective-permute-start(bf16[192,3072]{1,0:T(8,128)(2,1)} %constant_dynamic-slice_fusion), channel_id=1, source_target_pairs={{0,16},{16,0},{1,17},{17,1},{2,18},{18,2},{3,19},{19,3},{4,20},{20... | collective-permute-start | bytes 3538952 | tf_op jit(solution)/shard_map/ppermute | solution.py:92
  28.1 2.4 slice-start
  28.8 1.8 slice-start.1
  30.4 1.3 copy-start.1
  48.7 18.0 %collective-permute-start.1 = (bf16[192,3072]{1,0:T(8,128)(2,1)}, bf16[192,3072]{1,0:T(8,128)(2,1)S(1)}, u32[]{:S(2)}, u32[]{:S(2)}) collective-permute-start(bf16[192,3072]{1,0:T(8,128)(2,1)} %collective-permute-done), channel_id=1, source_target_pairs={{0,1},{1,0},{2,3},{3,2},{4,5},{5,4},{6,7},{7,6},{8,9},{9,8},{10,11... | collective-permute-start | bytes 3538952 | tf_op jit(solution)/shard_map/ppermute | solution.py:95
  73.0 5.0 %copy-start.3 = (bf16[3072]{0:T(1024)(128)(2,1)S(1)}, bf16[3072]{0:T(1024)(128)(2,1)}, u32[]{:S(2)}) copy-start(bf16[3072]{0:T(1024)(128)(2,1)} %param.20) | copy-start | bytes 18436
  73.0 41.4 %all-to-all-start.2 = ((bf16[4,128,3072]{2,1,0:T(8,128)(2,1)}), bf16[4,128,3072]{2,1,0:T(8,128)(2,1)}, u32[]{:S(2)}, u32[]{:S(2)}) async-start(bf16[4,128,3072]{2,1,0:T(8,128)(2,1)} %bitcast.28), calls=%async_computation.2 | async-start | bytes 6291456 | tf_op jit(solution)/shard_map/all_to_all | solution.py:108
  78.0 39.0 %copy-start = (bf16[128,3072]{1,0:T(8,128)(2,1)S(1)}, bf16[128,3072]{1,0:T(8,128)(2,1)}, u32[]{:S(2)}) copy-start(bf16[128,3072]{1,0:T(8,128)(2,1)} %param.12) | copy-start | bytes 2359300
  119.7 44.7 %all-to-all-start.3 = ((bf16[8,64,3072]{2,1,0:T(8,128)(2,1)}), bf16[8,64,3072]{2,1,0:T(8,128)(2,1)}, u32[]{:S(2)}, u32[]{:S(2)}) async-start(bf16[8,64,3072]{2,1,0:T(8,128)(2,1)} %broadcast_in_dim.94), calls=%async_computation.3 | async-start | bytes 6291456 | tf_op jit(solution)/shard_map/all_to_all | solution.py:126
  126.8 50.4 %collective-permute-start.2 = (bf16[3072,512]{1,0:T(8,128)(2,1)}, bf16[3072,512]{1,0:T(8,128)(2,1)}, u32[]{:S(2)}, u32[]{:S(2)}) collective-permute-start(bf16[3072,512]{1,0:T(8,128)(2,1)} %param.21), channel_id=1, source_target_pairs={{0,1},{1,0},{2,3},{3,2},{4,5},{5,4},{6,7},{7,6},{8,9},{9,8},{10,11... | collective-permute-start | bytes 9437192 | tf_op jit(solution)/shard_map/ppermute | solution.py:117
  129.1 63.0 %collective-permute-start.3 = (bf16[3072,512]{1,0:T(8,128)(2,1)}, bf16[3072,512]{1,0:T(8,128)(2,1)}, u32[]{:S(2)}, u32[]{:S(2)}) collective-permute-start(bf16[3072,512]{1,0:T(8,128)(2,1)} %param.22), channel_id=1, source_target_pairs={{0,1},{1,0},{2,3},{3,2},{4,5},{5,4},{6,7},{7,6},{8,9},{9,8},{10,11... | collective-permute-start | bytes 9437192 | tf_op jit(solution)/shard_map/ppermute | solution.py:117
  129.2 62.9 %collective-permute-start.4 = (bf16[512,3072]{1,0:T(8,128)(2,1)}, bf16[512,3072]{1,0:T(8,128)(2,1)}, u32[]{:S(2)}, u32[]{:S(2)}) collective-permute-start(bf16[512,3072]{1,0:T(8,128)(2,1)} %param.23), channel_id=1, source_target_pairs={{0,1},{1,0},{2,3},{3,2},{4,5},{5,4},{6,7},{7,6},{8,9},{9,8},{10,11... | collective-permute-start | bytes 9437192 | tf_op jit(solution)/shard_map/ppermute | solution.py:117
  166.5 42.7 %all-to-all-start.5 = ((bf16[8,64,3072]{2,1,0:T(8,128)(2,1)}), bf16[8,64,3072]{2,1,0:T(8,128)(2,1)}, u32[]{:S(2)}, u32[]{:S(2)}) async-start(bf16[8,64,3072]{2,1,0:T(8,128)(2,1)} %broadcast_in_dim.95), calls=%async_computation.5 | async-start | bytes 6291456 | tf_op jit(solution)/shard_map/all_to_all | solution.py:126
  209.2 42.7 %all-to-all-start.4 = ((bf16[8,64,3072]{2,1,0:T(8,128)(2,1)}), bf16[8,64,3072]{2,1,0:T(8,128)(2,1)}, u32[]{:S(2)}, u32[]{:S(2)}) async-start(bf16[8,64,3072]{2,1,0:T(8,128)(2,1)} %bitcast.129), calls=%async_computation.4 | async-start | bytes 6291456 | tf_op jit(solution)/shard_map/all_to_all | solution.py:136
  251.9 42.7 %all-to-all-start.6 = ((bf16[8,64,3072]{2,1,0:T(8,128)(2,1)}), bf16[8,64,3072]{2,1,0:T(8,128)(2,1)}, u32[]{:S(2)}, u32[]{:S(2)}) async-start(bf16[8,64,3072]{2,1,0:T(8,128)(2,1)} %bitcast.130), calls=%async_computation.6 | async-start | bytes 6291456 | tf_op jit(solution)/shard_map/all_to_all | solution.py:136
